TPU v7x, 32 devices: a whole 2x2x4 slice. The times are simulated.
32 devices in a mesh: seq: 8 (over z, x), kvh: 4 (over y, core).
Axes of the slice: x: 2, y: 2, z: 4, core: 2. Of those that a mesh axis runs over, the one named last changes fastest.
Arguments:
- queries: bfloat16 [2048, 16384], P(('seq', 'kvh')), may hold values from -48 to 48
- key_rows: bfloat16 [2048, 1024], P(('seq', 'kvh')), may hold values from -6 to 6
- value_rows: bfloat16 [2048, 1024], P(('seq', 'kvh')), may hold values from -6 to 6
- doc_lengths: int32 [8], replicated, may hold values from 1 to 512, 2048 in all
Outputs:
- attended: bfloat16 [2048, 16384], P(('seq', 'kvh'))
Inputs may be any that keep to these rules, and one draw needn't show every extreme that they name: `doc_lengths`: the lengths add up to 2048; the longest document has exactly 512 tokens.
All inputs are finite; a program needn't handle non-finite values.
Results may differ from a plain program's by a relative error of at most 0.004.
Values may be sent and summed in bfloat16 or wider, within the bound.
No kernel may reach another device: no remote copies, remote signals or barrier semaphores. Data moves between devices by JAX's collectives and lax.ppermute only.
A program may use at most 64 MiB of HBM per device.

v0:
```python
import functools
import math

import jax
import jax.numpy as jnp
from jax import lax
from jax.experimental import pallas as pl
from jax.experimental.pallas import tpu as pltpu
from jax.sharding import PartitionSpec as P

DH = 128


def shifted(block, axis, distance):
    devices = range(lax.axis_size(axis))
    route = [(i - distance, i) for i in devices if i - distance in devices]
    return lax.ppermute(block, axis, route)


def doc_start(position, doc_ends, doc_lengths):
    return jnp.sum(
        jnp.where(doc_ends[None, :] <= position[:, None], doc_lengths[None, :], 0), axis=1
    )


def attend_kernel(
    blocks_ref, q_ref, start_ref, k_ref, v_ref, out_ref, kt_buf, v_buf,
    *, half_rows, group_size, pad_rows, window
):
    side = pl.program_id(0)
    block_id = blocks_ref[side]
    needed = blocks_ref[2 + side]
    kt_buf[...] = k_ref[...].T
    v_buf[:, :DH] = v_ref[...]
    lane = lax.broadcasted_iota(jnp.int32, (window, DH), 1)
    v_buf[:, DH:] = jnp.where(lane == 0, 1.0, 0.0).astype(v_buf.dtype)
    scale = 1.0 / math.sqrt(DH)
    row_start = start_ref[...]

    def dense(span):
        skip = window - span
        row_pos = block_id * half_rows + lax.broadcasted_iota(jnp.int32, (half_rows, span), 0)
        key_pos = block_id * half_rows - pad_rows + skip + lax.broadcasted_iota(
            jnp.int32, (half_rows, span), 1
        )
        allowed = (key_pos <= row_pos) & (key_pos >= row_start)
        bias = jnp.where(allowed, 0.0, -jnp.inf).astype(jnp.float32)

        def one_member(g, carry):
            col = pl.multiple_of(g * DH, DH)
            q_g = q_ref[:, pl.ds(col, DH)]
            scores = jnp.dot(q_g, kt_buf[:, skip:], preferred_element_type=jnp.float32)
            scores = scores * scale + bias
            top = jnp.max(scores, axis=1, keepdims=True)
            weights = jnp.exp(scores - top)
            mixed = jnp.dot(
                weights.astype(jnp.bfloat16), v_buf[skip:, :], preferred_element_type=jnp.float32
            )
            total = mixed[:, DH : DH + 1]
            out_ref[:, pl.ds(col, DH)] = (mixed[:, :DH] / total).astype(out_ref.dtype)
            return carry

        lax.fori_loop(0, group_size, one_member, 0, unroll=True)

    for count in range(1, window // half_rows + 1):

        @pl.when(needed == count)
        def _(count=count):
            dense(count * half_rows)


def on_device(queries, key_rows, value_rows, doc_lengths):
    shards = lax.axis_size("seq")
    kvh = lax.axis_size("kvh")
    my_shard = lax.axis_index("seq")
    rows_in = key_rows.shape[0]
    head_queries = lax.all_to_all(queries, "kvh", split_axis=1, concat_axis=0, tiled=True)
    kv_cols = key_rows.shape[1] // kvh
    kv_local = jnp.concatenate(
        [key_rows.reshape(rows_in, kvh, kv_cols), value_rows.reshape(rows_in, kvh, kv_cols)],
        axis=2,
    )
    kv_slab = lax.all_to_all(kv_local, "kvh", split_axis=1, concat_axis=0, tiled=True)
    dev_rows = kv_slab.shape[0]
    kv_slab = kv_slab.reshape(dev_rows, 2 * kv_cols)
    half_rows = dev_rows // 2
    kv_feat = kv_cols
    kv_heads = kv_feat // DH
    group_size = head_queries.shape[1] // kv_feat
    seq_total = dev_rows * shards
    longest = min(13 * half_rows, seq_total // 4)
    lookback = (longest + half_rows - 2) // half_rows
    pad_rows = lookback * half_rows
    window = pad_rows + half_rows

    first_half = kv_slab[:half_rows]
    second_half = kv_slab[half_rows:]
    blank = jnp.zeros_like(first_half)
    low_side = [first_half]
    high_side = [second_half]
    for back in range(1, lookback + 1):
        from_low = shifted(first_half, "seq", back)
        from_high = shifted(second_half, "seq", -back)
        mirror = [(t, 2 * shards - 1 - back - t) for t in range(shards)]
        mirror = [(t, u) for t, u in mirror if 0 <= u < shards and u != t]
        from_mirror = lax.ppermute(first_half, "seq", mirror) if mirror else blank
        wanted = 2 * shards - 1 - my_shard - back
        high_pick = jnp.where(
            wanted >= shards, from_high, jnp.where(wanted == my_shard, first_half, from_mirror)
        )
        low_side.append(from_low)
        high_side.append(high_pick)
    windows = jnp.stack(
        [jnp.concatenate(low_side[::-1], axis=0), jnp.concatenate(high_side[::-1], axis=0)]
    )

    doc_ends = jnp.cumsum(doc_lengths)
    block_ids = jnp.stack([my_shard, 2 * shards - 1 - my_shard]).astype(jnp.int32)
    positions = block_ids[:, None] * half_rows + jnp.arange(half_rows, dtype=jnp.int32)[None, :]
    starts = doc_start(positions.reshape(-1), doc_ends, doc_lengths).astype(jnp.int32)
    needed = 1 + jnp.clip((block_ids * half_rows - starts[::half_rows] + half_rows - 1) // half_rows, 0, lookback)
    block_ids = jnp.concatenate([block_ids, needed.astype(jnp.int32)])
    starts = starts.reshape(2, half_rows, 1)

    kernel = functools.partial(
        attend_kernel,
        half_rows=half_rows,
        group_size=group_size,
        pad_rows=pad_rows,
        window=window,
    )
    q_cols = group_size * DH
    merged = pl.pallas_call(
        kernel,
        out_shape=jax.ShapeDtypeStruct(head_queries.shape, head_queries.dtype),
        grid_spec=pltpu.PrefetchScalarGridSpec(
            num_scalar_prefetch=1,
            grid=(2, kv_heads),
            in_specs=[
                pl.BlockSpec((half_rows, q_cols), lambda s, h, b: (s, h)),
                pl.BlockSpec((None, half_rows, 1), lambda s, h, b: (s, 0, 0)),
                pl.BlockSpec((None, window, DH), lambda s, h, b: (s, 0, h)),
                pl.BlockSpec((None, window, DH), lambda s, h, b, n=kv_heads: (s, 0, n + h)),
            ],
            out_specs=pl.BlockSpec((half_rows, q_cols), lambda s, h, b: (s, h)),
            scratch_shapes=[
                pltpu.VMEM((DH, window), kv_slab.dtype),
                pltpu.VMEM((window, 2 * DH), kv_slab.dtype),
            ],
        ),
    )(block_ids, head_queries, starts, windows, windows)
    return lax.all_to_all(merged, "kvh", split_axis=0, concat_axis=1, tiled=True)


def solution(mesh):
    return jax.shard_map(
        on_device,
        mesh=mesh,
        in_specs=(P(("seq", "kvh"), None), P(("seq", "kvh"), None), P(("seq", "kvh"), None), P()),
        out_specs=P(("seq", "kvh"), None),
        check_vma=False,
    )
```

profile of v0, /device:TPU:0, one launch (start us, length us, event | category | flops | bytes accessed | tf_op | source)
XLA Modules:
  0.0 106.2 jit_solution(10802254655040612843)
XLA Ops:
  0.0 1.0 copy_bitcast_fusion.1
  1.0 0.7 pad_maximum_fusion.1
  1.7 4.2 %all-to-all-start.1 = ((bf16[64,4,512]{2,0,1:T(8,128)(2,1)}), bf16[64,4,512]{2,0,1:T(8,128)(2,1)S(1)}, u32[]{:S(2)}, u32[]{:S(2)}) async-start(bf16[64,4,512]{2,0,1:T(8,128)(2,1)} %pad_maximum_fusion.1), calls=%async_computation.1 | async-start | bytes 524288 | tf_op jit(solution)/shard_map/all_to_all | solution.py:83
  5.9 0.1 add_multiply_fusion
  6.0 0.1 add_bitcast_fusion
  6.1 0.8 reduce-window.8
  6.9 0.7 select_reduce_fusion
  7.7 0.1 slice.15
  7.8 3.1 %copy.26 = bf16[8,4,8,4096]{3,2,0,1:T(8,128)(2,1)} copy(bf16[8,4,8,4096]{3,2,1,0:T(8,128)(2,1)} %bitcast.45) | data formatting | bytes 4194304 | tf_op jit(solution)/shard_map/all_to_all | solution.py:77
  10.9 1.1 %all-to-all-done.1 = bf16[64,4,512]{2,0,1:T(8,128)(2,1)S(1)} async-done(((bf16[64,4,512]{2,0,1:T(8,128)(2,1)}), bf16[64,4,512]{2,0,1:T(8,128)(2,1)S(1)}, u32[]{:S(2)}, u32[]{:S(2)}) %all-to-all-start.1) | async-done | bytes 262176 | tf_op jit(solution)/shard_map/all_to_all | solution.py:83
  12.0 3.6 %all-to-all-start = ((bf16[64,4,4096]{2,0,1:T(8,128)(2,1)}), bf16[64,4,4096]{2,0,1:T(8,128)(2,1)S(1)}, u32[]{:S(2)}, u32[]{:S(2)}) async-start(bf16[64,4,4096]{2,0,1:T(8,128)(2,1)} %bitcast.30), calls=%async_computation | async-start | bytes 4194304 | tf_op jit(solution)/shard_map/all_to_all | solution.py:77
  15.6 1.3 %collective-permute-start.4 = (bf16[128,512]{1,0:T(8,128)(2,1)S(1)}, bf16[128,512]{1,0:T(8,128)(2,1)S(1)}, u32[]{:S(2)}, u32[]{:S(2)}) collective-permute-start(bf16[128,512]{1,0:T(8,128)(2,1)S(1)} %bitcast.49), channel_id=1, source_target_pairs={{16,0},{20,4},{24,8},{28,12},{17,1},{21,5},{25,9},{29,13},{18,2},{... | collective-permute-start | bytes 393224 | tf_op jit(solution)/shard_map/ppermute | solution.py:17
  16.9 0.7 collective-permute-start.5
  17.6 0.1 clamp_add_fusion
  17.7 0.8 copy.17.start_ref
  18.5 0.6 pad_add_fusion.blocks_ref
  19.1 9.8 %collective-permute-start = (bf16[128,512]{1,0:T(8,128)(2,1)S(1)}, bf16[128,512]{1,0:T(8,128)(2,1)S(1)}, u32[]{:S(2)}, u32[]{:S(2)}) collective-permute-start(bf16[128,512]{1,0:T(8,128)(2,1)S(1)} %bitcast.35), channel_id=1, source_target_pairs={{0,16},{4,20},{8,24},{12,28},{1,17},{5,21},{9,25},{13,29},{2,18},{... | collective-permute-start | bytes 393224 | tf_op jit(solution)/shard_map/ppermute | solution.py:17
  28.8 1.9 %collective-permute-start.1 = (bf16[128,512]{1,0:T(8,128)(2,1)S(1)}, bf16[128,512]{1,0:T(8,128)(2,1)S(1)}, u32[]{:S(2)}, u32[]{:S(2)}) collective-permute-start(bf16[128,512]{1,0:T(8,128)(2,1)S(1)} %bitcast.36), channel_id=1, source_target_pairs={{0,12},{4,16},{8,20},{12,24},{16,28},{1,13},{5,17},{9,21},{13,25},... | collective-permute-start | bytes 393224 | tf_op jit(solution)/shard_map/ppermute | solution.py:17
  30.8 1.8 %collective-permute-start.2 = (bf16[128,512]{1,0:T(8,128)(2,1)S(1)}, bf16[128,512]{1,0:T(8,128)(2,1)S(1)}, u32[]{:S(2)}, u32[]{:S(2)}) collective-permute-start(bf16[128,512]{1,0:T(8,128)(2,1)S(1)} %bitcast.37), channel_id=1, source_target_pairs={{0,8},{4,12},{8,16},{12,20},{16,24},{20,28},{1,9},{5,13},{9,17},{1... | collective-permute-start | bytes 393224 | tf_op jit(solution)/shard_map/ppermute | solution.py:17
  32.6 0.0 collective-permute-done.4
  32.6 1.3 %collective-permute-start.6 = (bf16[128,512]{1,0:T(8,128)(2,1)S(1)}, bf16[128,512]{1,0:T(8,128)(2,1)S(1)}, u32[]{:S(2)}, u32[]{:S(2)}) collective-permute-start(bf16[128,512]{1,0:T(8,128)(2,1)S(1)} %bitcast.50), channel_id=1, source_target_pairs={{12,0},{16,4},{20,8},{24,12},{28,16},{13,1},{17,5},{21,9},{25,13},... | collective-permute-start | bytes 393224 | tf_op jit(solution)/shard_map/ppermute | solution.py:17
  33.9 0.0 collective-permute-done.5
  33.9 0.7 collective-permute-start.7
  34.6 0.1 select_dynamic-update-slice_fusion.3
  34.7 5.7 %collective-permute-done.6 = bf16[128,512]{1,0:T(8,128)(2,1)S(1)} collective-permute-done((bf16[128,512]{1,0:T(8,128)(2,1)S(1)}, bf16[128,512]{1,0:T(8,128)(2,1)S(1)}, u32[]{:S(2)}, u32[]{:S(2)}) %collective-permute-start.6) | collective-permute-done | bytes 131104 | tf_op jit(solution)/shard_map/ppermute | solution.py:17
  40.4 1.3 %collective-permute-start.8 = (bf16[128,512]{1,0:T(8,128)(2,1)S(1)}, bf16[128,512]{1,0:T(8,128)(2,1)S(1)}, u32[]{:S(2)}, u32[]{:S(2)}) collective-permute-start(bf16[128,512]{1,0:T(8,128)(2,1)S(1)} %bitcast.51), channel_id=1, source_target_pairs={{8,0},{12,4},{16,8},{20,12},{24,16},{28,20},{9,1},{13,5},{17,9},{2... | collective-permute-start | bytes 393224 | tf_op jit(solution)/shard_map/ppermute | solution.py:17
  41.7 0.0 collective-permute-done.7
  41.7 0.7 collective-permute-start.9
  42.3 0.1 select_dynamic-update-slice_fusion.2
  42.4 4.8 %collective-permute-done.8 = bf16[128,512]{1,0:T(8,128)(2,1)S(1)} collective-permute-done((bf16[128,512]{1,0:T(8,128)(2,1)S(1)}, bf16[128,512]{1,0:T(8,128)(2,1)S(1)}, u32[]{:S(2)}, u32[]{:S(2)}) %collective-permute-start.8) | collective-permute-done | bytes 131104 | tf_op jit(solution)/shard_map/ppermute | solution.py:17
  47.2 6.9 %collective-permute-start.3 = (bf16[128,512]{1,0:T(8,128)(2,1)S(1)}, bf16[128,512]{1,0:T(8,128)(2,1)S(1)}, u32[]{:S(2)}, u32[]{:S(2)}) collective-permute-start(bf16[128,512]{1,0:T(8,128)(2,1)S(1)} %bitcast.42), channel_id=1, source_target_pairs={{0,4},{4,8},{8,12},{12,16},{16,20},{20,24},{24,28},{1,5},{5,9},{9,... | collective-permute-start | bytes 393224 | tf_op jit(solution)/shard_map/ppermute | solution.py:17
  54.2 0.0 collective-permute-done.9
  54.2 1.3 %collective-permute-start.10 = (bf16[128,512]{1,0:T(8,128)(2,1)S(1)}, bf16[128,512]{1,0:T(8,128)(2,1)S(1)}, u32[]{:S(2)}, u32[]{:S(2)}) collective-permute-start(bf16[128,512]{1,0:T(8,128)(2,1)S(1)} %bitcast.52), channel_id=1, source_target_pairs={{4,0},{8,4},{12,8},{16,12},{20,16},{24,20},{28,24},{5,1},{9,5},{13... | collective-permute-start | bytes 393224 | tf_op jit(solution)/shard_map/ppermute | solution.py:17
  55.5 0.1 select_dynamic-update-slice_fusion.1
  55.5 0.0 collective-permute-done
  55.6 0.0 collective-permute-done.1
  55.6 0.0 collective-permute-done.2
  55.6 2.4 %collective-permute-done.3 = bf16[128,512]{1,0:T(8,128)(2,1)S(1)} collective-permute-done((bf16[128,512]{1,0:T(8,128)(2,1)S(1)}, bf16[128,512]{1,0:T(8,128)(2,1)S(1)}, u32[]{:S(2)}, u32[]{:S(2)}) %collective-permute-start.3) | collective-permute-done | bytes 131104 | tf_op jit(solution)/shard_map/ppermute | solution.py:17
  58.1 3.0 %collective-permute-done.10 = bf16[128,512]{1,0:T(8,128)(2,1)S(1)} collective-permute-done((bf16[128,512]{1,0:T(8,128)(2,1)S(1)}, bf16[128,512]{1,0:T(8,128)(2,1)S(1)}, u32[]{:S(2)}, u32[]{:S(2)}) %collective-permute-start.10) | collective-permute-done | bytes 131104 | tf_op jit(solution)/shard_map/ppermute | solution.py:17
  61.1 1.2 %pad_maximum_fusion.k_ref.v_ref = bf16[2,640,512]{2,1,0:T(8,128)(2,1)} fusion(bf16[1,640,512]{2,1,0:T(8,128)(2,1)S(1)} %bitcast.48, bf16[1,640,512]{2,1,0:T(8,128)(2,1)S(1)} %bitcast.47), kind=kLoop, calls=%fused_computation.1 | loop fusion | flops 655360 | bytes 2621440 | tf_op jit(solution)/shard_map/stack | solution.py:113
  62.3 0.0 all-to-all-done
  62.3 0.0 copy-start
  62.3 1.3 %copy-done = bf16[64,4,4096]{2,0,1:T(8,128)(2,1)} copy-done((bf16[64,4,4096]{2,0,1:T(8,128)(2,1)}, bf16[64,4,4096]{2,0,1:T(8,128)(2,1)S(1)}, u32[]{:S(2)}) %copy-start) | copy-done | bytes 2097176
  63.6 11.8 %shard_map.46 = bf16[256,4096]{1,0:T(8,128)(2,1)} custom-call(s32[4]{0:T(128)} %pad_add_fusion.blocks_ref, bf16[256,4096]{1,0:T(8,128)(2,1)} %bitcast.31, s32[2,128,1]{2,1,0:T(8,128)} %copy.17.start_ref, bf16[2,640,512]{2,1,0:T(8,128)(2,1)} %pad_maximum_fusion.k_ref.v_ref, bf16[2,640,512]{2,1,0:T(8,128)(2,1)} %pad_maximum_fusion.k_ref.v_ref), custom_call_target="tpu_custom_call" | custom-call | tf_op jit(solution)/shard_map/pallas_call | solution.py:133
  75.4 29.3 %all_to_all.53 = bf16[4,64,4096]{2,1,0:T(8,128)(2,1)S(1)} all-to-all(bf16[4,64,4096]{2,1,0:T(8,128)(2,1)} %bitcast.32), channel_id=1, replica_groups=mesh['seq'=8,'kvh'=4] {'kvh'}, dimensions={0} | all-to-all | bytes 4194304 | tf_op jit(solution)/shard_map/all_to_all | solution.py:152
  104.7 1.5 %copy.22 = bf16[4,8,8,4096]{3,2,0,1:T(8,128)(2,1)} copy(bf16[4,8,8,4096]{3,2,1,0:T(8,128)(2,1)S(1)} %bitcast.33) | data formatting | bytes 4194304 | tf_op jit(solution)/shard_map/all_to_all | solution.py:152
  (7 shorter events, 0.1 us)
Async XLA Ops:
  1.7 10.3 %all-to-all-start.1 = ((bf16[64,4,512]{2,0,1:T(8,128)(2,1)}), bf16[64,4,512]{2,0,1:T(8,128)(2,1)S(1)}, u32[]{:S(2)}, u32[]{:S(2)}) async-start(bf16[64,4,512]{2,0,1:T(8,128)(2,1)} %pad_maximum_fusion.1), calls=%async_computation.1 | async-start | bytes 524288 | tf_op jit(solution)/shard_map/all_to_all | solution.py:83
  12.0 50.3 %all-to-all-start = ((bf16[64,4,4096]{2,0,1:T(8,128)(2,1)}), bf16[64,4,4096]{2,0,1:T(8,128)(2,1)S(1)}, u32[]{:S(2)}, u32[]{:S(2)}) async-start(bf16[64,4,4096]{2,0,1:T(8,128)(2,1)} %bitcast.30), calls=%async_computation | async-start | bytes 4194304 | tf_op jit(solution)/shard_map/all_to_all | solution.py:77
  15.6 17.0 %collective-permute-start.4 = (bf16[128,512]{1,0:T(8,128)(2,1)S(1)}, bf16[128,512]{1,0:T(8,128)(2,1)S(1)}, u32[]{:S(2)}, u32[]{:S(2)}) collective-permute-start(bf16[128,512]{1,0:T(8,128)(2,1)S(1)} %bitcast.49), channel_id=1, source_target_pairs={{16,0},{20,4},{24,8},{28,12},{17,1},{21,5},{25,9},{29,13},{18,2},{... | collective-permute-start | bytes 393224 | tf_op jit(solution)/shard_map/ppermute | solution.py:17
  16.9 17.0 %collective-permute-start.5 = (bf16[128,512]{1,0:T(8,128)(2,1)S(1)}, bf16[128,512]{1,0:T(8,128)(2,1)S(1)}, u32[]{:S(2)}, u32[]{:S(2)}) collective-permute-start(bf16[128,512]{1,0:T(8,128)(2,1)S(1)} %bitcast.34), channel_id=1, source_target_pairs={{16,28},{20,24},{24,20},{28,16},{17,29},{21,25},{25,21},{29,17},{1... | collective-permute-start | bytes 393224 | tf_op jit(solution)/shard_map/ppermute | solution.py:106
  19.1 36.5 %collective-permute-start = (bf16[128,512]{1,0:T(8,128)(2,1)S(1)}, bf16[128,512]{1,0:T(8,128)(2,1)S(1)}, u32[]{:S(2)}, u32[]{:S(2)}) collective-permute-start(bf16[128,512]{1,0:T(8,128)(2,1)S(1)} %bitcast.35), channel_id=1, source_target_pairs={{0,16},{4,20},{8,24},{12,28},{1,17},{5,21},{9,25},{13,29},{2,18},{... | collective-permute-start | bytes 393224 | tf_op jit(solution)/shard_map/ppermute | solution.py:17
  28.8 26.7 %collective-permute-start.1 = (bf16[128,512]{1,0:T(8,128)(2,1)S(1)}, bf16[128,512]{1,0:T(8,128)(2,1)S(1)}, u32[]{:S(2)}, u32[]{:S(2)}) collective-permute-start(bf16[128,512]{1,0:T(8,128)(2,1)S(1)} %bitcast.36), channel_id=1, source_target_pairs={{0,12},{4,16},{8,20},{12,24},{16,28},{1,13},{5,17},{9,21},{13,25},... | collective-permute-start | bytes 393224 | tf_op jit(solution)/shard_map/ppermute | solution.py:17
  30.8 24.8 %collective-permute-start.2 = (bf16[128,512]{1,0:T(8,128)(2,1)S(1)}, bf16[128,512]{1,0:T(8,128)(2,1)S(1)}, u32[]{:S(2)}, u32[]{:S(2)}) collective-permute-start(bf16[128,512]{1,0:T(8,128)(2,1)S(1)} %bitcast.37), channel_id=1, source_target_pairs={{0,8},{4,12},{8,16},{12,20},{16,24},{20,28},{1,9},{5,13},{9,17},{1... | collective-permute-start | bytes 393224 | tf_op jit(solution)/shard_map/ppermute | solution.py:17
  32.6 7.8 %collective-permute-start.6 = (bf16[128,512]{1,0:T(8,128)(2,1)S(1)}, bf16[128,512]{1,0:T(8,128)(2,1)S(1)}, u32[]{:S(2)}, u32[]{:S(2)}) collective-permute-start(bf16[128,512]{1,0:T(8,128)(2,1)S(1)} %bitcast.50), channel_id=1, source_target_pairs={{12,0},{16,4},{20,8},{24,12},{28,16},{13,1},{17,5},{21,9},{25,13},... | collective-permute-start | bytes 393224 | tf_op jit(solution)/shard_map/ppermute | solution.py:17
  33.9 7.7 %collective-permute-start.7 = (bf16[128,512]{1,0:T(8,128)(2,1)S(1)}, bf16[128,512]{1,0:T(8,128)(2,1)S(1)}, u32[]{:S(2)}, u32[]{:S(2)}) collective-permute-start(bf16[128,512]{1,0:T(8,128)(2,1)S(1)} %bitcast.38), channel_id=1, source_target_pairs={{20,28},{28,20},{21,29},{29,21},{22,30},{30,22},{23,31},{31,23}} | collective-permute-start | bytes 393224 | tf_op jit(solution)/shard_map/ppermute | solution.py:106
  40.4 6.8 %collective-permute-start.8 = (bf16[128,512]{1,0:T(8,128)(2,1)S(1)}, bf16[128,512]{1,0:T(8,128)(2,1)S(1)}, u32[]{:S(2)}, u32[]{:S(2)}) collective-permute-start(bf16[128,512]{1,0:T(8,128)(2,1)S(1)} %bitcast.51), channel_id=1, source_target_pairs={{8,0},{12,4},{16,8},{20,12},{24,16},{28,20},{9,1},{13,5},{17,9},{2... | collective-permute-start | bytes 393224 | tf_op jit(solution)/shard_map/ppermute | solution.py:17
  41.7 12.5 %collective-permute-start.9 = (bf16[128,512]{1,0:T(8,128)(2,1)S(1)}, bf16[128,512]{1,0:T(8,128)(2,1)S(1)}, u32[]{:S(2)}, u32[]{:S(2)}) collective-permute-start(bf16[128,512]{1,0:T(8,128)(2,1)S(1)} %bitcast.40), channel_id=1, source_target_pairs={{24,28},{28,24},{25,29},{29,25},{26,30},{30,26},{27,31},{31,27}} | collective-permute-start | bytes 393224 | tf_op jit(solution)/shard_map/ppermute | solution.py:106
  47.2 10.8 %collective-permute-start.3 = (bf16[128,512]{1,0:T(8,128)(2,1)S(1)}, bf16[128,512]{1,0:T(8,128)(2,1)S(1)}, u32[]{:S(2)}, u32[]{:S(2)}) collective-permute-start(bf16[128,512]{1,0:T(8,128)(2,1)S(1)} %bitcast.42), channel_id=1, source_target_pairs={{0,4},{4,8},{8,12},{12,16},{16,20},{20,24},{24,28},{1,5},{5,9},{9,... | collective-permute-start | bytes 393224 | tf_op jit(solution)/shard_map/ppermute | solution.py:17
  54.2 6.9 %collective-permute-start.10 = (bf16[128,512]{1,0:T(8,128)(2,1)S(1)}, bf16[128,512]{1,0:T(8,128)(2,1)S(1)}, u32[]{:S(2)}, u32[]{:S(2)}) collective-permute-start(bf16[128,512]{1,0:T(8,128)(2,1)S(1)} %bitcast.52), channel_id=1, source_target_pairs={{4,0},{8,4},{12,8},{16,12},{20,16},{24,20},{28,24},{5,1},{9,5},{13... | collective-permute-start | bytes 393224 | tf_op jit(solution)/shard_map/ppermute | solution.py:17
  62.3 1.3 %copy-start = (bf16[64,4,4096]{2,0,1:T(8,128)(2,1)}, bf16[64,4,4096]{2,0,1:T(8,128)(2,1)S(1)}, u32[]{:S(2)}) copy-start(bf16[64,4,4096]{2,0,1:T(8,128)(2,1)S(1)} %all-to-all-done) | copy-start | bytes 6291460
where the time goes:
time: 107 us; the launch traced here: 106 us
  starting transfers between devices  35.5 us (33%)
  blocking collectives  29.3 us (27%)
  waiting for transfers between devices  17 us (16%)
  Pallas kernels  11.8 us (11%)
  local copies, waits for them, and re-layouts  7.93 us (7%)
  other arithmetic  4.48 us (4%)
    all_to_all x1, blocking collectives, on_device(): lax.all_to_all(merged, 'kvh', split_axis=0, concat_axis=1, tiled=True)  29.3 us
    ppermute x8, starting transfers between devices, shifted(): return lax.ppermute(block, axis, route)  25.6 us
    ppermute x8, waiting for transfers between devices, shifted(): return lax.ppermute(block, axis, route)  15.9 us
    pallas_call x1, Pallas kernels, on_device(): pl.pallas_call(kernel, out_shape=jax.ShapeDtypeStruct(head_queries.shape,...  11.8 us
    all_to_all x1, starting transfers between devices, on_device(): lax.all_to_all(kv_local, 'kvh', split_axis=1, concat_axis=0, tiled=True)  4.24 us
    all_to_all x1, starting transfers between devices, on_device(): lax.all_to_all(queries, 'kvh', split_axis=1, concat_axis=0, tiled=True)  3.61 us
    all_to_all x1, local copies, waits for them, and re-layouts, on_device(): lax.all_to_all(queries, 'kvh', split_axis=1, concat_axis=0, tiled=True)  3.13 us
  transfers between devices with their start and end apart: 13, of which 5 were waited for; matrix products, arithmetic and copies ran while one was open for 7% of the time, Pallas kernels for 0%

commit v1 on v0

--- a/solution.py
+++ b/solution.py
@@ -29,44 +29,50 @@
 ):
     side = pl.program_id(0)
     block_id = blocks_ref[side]
-    needed = blocks_ref[2 + side]
     kt_buf[...] = k_ref[...].T
     v_buf[:, :DH] = v_ref[...]
     lane = lax.broadcasted_iota(jnp.int32, (window, DH), 1)
     v_buf[:, DH:] = jnp.where(lane == 0, 1.0, 0.0).astype(v_buf.dtype)
     scale = 1.0 / math.sqrt(DH)
-    row_start = start_ref[...]
+    sub_rows = half_rows // 2
 
-    def dense(span):
-        skip = window - span
-        row_pos = block_id * half_rows + lax.broadcasted_iota(jnp.int32, (half_rows, span), 0)
-        key_pos = block_id * half_rows - pad_rows + skip + lax.broadcasted_iota(
-            jnp.int32, (half_rows, span), 1
+    def dense(part, count):
+        lo = pad_rows - (count - 1) * half_rows
+        hi = pad_rows + (part + 1) * sub_rows
+        span = hi - lo
+        rows = slice(part * sub_rows, (part + 1) * sub_rows)
+        row_pos = block_id * half_rows + part * sub_rows + lax.broadcasted_iota(
+            jnp.int32, (sub_rows, span), 0
         )
-        allowed = (key_pos <= row_pos) & (key_pos >= row_start)
+        key_pos = block_id * half_rows - pad_rows + lo + lax.broadcasted_iota(
+            jnp.int32, (sub_rows, span), 1
+        )
+        allowed = (key_pos <= row_pos) & (key_pos >= start_ref[rows, :])
         bias = jnp.where(allowed, 0.0, -jnp.inf).astype(jnp.float32)
 
         def one_member(g, carry):
             col = pl.multiple_of(g * DH, DH)
-            q_g = q_ref[:, pl.ds(col, DH)]
-            scores = jnp.dot(q_g, kt_buf[:, skip:], preferred_element_type=jnp.float32)
+            q_g = q_ref[rows, pl.ds(col, DH)]
+            scores = jnp.dot(q_g, kt_buf[:, lo:hi], preferred_element_type=jnp.float32)
             scores = scores * scale + bias
             top = jnp.max(scores, axis=1, keepdims=True)
             weights = jnp.exp(scores - top)
             mixed = jnp.dot(
-                weights.astype(jnp.bfloat16), v_buf[skip:, :], preferred_element_type=jnp.float32
+                weights.astype(jnp.bfloat16), v_buf[lo:hi, :], preferred_element_type=jnp.float32
             )
             total = mixed[:, DH : DH + 1]
-            out_ref[:, pl.ds(col, DH)] = (mixed[:, :DH] / total).astype(out_ref.dtype)
+            out_ref[rows, pl.ds(col, DH)] = (mixed[:, :DH] / total).astype(out_ref.dtype)
             return carry
 
         lax.fori_loop(0, group_size, one_member, 0, unroll=True)
 
-    for count in range(1, window // half_rows + 1):
+    for part in range(2):
+        needed = blocks_ref[2 + 2 * side + part]
+        for count in range(1, window // half_rows + 1):
 
-        @pl.when(needed == count)
-        def _(count=count):
-            dense(count * half_rows)
+            @pl.when(needed == count)
+            def _(part=part, count=count):
+                dense(part, count)
 
 
 def on_device(queries, key_rows, value_rows, doc_lengths):
@@ -118,8 +124,12 @@
     block_ids = jnp.stack([my_shard, 2 * shards - 1 - my_shard]).astype(jnp.int32)
     positions = block_ids[:, None] * half_rows + jnp.arange(half_rows, dtype=jnp.int32)[None, :]
     starts = doc_start(positions.reshape(-1), doc_ends, doc_lengths).astype(jnp.int32)
-    needed = 1 + jnp.clip((block_ids * half_rows - starts[::half_rows] + half_rows - 1) // half_rows, 0, lookback)
-    block_ids = jnp.concatenate([block_ids, needed.astype(jnp.int32)])
+    sub_rows = half_rows // 2
+    firsts = starts.reshape(2, 2, sub_rows)[:, :, 0]
+    needed = 1 + jnp.clip(
+        (block_ids[:, None] * half_rows - firsts + half_rows - 1) // half_rows, 0, lookback
+    )
+    block_ids = jnp.concatenate([block_ids, needed.reshape(-1).astype(jnp.int32)])
     starts = starts.reshape(2, half_rows, 1)
 
     kernel = functools.partial(

time: 107 us -> 116 us (1.084)
  Pallas kernels: 11.8 us -> 20.8 us
    pallas_call x1, Pallas kernels: 11.8 us -> 20.8 us  [on_device(): pl.pallas_call(kernel, out_shape=jax.ShapeDtypeStruct(head_queries.shape,...]
where the time goes in v1:
time: 116 us; the launch traced here: 115 us
  starting transfers between devices  35.5 us (31%)
  blocking collectives  29.3 us (25%)
  Pallas kernels  20.8 us (18%)
  waiting for transfers between devices  16.6 us (14%)
  local copies, waits for them, and re-layouts  8.31 us (7%)
  other arithmetic  4.46 us (4%)
    all_to_all x1, blocking collectives, on_device(): lax.all_to_all(merged, 'kvh', split_axis=0, concat_axis=1, tiled=True)  29.3 us
    ppermute x8, starting transfers between devices, shifted(): return lax.ppermute(block, axis, route)  25.6 us
    pallas_call x1, Pallas kernels, on_device(): pl.pallas_call(kernel, out_shape=jax.ShapeDtypeStruct(head_queries.shape,...  20.8 us
    ppermute x8, waiting for transfers between devices, shifted(): return lax.ppermute(block, axis, route)  15.9 us
    all_to_all x1, starting transfers between devices, on_device(): lax.all_to_all(kv_local, 'kvh', split_axis=1, concat_axis=0, tiled=True)  4.24 us
    all_to_all x1, starting transfers between devices, on_device(): lax.all_to_all(queries, 'kvh', split_axis=1, concat_axis=0, tiled=True)  3.61 us
    all_to_all x1, local copies, waits for them, and re-layouts, on_device(): lax.all_to_all(queries, 'kvh', split_axis=1, concat_axis=0, tiled=True)  3.14 us
  transfers between devices with their start and end apart: 13, of which 5 were waited for; matrix products, arithmetic and copies ran while one was open for 7% of the time, Pallas kernels for 0%

profile of v1, /device:TPU:0, one launch (start us, length us, event | category | flops | bytes accessed | tf_op | source)
XLA Modules:
  0.0 115.2 jit_solution(13414437185128032018)
XLA Ops:
  0.0 1.0 copy_bitcast_fusion.1
  1.0 0.7 pad_maximum_fusion.1
  1.7 4.2 %all-to-all-start.1 = ((bf16[64,4,512]{2,0,1:T(8,128)(2,1)}), bf16[64,4,512]{2,0,1:T(8,128)(2,1)S(1)}, u32[]{:S(2)}, u32[]{:S(2)}) async-start(bf16[64,4,512]{2,0,1:T(8,128)(2,1)} %pad_maximum_fusion.1), calls=%async_computation.1 | async-start | bytes 524288 | tf_op jit(solution)/shard_map/all_to_all | solution.py:89
  6.0 0.1 add_multiply_fusion
  6.0 0.1 add_bitcast_fusion
  6.1 0.1 sub.40
  6.2 0.1 sub.41
  6.3 0.8 reduce-window.8
  7.1 0.7 select_reduce_fusion
  7.8 0.1 reshape.84
  7.9 0.1 slice_reduce_fusion
  8.1 0.1 squeeze.3
  8.1 3.1 %copy.31 = bf16[8,4,8,4096]{3,2,0,1:T(8,128)(2,1)} copy(bf16[8,4,8,4096]{3,2,1,0:T(8,128)(2,1)} %bitcast.45) | data formatting | bytes 4194304 | tf_op jit(solution)/shard_map/all_to_all | solution.py:83
  11.3 0.7 all-to-all-done.1
  12.0 3.6 %all-to-all-start = ((bf16[64,4,4096]{2,0,1:T(8,128)(2,1)}), bf16[64,4,4096]{2,0,1:T(8,128)(2,1)S(1)}, u32[]{:S(2)}, u32[]{:S(2)}) async-start(bf16[64,4,4096]{2,0,1:T(8,128)(2,1)} %bitcast.30), calls=%async_computation | async-start | bytes 4194304 | tf_op jit(solution)/shard_map/all_to_all | solution.py:83
  15.6 1.3 %collective-permute-start.4 = (bf16[128,512]{1,0:T(8,128)(2,1)S(1)}, bf16[128,512]{1,0:T(8,128)(2,1)S(1)}, u32[]{:S(2)}, u32[]{:S(2)}) collective-permute-start(bf16[128,512]{1,0:T(8,128)(2,1)S(1)} %bitcast.49), channel_id=1, source_target_pairs={{16,0},{20,4},{24,8},{28,12},{17,1},{21,5},{25,9},{29,13},{18,2},{... | collective-permute-start | bytes 393224 | tf_op jit(solution)/shard_map/ppermute | solution.py:17
  16.9 0.7 collective-permute-start.5
  17.7 0.8 copy.22.start_ref
  18.5 0.6 pad_add_fusion.blocks_ref
  19.1 9.8 %collective-permute-start = (bf16[128,512]{1,0:T(8,128)(2,1)S(1)}, bf16[128,512]{1,0:T(8,128)(2,1)S(1)}, u32[]{:S(2)}, u32[]{:S(2)}) collective-permute-start(bf16[128,512]{1,0:T(8,128)(2,1)S(1)} %bitcast.35), channel_id=1, source_target_pairs={{0,16},{4,20},{8,24},{12,28},{1,17},{5,21},{9,25},{13,29},{2,18},{... | collective-permute-start | bytes 393224 | tf_op jit(solution)/shard_map/ppermute | solution.py:17
  28.8 1.9 %collective-permute-start.1 = (bf16[128,512]{1,0:T(8,128)(2,1)S(1)}, bf16[128,512]{1,0:T(8,128)(2,1)S(1)}, u32[]{:S(2)}, u32[]{:S(2)}) collective-permute-start(bf16[128,512]{1,0:T(8,128)(2,1)S(1)} %bitcast.36), channel_id=1, source_target_pairs={{0,12},{4,16},{8,20},{12,24},{16,28},{1,13},{5,17},{9,21},{13,25},... | collective-permute-start | bytes 393224 | tf_op jit(solution)/shard_map/ppermute | solution.py:17
  30.8 1.8 %collective-permute-start.2 = (bf16[128,512]{1,0:T(8,128)(2,1)S(1)}, bf16[128,512]{1,0:T(8,128)(2,1)S(1)}, u32[]{:S(2)}, u32[]{:S(2)}) collective-permute-start(bf16[128,512]{1,0:T(8,128)(2,1)S(1)} %bitcast.37), channel_id=1, source_target_pairs={{0,8},{4,12},{8,16},{12,20},{16,24},{20,28},{1,9},{5,13},{9,17},{1... | collective-permute-start | bytes 393224 | tf_op jit(solution)/shard_map/ppermute | solution.py:17
  32.6 0.0 collective-permute-done.4
  32.6 1.3 %collective-permute-start.6 = (bf16[128,512]{1,0:T(8,128)(2,1)S(1)}, bf16[128,512]{1,0:T(8,128)(2,1)S(1)}, u32[]{:S(2)}, u32[]{:S(2)}) collective-permute-start(bf16[128,512]{1,0:T(8,128)(2,1)S(1)} %bitcast.50), channel_id=1, source_target_pairs={{12,0},{16,4},{20,8},{24,12},{28,16},{13,1},{17,5},{21,9},{25,13},... | collective-permute-start | bytes 393224 | tf_op jit(solution)/shard_map/ppermute | solution.py:17
  33.9 0.0 collective-permute-done.5
  33.9 0.7 collective-permute-start.7
  34.6 0.1 select_dynamic-update-slice_fusion.3
  34.7 5.7 %collective-permute-done.6 = bf16[128,512]{1,0:T(8,128)(2,1)S(1)} collective-permute-done((bf16[128,512]{1,0:T(8,128)(2,1)S(1)}, bf16[128,512]{1,0:T(8,128)(2,1)S(1)}, u32[]{:S(2)}, u32[]{:S(2)}) %collective-permute-start.6) | collective-permute-done | bytes 131104 | tf_op jit(solution)/shard_map/ppermute | solution.py:17
  40.4 1.3 %collective-permute-start.8 = (bf16[128,512]{1,0:T(8,128)(2,1)S(1)}, bf16[128,512]{1,0:T(8,128)(2,1)S(1)}, u32[]{:S(2)}, u32[]{:S(2)}) collective-permute-start(bf16[128,512]{1,0:T(8,128)(2,1)S(1)} %bitcast.51), channel_id=1, source_target_pairs={{8,0},{12,4},{16,8},{20,12},{24,16},{28,20},{9,1},{13,5},{17,9},{2... | collective-permute-start | bytes 393224 | tf_op jit(solution)/shard_map/ppermute | solution.py:17
  41.6 0.0 collective-permute-done.7
  41.7 0.7 collective-permute-start.9
  42.3 0.1 select_dynamic-update-slice_fusion.2
  42.4 4.8 %collective-permute-done.8 = bf16[128,512]{1,0:T(8,128)(2,1)S(1)} collective-permute-done((bf16[128,512]{1,0:T(8,128)(2,1)S(1)}, bf16[128,512]{1,0:T(8,128)(2,1)S(1)}, u32[]{:S(2)}, u32[]{:S(2)}) %collective-permute-start.8) | collective-permute-done | bytes 131104 | tf_op jit(solution)/shard_map/ppermute | solution.py:17
  47.2 6.9 %collective-permute-start.3 = (bf16[128,512]{1,0:T(8,128)(2,1)S(1)}, bf16[128,512]{1,0:T(8,128)(2,1)S(1)}, u32[]{:S(2)}, u32[]{:S(2)}) collective-permute-start(bf16[128,512]{1,0:T(8,128)(2,1)S(1)} %bitcast.42), channel_id=1, source_target_pairs={{0,4},{4,8},{8,12},{12,16},{16,20},{20,24},{24,28},{1,5},{5,9},{9,... | collective-permute-start | bytes 393224 | tf_op jit(solution)/shard_map/ppermute | solution.py:17
  54.2 0.0 collective-permute-done.9
  54.2 1.3 %collective-permute-start.10 = (bf16[128,512]{1,0:T(8,128)(2,1)S(1)}, bf16[128,512]{1,0:T(8,128)(2,1)S(1)}, u32[]{:S(2)}, u32[]{:S(2)}) collective-permute-start(bf16[128,512]{1,0:T(8,128)(2,1)S(1)} %bitcast.52), channel_id=1, source_target_pairs={{4,0},{8,4},{12,8},{16,12},{20,16},{24,20},{28,24},{5,1},{9,5},{13... | collective-permute-start | bytes 393224 | tf_op jit(solution)/shard_map/ppermute | solution.py:17
  55.5 0.1 select_dynamic-update-slice_fusion.1
  55.5 0.0 collective-permute-done
  55.6 0.0 collective-permute-done.1
  55.6 0.0 collective-permute-done.2
  55.6 2.4 %collective-permute-done.3 = bf16[128,512]{1,0:T(8,128)(2,1)S(1)} collective-permute-done((bf16[128,512]{1,0:T(8,128)(2,1)S(1)}, bf16[128,512]{1,0:T(8,128)(2,1)S(1)}, u32[]{:S(2)}, u32[]{:S(2)}) %collective-permute-start.3) | collective-permute-done | bytes 131104 | tf_op jit(solution)/shard_map/ppermute | solution.py:17
  58.1 3.0 %collective-permute-done.10 = bf16[128,512]{1,0:T(8,128)(2,1)S(1)} collective-permute-done((bf16[128,512]{1,0:T(8,128)(2,1)S(1)}, bf16[128,512]{1,0:T(8,128)(2,1)S(1)}, u32[]{:S(2)}, u32[]{:S(2)}) %collective-permute-start.10) | collective-permute-done | bytes 131104 | tf_op jit(solution)/shard_map/ppermute | solution.py:17
  61.1 1.2 %pad_maximum_fusion.k_ref.v_ref = bf16[2,640,512]{2,1,0:T(8,128)(2,1)} fusion(bf16[1,640,512]{2,1,0:T(8,128)(2,1)S(1)} %bitcast.48, bf16[1,640,512]{2,1,0:T(8,128)(2,1)S(1)} %bitcast.47), kind=kLoop, calls=%fused_computation.1 | loop fusion | flops 655360 | bytes 2621440 | tf_op jit(solution)/shard_map/stack | solution.py:119
  62.3 0.0 all-to-all-done
  62.3 0.0 copy-start
  62.3 1.3 %copy-done = bf16[64,4,4096]{2,0,1:T(8,128)(2,1)} copy-done((bf16[64,4,4096]{2,0,1:T(8,128)(2,1)}, bf16[64,4,4096]{2,0,1:T(8,128)(2,1)S(1)}, u32[]{:S(2)}) %copy-start) | copy-done | bytes 2097176
  63.6 20.8 %shard_map.46 = bf16[256,4096]{1,0:T(8,128)(2,1)} custom-call(s32[6]{0:T(128)} %pad_add_fusion.blocks_ref, bf16[256,4096]{1,0:T(8,128)(2,1)} %bitcast.31, s32[2,128,1]{2,1,0:T(8,128)} %copy.22.start_ref, bf16[2,640,512]{2,1,0:T(8,128)(2,1)} %pad_maximum_fusion.k_ref.v_ref, bf16[2,640,512]{2,1,0:T(8,128)(2,1)} %pad_maximum_fusion.k_ref.v_ref), custom_call_target="tpu_custom_call" | custom-call | tf_op jit(solution)/shard_map/pallas_call | solution.py:143
  84.4 29.3 %all_to_all.53 = bf16[4,64,4096]{2,1,0:T(8,128)(2,1)S(1)} all-to-all(bf16[4,64,4096]{2,1,0:T(8,128)(2,1)} %bitcast.32), channel_id=1, replica_groups=mesh['seq'=8,'kvh'=4] {'kvh'}, dimensions={0} | all-to-all | bytes 4194304 | tf_op jit(solution)/shard_map/all_to_all | solution.py:162
  113.6 1.5 %copy.27 = bf16[4,8,8,4096]{3,2,0,1:T(8,128)(2,1)} copy(bf16[4,8,8,4096]{3,2,1,0:T(8,128)(2,1)S(1)} %bitcast.33) | data formatting | bytes 4194304 | tf_op jit(solution)/shard_map/all_to_all | solution.py:162
  (8 shorter events, 0.1 us)
Async XLA Ops:
  1.7 10.3 %all-to-all-start.1 = ((bf16[64,4,512]{2,0,1:T(8,128)(2,1)}), bf16[64,4,512]{2,0,1:T(8,128)(2,1)S(1)}, u32[]{:S(2)}, u32[]{:S(2)}) async-start(bf16[64,4,512]{2,0,1:T(8,128)(2,1)} %pad_maximum_fusion.1), calls=%async_computation.1 | async-start | bytes 524288 | tf_op jit(solution)/shard_map/all_to_all | solution.py:89
  12.0 50.3 %all-to-all-start = ((bf16[64,4,4096]{2,0,1:T(8,128)(2,1)}), bf16[64,4,4096]{2,0,1:T(8,128)(2,1)S(1)}, u32[]{:S(2)}, u32[]{:S(2)}) async-start(bf16[64,4,4096]{2,0,1:T(8,128)(2,1)} %bitcast.30), calls=%async_computation | async-start | bytes 4194304 | tf_op jit(solution)/shard_map/all_to_all | solution.py:83
  15.6 16.9 %collective-permute-start.4 = (bf16[128,512]{1,0:T(8,128)(2,1)S(1)}, bf16[128,512]{1,0:T(8,128)(2,1)S(1)}, u32[]{:S(2)}, u32[]{:S(2)}) collective-permute-start(bf16[128,512]{1,0:T(8,128)(2,1)S(1)} %bitcast.49), channel_id=1, source_target_pairs={{16,0},{20,4},{24,8},{28,12},{17,1},{21,5},{25,9},{29,13},{18,2},{... | collective-permute-start | bytes 393224 | tf_op jit(solution)/shard_map/ppermute | solution.py:17
  16.9 17.0 %collective-permute-start.5 = (bf16[128,512]{1,0:T(8,128)(2,1)S(1)}, bf16[128,512]{1,0:T(8,128)(2,1)S(1)}, u32[]{:S(2)}, u32[]{:S(2)}) collective-permute-start(bf16[128,512]{1,0:T(8,128)(2,1)S(1)} %bitcast.34), channel_id=1, source_target_pairs={{16,28},{20,24},{24,20},{28,16},{17,29},{21,25},{25,21},{29,17},{1... | collective-permute-start | bytes 393224 | tf_op jit(solution)/shard_map/ppermute | solution.py:112
  19.1 36.5 %collective-permute-start = (bf16[128,512]{1,0:T(8,128)(2,1)S(1)}, bf16[128,512]{1,0:T(8,128)(2,1)S(1)}, u32[]{:S(2)}, u32[]{:S(2)}) collective-permute-start(bf16[128,512]{1,0:T(8,128)(2,1)S(1)} %bitcast.35), channel_id=1, source_target_pairs={{0,16},{4,20},{8,24},{12,28},{1,17},{5,21},{9,25},{13,29},{2,18},{... | collective-permute-start | bytes 393224 | tf_op jit(solution)/shard_map/ppermute | solution.py:17
  28.8 26.7 %collective-permute-start.1 = (bf16[128,512]{1,0:T(8,128)(2,1)S(1)}, bf16[128,512]{1,0:T(8,128)(2,1)S(1)}, u32[]{:S(2)}, u32[]{:S(2)}) collective-permute-start(bf16[128,512]{1,0:T(8,128)(2,1)S(1)} %bitcast.36), channel_id=1, source_target_pairs={{0,12},{4,16},{8,20},{12,24},{16,28},{1,13},{5,17},{9,21},{13,25},... | collective-permute-start | bytes 393224 | tf_op jit(solution)/shard_map/ppermute | solution.py:17
  30.8 24.8 %collective-permute-start.2 = (bf16[128,512]{1,0:T(8,128)(2,1)S(1)}, bf16[128,512]{1,0:T(8,128)(2,1)S(1)}, u32[]{:S(2)}, u32[]{:S(2)}) collective-permute-start(bf16[128,512]{1,0:T(8,128)(2,1)S(1)} %bitcast.37), channel_id=1, source_target_pairs={{0,8},{4,12},{8,16},{12,20},{16,24},{20,28},{1,9},{5,13},{9,17},{1... | collective-permute-start | bytes 393224 | tf_op jit(solution)/shard_map/ppermute | solution.py:17
  32.6 7.8 %collective-permute-start.6 = (bf16[128,512]{1,0:T(8,128)(2,1)S(1)}, bf16[128,512]{1,0:T(8,128)(2,1)S(1)}, u32[]{:S(2)}, u32[]{:S(2)}) collective-permute-start(bf16[128,512]{1,0:T(8,128)(2,1)S(1)} %bitcast.50), channel_id=1, source_target_pairs={{12,0},{16,4},{20,8},{24,12},{28,16},{13,1},{17,5},{21,9},{25,13},... | collective-permute-start | bytes 393224 | tf_op jit(solution)/shard_map/ppermute | solution.py:17
  33.9 7.7 %collective-permute-start.7 = (bf16[128,512]{1,0:T(8,128)(2,1)S(1)}, bf16[128,512]{1,0:T(8,128)(2,1)S(1)}, u32[]{:S(2)}, u32[]{:S(2)}) collective-permute-start(bf16[128,512]{1,0:T(8,128)(2,1)S(1)} %bitcast.38), channel_id=1, source_target_pairs={{20,28},{28,20},{21,29},{29,21},{22,30},{30,22},{23,31},{31,23}} | collective-permute-start | bytes 393224 | tf_op jit(solution)/shard_map/ppermute | solution.py:112
  40.4 6.8 %collective-permute-start.8 = (bf16[128,512]{1,0:T(8,128)(2,1)S(1)}, bf16[128,512]{1,0:T(8,128)(2,1)S(1)}, u32[]{:S(2)}, u32[]{:S(2)}) collective-permute-start(bf16[128,512]{1,0:T(8,128)(2,1)S(1)} %bitcast.51), channel_id=1, source_target_pairs={{8,0},{12,4},{16,8},{20,12},{24,16},{28,20},{9,1},{13,5},{17,9},{2... | collective-permute-start | bytes 393224 | tf_op jit(solution)/shard_map/ppermute | solution.py:17
  41.7 12.5 %collective-permute-start.9 = (bf16[128,512]{1,0:T(8,128)(2,1)S(1)}, bf16[128,512]{1,0:T(8,128)(2,1)S(1)}, u32[]{:S(2)}, u32[]{:S(2)}) collective-permute-start(bf16[128,512]{1,0:T(8,128)(2,1)S(1)} %bitcast.40), channel_id=1, source_target_pairs={{24,28},{28,24},{25,29},{29,25},{26,30},{30,26},{27,31},{31,27}} | collective-permute-start | bytes 393224 | tf_op jit(solution)/shard_map/ppermute | solution.py:112
  47.2 10.8 %collective-permute-start.3 = (bf16[128,512]{1,0:T(8,128)(2,1)S(1)}, bf16[128,512]{1,0:T(8,128)(2,1)S(1)}, u32[]{:S(2)}, u32[]{:S(2)}) collective-permute-start(bf16[128,512]{1,0:T(8,128)(2,1)S(1)} %bitcast.42), channel_id=1, source_target_pairs={{0,4},{4,8},{8,12},{12,16},{16,20},{20,24},{24,28},{1,5},{5,9},{9,... | collective-permute-start | bytes 393224 | tf_op jit(solution)/shard_map/ppermute | solution.py:17
  54.2 6.9 %collective-permute-start.10 = (bf16[128,512]{1,0:T(8,128)(2,1)S(1)}, bf16[128,512]{1,0:T(8,128)(2,1)S(1)}, u32[]{:S(2)}, u32[]{:S(2)}) collective-permute-start(bf16[128,512]{1,0:T(8,128)(2,1)S(1)} %bitcast.52), channel_id=1, source_target_pairs={{4,0},{8,4},{12,8},{16,12},{20,16},{24,20},{28,24},{5,1},{9,5},{13... | collective-permute-start | bytes 393224 | tf_op jit(solution)/shard_map/ppermute | solution.py:17
  62.3 1.3 %copy-start = (bf16[64,4,4096]{2,0,1:T(8,128)(2,1)}, bf16[64,4,4096]{2,0,1:T(8,128)(2,1)S(1)}, u32[]{:S(2)}) copy-start(bf16[64,4,4096]{2,0,1:T(8,128)(2,1)S(1)} %all-to-all-done) | copy-start | bytes 6291460

commit v2 on v0

--- a/solution.py
+++ b/solution.py
@@ -46,21 +46,24 @@
         allowed = (key_pos <= row_pos) & (key_pos >= row_start)
         bias = jnp.where(allowed, 0.0, -jnp.inf).astype(jnp.float32)
 
-        def one_member(g, carry):
-            col = pl.multiple_of(g * DH, DH)
-            q_g = q_ref[:, pl.ds(col, DH)]
-            scores = jnp.dot(q_g, kt_buf[:, skip:], preferred_element_type=jnp.float32)
-            scores = scores * scale + bias
-            top = jnp.max(scores, axis=1, keepdims=True)
-            weights = jnp.exp(scores - top)
+        def one_pair(pair, carry):
+            cols = [pl.multiple_of((2 * pair + i) * DH, DH) for i in range(2)]
+            q_two = jnp.concatenate([q_ref[:, pl.ds(c, DH)] for c in cols], axis=0)
+            scores = jnp.dot(q_two, kt_buf[:, skip:], preferred_element_type=jnp.float32)
+            scores = scores.reshape(2, half_rows, span) * scale + bias[None]
+            top = jnp.max(scores, axis=2, keepdims=True)
+            weights = jnp.exp(scores - top).reshape(2 * half_rows, span)
             mixed = jnp.dot(
                 weights.astype(jnp.bfloat16), v_buf[skip:, :], preferred_element_type=jnp.float32
             )
-            total = mixed[:, DH : DH + 1]
-            out_ref[:, pl.ds(col, DH)] = (mixed[:, :DH] / total).astype(out_ref.dtype)
+            normed = mixed[:, :DH] / mixed[:, DH : DH + 1]
+            for i in range(2):
+                out_ref[:, pl.ds(cols[i], DH)] = normed[i * half_rows : (i + 1) * half_rows].astype(
+                    out_ref.dtype
+                )
             return carry
 
-        lax.fori_loop(0, group_size, one_member, 0, unroll=True)
+        lax.fori_loop(0, group_size // 2, one_pair, 0, unroll=True)
 
     for count in range(1, window // half_rows + 1):
 

time: 107 us -> 106 us (level)
  Pallas kernels: 11.8 us -> 10.7 us
    pallas_call x1, Pallas kernels: 11.8 us -> 10.7 us  [on_device(): pl.pallas_call(kernel, out_shape=jax.ShapeDtypeStruct(head_queries.shape,...]
where the time goes in v2:
time: 106 us; the launch traced here: 105 us
  starting transfers between devices  35.5 us (33%)
  blocking collectives  29.3 us (28%)
  waiting for transfers between devices  17 us (16%)
  Pallas kernels  10.7 us (10%)
  local copies, waits for them, and re-layouts  7.93 us (7%)
  other arithmetic  4.48 us (4%)
    all_to_all x1, blocking collectives, on_device(): lax.all_to_all(merged, 'kvh', split_axis=0, concat_axis=1, tiled=True)  29.3 us
    ppermute x8, starting transfers between devices, shifted(): return lax.ppermute(block, axis, route)  25.6 us
    ppermute x8, waiting for transfers between devices, shifted(): return lax.ppermute(block, axis, route)  15.9 us
    pallas_call x1, Pallas kernels, on_device(): pl.pallas_call(kernel, out_shape=jax.ShapeDtypeStruct(head_queries.shape,...  10.7 us
    all_to_all x1, starting transfers between devices, on_device(): lax.all_to_all(kv_local, 'kvh', split_axis=1, concat_axis=0, tiled=True)  4.24 us
    all_to_all x1, starting transfers between devices, on_device(): lax.all_to_all(queries, 'kvh', split_axis=1, concat_axis=0, tiled=True)  3.61 us
    all_to_all x1, local copies, waits for them, and re-layouts, on_device(): lax.all_to_all(queries, 'kvh', split_axis=1, concat_axis=0, tiled=True)  3.13 us
  transfers between devices with their start and end apart: 13, of which 5 were waited for; matrix products, arithmetic and copies ran while one was open for 7% of the time, Pallas kernels for 0%

profile of v2, /device:TPU:0, one launch (start us, length us, event | category | flops | bytes accessed | tf_op | source)
XLA Modules:
  0.0 105.2 jit_solution(14898524414741996596)
XLA Ops:
  0.0 1.0 copy_bitcast_fusion.1
  1.0 0.7 pad_maximum_fusion.1
  1.7 4.2 %all-to-all-start.1 = ((bf16[64,4,512]{2,0,1:T(8,128)(2,1)}), bf16[64,4,512]{2,0,1:T(8,128)(2,1)S(1)}, u32[]{:S(2)}, u32[]{:S(2)}) async-start(bf16[64,4,512]{2,0,1:T(8,128)(2,1)} %pad_maximum_fusion.1), calls=%async_computation.1 | async-start | bytes 524288 | tf_op jit(solution)/shard_map/all_to_all | solution.py:86
  5.9 0.1 add_multiply_fusion
  6.0 0.1 add_bitcast_fusion
  6.1 0.8 reduce-window.8
  6.9 0.7 select_reduce_fusion
  7.7 0.1 slice.15
  7.8 3.1 %copy.26 = bf16[8,4,8,4096]{3,2,0,1:T(8,128)(2,1)} copy(bf16[8,4,8,4096]{3,2,1,0:T(8,128)(2,1)} %bitcast.45) | data formatting | bytes 4194304 | tf_op jit(solution)/shard_map/all_to_all | solution.py:80
  10.9 1.1 %all-to-all-done.1 = bf16[64,4,512]{2,0,1:T(8,128)(2,1)S(1)} async-done(((bf16[64,4,512]{2,0,1:T(8,128)(2,1)}), bf16[64,4,512]{2,0,1:T(8,128)(2,1)S(1)}, u32[]{:S(2)}, u32[]{:S(2)}) %all-to-all-start.1) | async-done | bytes 262176 | tf_op jit(solution)/shard_map/all_to_all | solution.py:86
  12.0 3.6 %all-to-all-start = ((bf16[64,4,4096]{2,0,1:T(8,128)(2,1)}), bf16[64,4,4096]{2,0,1:T(8,128)(2,1)S(1)}, u32[]{:S(2)}, u32[]{:S(2)}) async-start(bf16[64,4,4096]{2,0,1:T(8,128)(2,1)} %bitcast.30), calls=%async_computation | async-start | bytes 4194304 | tf_op jit(solution)/shard_map/all_to_all | solution.py:80
  15.6 1.3 %collective-permute-start.4 = (bf16[128,512]{1,0:T(8,128)(2,1)S(1)}, bf16[128,512]{1,0:T(8,128)(2,1)S(1)}, u32[]{:S(2)}, u32[]{:S(2)}) collective-permute-start(bf16[128,512]{1,0:T(8,128)(2,1)S(1)} %bitcast.49), channel_id=1, source_target_pairs={{16,0},{20,4},{24,8},{28,12},{17,1},{21,5},{25,9},{29,13},{18,2},{... | collective-permute-start | bytes 393224 | tf_op jit(solution)/shard_map/ppermute | solution.py:17
  16.9 0.7 collective-permute-start.5
  17.6 0.1 clamp_add_fusion
  17.7 0.8 copy.17.start_ref
  18.5 0.6 pad_add_fusion.blocks_ref
  19.1 9.8 %collective-permute-start = (bf16[128,512]{1,0:T(8,128)(2,1)S(1)}, bf16[128,512]{1,0:T(8,128)(2,1)S(1)}, u32[]{:S(2)}, u32[]{:S(2)}) collective-permute-start(bf16[128,512]{1,0:T(8,128)(2,1)S(1)} %bitcast.35), channel_id=1, source_target_pairs={{0,16},{4,20},{8,24},{12,28},{1,17},{5,21},{9,25},{13,29},{2,18},{... | collective-permute-start | bytes 393224 | tf_op jit(solution)/shard_map/ppermute | solution.py:17
  28.8 1.9 %collective-permute-start.1 = (bf16[128,512]{1,0:T(8,128)(2,1)S(1)}, bf16[128,512]{1,0:T(8,128)(2,1)S(1)}, u32[]{:S(2)}, u32[]{:S(2)}) collective-permute-start(bf16[128,512]{1,0:T(8,128)(2,1)S(1)} %bitcast.36), channel_id=1, source_target_pairs={{0,12},{4,16},{8,20},{12,24},{16,28},{1,13},{5,17},{9,21},{13,25},... | collective-permute-start | bytes 393224 | tf_op jit(solution)/shard_map/ppermute | solution.py:17
  30.8 1.8 %collective-permute-start.2 = (bf16[128,512]{1,0:T(8,128)(2,1)S(1)}, bf16[128,512]{1,0:T(8,128)(2,1)S(1)}, u32[]{:S(2)}, u32[]{:S(2)}) collective-permute-start(bf16[128,512]{1,0:T(8,128)(2,1)S(1)} %bitcast.37), channel_id=1, source_target_pairs={{0,8},{4,12},{8,16},{12,20},{16,24},{20,28},{1,9},{5,13},{9,17},{1... | collective-permute-start | bytes 393224 | tf_op jit(solution)/shard_map/ppermute | solution.py:17
  32.6 0.0 collective-permute-done.4
  32.6 1.3 %collective-permute-start.6 = (bf16[128,512]{1,0:T(8,128)(2,1)S(1)}, bf16[128,512]{1,0:T(8,128)(2,1)S(1)}, u32[]{:S(2)}, u32[]{:S(2)}) collective-permute-start(bf16[128,512]{1,0:T(8,128)(2,1)S(1)} %bitcast.50), channel_id=1, source_target_pairs={{12,0},{16,4},{20,8},{24,12},{28,16},{13,1},{17,5},{21,9},{25,13},... | collective-permute-start | bytes 393224 | tf_op jit(solution)/shard_map/ppermute | solution.py:17
  33.9 0.0 collective-permute-done.5
  33.9 0.7 collective-permute-start.7
  34.6 0.1 select_dynamic-update-slice_fusion.3
  34.7 5.7 %collective-permute-done.6 = bf16[128,512]{1,0:T(8,128)(2,1)S(1)} collective-permute-done((bf16[128,512]{1,0:T(8,128)(2,1)S(1)}, bf16[128,512]{1,0:T(8,128)(2,1)S(1)}, u32[]{:S(2)}, u32[]{:S(2)}) %collective-permute-start.6) | collective-permute-done | bytes 131104 | tf_op jit(solution)/shard_map/ppermute | solution.py:17
  40.4 1.3 %collective-permute-start.8 = (bf16[128,512]{1,0:T(8,128)(2,1)S(1)}, bf16[128,512]{1,0:T(8,128)(2,1)S(1)}, u32[]{:S(2)}, u32[]{:S(2)}) collective-permute-start(bf16[128,512]{1,0:T(8,128)(2,1)S(1)} %bitcast.51), channel_id=1, source_target_pairs={{8,0},{12,4},{16,8},{20,12},{24,16},{28,20},{9,1},{13,5},{17,9},{2... | collective-permute-start | bytes 393224 | tf_op jit(solution)/shard_map/ppermute | solution.py:17
  41.7 0.0 collective-permute-done.7
  41.7 0.7 collective-permute-start.9
  42.3 0.1 select_dynamic-update-slice_fusion.2
  42.4 4.8 %collective-permute-done.8 = bf16[128,512]{1,0:T(8,128)(2,1)S(1)} collective-permute-done((bf16[128,512]{1,0:T(8,128)(2,1)S(1)}, bf16[128,512]{1,0:T(8,128)(2,1)S(1)}, u32[]{:S(2)}, u32[]{:S(2)}) %collective-permute-start.8) | collective-permute-done | bytes 131104 | tf_op jit(solution)/shard_map/ppermute | solution.py:17
  47.2 6.9 %collective-permute-start.3 = (bf16[128,512]{1,0:T(8,128)(2,1)S(1)}, bf16[128,512]{1,0:T(8,128)(2,1)S(1)}, u32[]{:S(2)}, u32[]{:S(2)}) collective-permute-start(bf16[128,512]{1,0:T(8,128)(2,1)S(1)} %bitcast.42), channel_id=1, source_target_pairs={{0,4},{4,8},{8,12},{12,16},{16,20},{20,24},{24,28},{1,5},{5,9},{9,... | collective-permute-start | bytes 393224 | tf_op jit(solution)/shard_map/ppermute | solution.py:17
  54.2 0.0 collective-permute-done.9
  54.2 1.3 %collective-permute-start.10 = (bf16[128,512]{1,0:T(8,128)(2,1)S(1)}, bf16[128,512]{1,0:T(8,128)(2,1)S(1)}, u32[]{:S(2)}, u32[]{:S(2)}) collective-permute-start(bf16[128,512]{1,0:T(8,128)(2,1)S(1)} %bitcast.52), channel_id=1, source_target_pairs={{4,0},{8,4},{12,8},{16,12},{20,16},{24,20},{28,24},{5,1},{9,5},{13... | collective-permute-start | bytes 393224 | tf_op jit(solution)/shard_map/ppermute | solution.py:17
  55.5 0.1 select_dynamic-update-slice_fusion.1
  55.5 0.0 collective-permute-done
  55.6 0.0 collective-permute-done.1
  55.6 0.0 collective-permute-done.2
  55.6 2.4 %collective-permute-done.3 = bf16[128,512]{1,0:T(8,128)(2,1)S(1)} collective-permute-done((bf16[128,512]{1,0:T(8,128)(2,1)S(1)}, bf16[128,512]{1,0:T(8,128)(2,1)S(1)}, u32[]{:S(2)}, u32[]{:S(2)}) %collective-permute-start.3) | collective-permute-done | bytes 131104 | tf_op jit(solution)/shard_map/ppermute | solution.py:17
  58.1 3.0 %collective-permute-done.10 = bf16[128,512]{1,0:T(8,128)(2,1)S(1)} collective-permute-done((bf16[128,512]{1,0:T(8,128)(2,1)S(1)}, bf16[128,512]{1,0:T(8,128)(2,1)S(1)}, u32[]{:S(2)}, u32[]{:S(2)}) %collective-permute-start.10) | collective-permute-done | bytes 131104 | tf_op jit(solution)/shard_map/ppermute | solution.py:17
  61.1 1.2 %pad_maximum_fusion.k_ref.v_ref = bf16[2,640,512]{2,1,0:T(8,128)(2,1)} fusion(bf16[1,640,512]{2,1,0:T(8,128)(2,1)S(1)} %bitcast.48, bf16[1,640,512]{2,1,0:T(8,128)(2,1)S(1)} %bitcast.47), kind=kLoop, calls=%fused_computation.1 | loop fusion | flops 655360 | bytes 2621440 | tf_op jit(solution)/shard_map/stack | solution.py:116
  62.3 0.0 all-to-all-done
  62.3 0.0 copy-start
  62.3 1.3 %copy-done = bf16[64,4,4096]{2,0,1:T(8,128)(2,1)} copy-done((bf16[64,4,4096]{2,0,1:T(8,128)(2,1)}, bf16[64,4,4096]{2,0,1:T(8,128)(2,1)S(1)}, u32[]{:S(2)}) %copy-start) | copy-done | bytes 2097176
  63.6 10.7 %shard_map.46 = bf16[256,4096]{1,0:T(8,128)(2,1)} custom-call(s32[4]{0:T(128)} %pad_add_fusion.blocks_ref, bf16[256,4096]{1,0:T(8,128)(2,1)} %bitcast.31, s32[2,128,1]{2,1,0:T(8,128)} %copy.17.start_ref, bf16[2,640,512]{2,1,0:T(8,128)(2,1)} %pad_maximum_fusion.k_ref.v_ref, bf16[2,640,512]{2,1,0:T(8,128)(2,1)} %pad_maximum_fusion.k_ref.v_ref), custom_call_target="tpu_custom_call" | custom-call | tf_op jit(solution)/shard_map/pallas_call | solution.py:136
  74.3 29.3 %all_to_all.53 = bf16[4,64,4096]{2,1,0:T(8,128)(2,1)S(1)} all-to-all(bf16[4,64,4096]{2,1,0:T(8,128)(2,1)} %bitcast.32), channel_id=1, replica_groups=mesh['seq'=8,'kvh'=4] {'kvh'}, dimensions={0} | all-to-all | bytes 4194304 | tf_op jit(solution)/shard_map/all_to_all | solution.py:155
  103.6 1.5 %copy.22 = bf16[4,8,8,4096]{3,2,0,1:T(8,128)(2,1)} copy(bf16[4,8,8,4096]{3,2,1,0:T(8,128)(2,1)S(1)} %bitcast.33) | data formatting | bytes 4194304 | tf_op jit(solution)/shard_map/all_to_all | solution.py:155
  (7 shorter events, 0.1 us)
Async XLA Ops:
  1.7 10.3 %all-to-all-start.1 = ((bf16[64,4,512]{2,0,1:T(8,128)(2,1)}), bf16[64,4,512]{2,0,1:T(8,128)(2,1)S(1)}, u32[]{:S(2)}, u32[]{:S(2)}) async-start(bf16[64,4,512]{2,0,1:T(8,128)(2,1)} %pad_maximum_fusion.1), calls=%async_computation.1 | async-start | bytes 524288 | tf_op jit(solution)/shard_map/all_to_all | solution.py:86
  12.0 50.3 %all-to-all-start = ((bf16[64,4,4096]{2,0,1:T(8,128)(2,1)}), bf16[64,4,4096]{2,0,1:T(8,128)(2,1)S(1)}, u32[]{:S(2)}, u32[]{:S(2)}) async-start(bf16[64,4,4096]{2,0,1:T(8,128)(2,1)} %bitcast.30), calls=%async_computation | async-start | bytes 4194304 | tf_op jit(solution)/shard_map/all_to_all | solution.py:80
  15.6 17.0 %collective-permute-start.4 = (bf16[128,512]{1,0:T(8,128)(2,1)S(1)}, bf16[128,512]{1,0:T(8,128)(2,1)S(1)}, u32[]{:S(2)}, u32[]{:S(2)}) collective-permute-start(bf16[128,512]{1,0:T(8,128)(2,1)S(1)} %bitcast.49), channel_id=1, source_target_pairs={{16,0},{20,4},{24,8},{28,12},{17,1},{21,5},{25,9},{29,13},{18,2},{... | collective-permute-start | bytes 393224 | tf_op jit(solution)/shard_map/ppermute | solution.py:17
  16.9 17.0 %collective-permute-start.5 = (bf16[128,512]{1,0:T(8,128)(2,1)S(1)}, bf16[128,512]{1,0:T(8,128)(2,1)S(1)}, u32[]{:S(2)}, u32[]{:S(2)}) collective-permute-start(bf16[128,512]{1,0:T(8,128)(2,1)S(1)} %bitcast.34), channel_id=1, source_target_pairs={{16,28},{20,24},{24,20},{28,16},{17,29},{21,25},{25,21},{29,17},{1... | collective-permute-start | bytes 393224 | tf_op jit(solution)/shard_map/ppermute | solution.py:109
  19.1 36.5 %collective-permute-start = (bf16[128,512]{1,0:T(8,128)(2,1)S(1)}, bf16[128,512]{1,0:T(8,128)(2,1)S(1)}, u32[]{:S(2)}, u32[]{:S(2)}) collective-permute-start(bf16[128,512]{1,0:T(8,128)(2,1)S(1)} %bitcast.35), channel_id=1, source_target_pairs={{0,16},{4,20},{8,24},{12,28},{1,17},{5,21},{9,25},{13,29},{2,18},{... | collective-permute-start | bytes 393224 | tf_op jit(solution)/shard_map/ppermute | solution.py:17
  28.8 26.7 %collective-permute-start.1 = (bf16[128,512]{1,0:T(8,128)(2,1)S(1)}, bf16[128,512]{1,0:T(8,128)(2,1)S(1)}, u32[]{:S(2)}, u32[]{:S(2)}) collective-permute-start(bf16[128,512]{1,0:T(8,128)(2,1)S(1)} %bitcast.36), channel_id=1, source_target_pairs={{0,12},{4,16},{8,20},{12,24},{16,28},{1,13},{5,17},{9,21},{13,25},... | collective-permute-start | bytes 393224 | tf_op jit(solution)/shard_map/ppermute | solution.py:17
  30.8 24.8 %collective-permute-start.2 = (bf16[128,512]{1,0:T(8,128)(2,1)S(1)}, bf16[128,512]{1,0:T(8,128)(2,1)S(1)}, u32[]{:S(2)}, u32[]{:S(2)}) collective-permute-start(bf16[128,512]{1,0:T(8,128)(2,1)S(1)} %bitcast.37), channel_id=1, source_target_pairs={{0,8},{4,12},{8,16},{12,20},{16,24},{20,28},{1,9},{5,13},{9,17},{1... | collective-permute-start | bytes 393224 | tf_op jit(solution)/shard_map/ppermute | solution.py:17
  32.6 7.8 %collective-permute-start.6 = (bf16[128,512]{1,0:T(8,128)(2,1)S(1)}, bf16[128,512]{1,0:T(8,128)(2,1)S(1)}, u32[]{:S(2)}, u32[]{:S(2)}) collective-permute-start(bf16[128,512]{1,0:T(8,128)(2,1)S(1)} %bitcast.50), channel_id=1, source_target_pairs={{12,0},{16,4},{20,8},{24,12},{28,16},{13,1},{17,5},{21,9},{25,13},... | collective-permute-start | bytes 393224 | tf_op jit(solution)/shard_map/ppermute | solution.py:17
  33.9 7.7 %collective-permute-start.7 = (bf16[128,512]{1,0:T(8,128)(2,1)S(1)}, bf16[128,512]{1,0:T(8,128)(2,1)S(1)}, u32[]{:S(2)}, u32[]{:S(2)}) collective-permute-start(bf16[128,512]{1,0:T(8,128)(2,1)S(1)} %bitcast.38), channel_id=1, source_target_pairs={{20,28},{28,20},{21,29},{29,21},{22,30},{30,22},{23,31},{31,23}} | collective-permute-start | bytes 393224 | tf_op jit(solution)/shard_map/ppermute | solution.py:109
  40.4 6.8 %collective-permute-start.8 = (bf16[128,512]{1,0:T(8,128)(2,1)S(1)}, bf16[128,512]{1,0:T(8,128)(2,1)S(1)}, u32[]{:S(2)}, u32[]{:S(2)}) collective-permute-start(bf16[128,512]{1,0:T(8,128)(2,1)S(1)} %bitcast.51), channel_id=1, source_target_pairs={{8,0},{12,4},{16,8},{20,12},{24,16},{28,20},{9,1},{13,5},{17,9},{2... | collective-permute-start | bytes 393224 | tf_op jit(solution)/shard_map/ppermute | solution.py:17
  41.7 12.5 %collective-permute-start.9 = (bf16[128,512]{1,0:T(8,128)(2,1)S(1)}, bf16[128,512]{1,0:T(8,128)(2,1)S(1)}, u32[]{:S(2)}, u32[]{:S(2)}) collective-permute-start(bf16[128,512]{1,0:T(8,128)(2,1)S(1)} %bitcast.40), channel_id=1, source_target_pairs={{24,28},{28,24},{25,29},{29,25},{26,30},{30,26},{27,31},{31,27}} | collective-permute-start | bytes 393224 | tf_op jit(solution)/shard_map/ppermute | solution.py:109
  47.2 10.8 %collective-permute-start.3 = (bf16[128,512]{1,0:T(8,128)(2,1)S(1)}, bf16[128,512]{1,0:T(8,128)(2,1)S(1)}, u32[]{:S(2)}, u32[]{:S(2)}) collective-permute-start(bf16[128,512]{1,0:T(8,128)(2,1)S(1)} %bitcast.42), channel_id=1, source_target_pairs={{0,4},{4,8},{8,12},{12,16},{16,20},{20,24},{24,28},{1,5},{5,9},{9,... | collective-permute-start | bytes 393224 | tf_op jit(solution)/shard_map/ppermute | solution.py:17
  54.2 6.9 %collective-permute-start.10 = (bf16[128,512]{1,0:T(8,128)(2,1)S(1)}, bf16[128,512]{1,0:T(8,128)(2,1)S(1)}, u32[]{:S(2)}, u32[]{:S(2)}) collective-permute-start(bf16[128,512]{1,0:T(8,128)(2,1)S(1)} %bitcast.52), channel_id=1, source_target_pairs={{4,0},{8,4},{12,8},{16,12},{20,16},{24,20},{28,24},{5,1},{9,5},{13... | collective-permute-start | bytes 393224 | tf_op jit(solution)/shard_map/ppermute | solution.py:17
  62.3 1.3 %copy-start = (bf16[64,4,4096]{2,0,1:T(8,128)(2,1)}, bf16[64,4,4096]{2,0,1:T(8,128)(2,1)S(1)}, u32[]{:S(2)}) copy-start(bf16[64,4,4096]{2,0,1:T(8,128)(2,1)S(1)} %all-to-all-done) | copy-start | bytes 6291460

commit v3 on v2

--- a/solution.py
+++ b/solution.py
@@ -9,6 +9,7 @@
 from jax.sharding import PartitionSpec as P
 
 DH = 128
+BUNCH = 4
 
 
 def shifted(block, axis, distance):
@@ -47,23 +48,23 @@
         bias = jnp.where(allowed, 0.0, -jnp.inf).astype(jnp.float32)
 
         def one_pair(pair, carry):
-            cols = [pl.multiple_of((2 * pair + i) * DH, DH) for i in range(2)]
+            cols = [pl.multiple_of((BUNCH * pair + i) * DH, DH) for i in range(BUNCH)]
             q_two = jnp.concatenate([q_ref[:, pl.ds(c, DH)] for c in cols], axis=0)
             scores = jnp.dot(q_two, kt_buf[:, skip:], preferred_element_type=jnp.float32)
-            scores = scores.reshape(2, half_rows, span) * scale + bias[None]
+            scores = scores.reshape(BUNCH, half_rows, span) * scale + bias[None]
             top = jnp.max(scores, axis=2, keepdims=True)
-            weights = jnp.exp(scores - top).reshape(2 * half_rows, span)
+            weights = jnp.exp(scores - top).reshape(BUNCH * half_rows, span)
             mixed = jnp.dot(
                 weights.astype(jnp.bfloat16), v_buf[skip:, :], preferred_element_type=jnp.float32
             )
             normed = mixed[:, :DH] / mixed[:, DH : DH + 1]
-            for i in range(2):
+            for i in range(BUNCH):
                 out_ref[:, pl.ds(cols[i], DH)] = normed[i * half_rows : (i + 1) * half_rows].astype(
                     out_ref.dtype
                 )
             return carry
 
-        lax.fori_loop(0, group_size // 2, one_pair, 0, unroll=True)
+        lax.fori_loop(0, group_size // BUNCH, one_pair, 0, unroll=True)
 
     for count in range(1, window // half_rows + 1):
 

time: 106 us -> 105 us (level)
  Pallas kernels: 10.7 us -> 8.95 us
    pallas_call x1, Pallas kernels: 10.7 us -> 8.95 us  [on_device(): pl.pallas_call(kernel, out_shape=jax.ShapeDtypeStruct(head_queries.shape,...]
  transfers between devices with their start and end apart: 13 -> 13, of which waited for: 5 -> 5; matrix products, arithmetic and copies ran while one was open for 7% -> 8% of each run, Pallas kernels for 0% -> 0%
where the time goes in v3:
time: 105 us; the launch traced here: 103 us
  starting transfers between devices  35.5 us (34%)
  blocking collectives  29.3 us (28%)
  waiting for transfers between devices  17 us (16%)
  Pallas kernels  8.95 us (9%)
  local copies, waits for them, and re-layouts  7.93 us (8%)
  other arithmetic  4.48 us (4%)
    all_to_all x1, blocking collectives, on_device(): lax.all_to_all(merged, 'kvh', split_axis=0, concat_axis=1, tiled=True)  29.3 us
    ppermute x8, starting transfers between devices, shifted(): return lax.ppermute(block, axis, route)  25.6 us
    ppermute x8, waiting for transfers between devices, shifted(): return lax.ppermute(block, axis, route)  15.9 us
    pallas_call x1, Pallas kernels, on_device(): pl.pallas_call(kernel, out_shape=jax.ShapeDtypeStruct(head_queries.shape,...  8.95 us
    all_to_all x1, starting transfers between devices, on_device(): lax.all_to_all(kv_local, 'kvh', split_axis=1, concat_axis=0, tiled=True)  4.24 us
    all_to_all x1, starting transfers between devices, on_device(): lax.all_to_all(queries, 'kvh', split_axis=1, concat_axis=0, tiled=True)  3.61 us
    all_to_all x1, local copies, waits for them, and re-layouts, on_device(): lax.all_to_all(queries, 'kvh', split_axis=1, concat_axis=0, tiled=True)  3.13 us
  transfers between devices with their start and end apart: 13, of which 5 were waited for; matrix products, arithmetic and copies ran while one was open for 8% of the time, Pallas kernels for 0%

profile of v3, /device:TPU:0, one launch (start us, length us, event | category | flops | bytes accessed | tf_op | source)
XLA Modules:
  0.0 103.4 jit_solution(9647660916122711561)
XLA Ops:
  0.0 1.0 copy_bitcast_fusion.1
  1.0 0.7 pad_maximum_fusion.1
  1.7 4.2 %all-to-all-start.1 = ((bf16[64,4,512]{2,0,1:T(8,128)(2,1)}), bf16[64,4,512]{2,0,1:T(8,128)(2,1)S(1)}, u32[]{:S(2)}, u32[]{:S(2)}) async-start(bf16[64,4,512]{2,0,1:T(8,128)(2,1)} %pad_maximum_fusion.1), calls=%async_computation.1 | async-start | bytes 524288 | tf_op jit(solution)/shard_map/all_to_all | solution.py:87
  5.9 0.1 add_multiply_fusion
  6.0 0.1 add_bitcast_fusion
  6.1 0.8 reduce-window.8
  6.9 0.7 select_reduce_fusion
  7.7 0.1 slice.15
  7.8 3.1 %copy.26 = bf16[8,4,8,4096]{3,2,0,1:T(8,128)(2,1)} copy(bf16[8,4,8,4096]{3,2,1,0:T(8,128)(2,1)} %bitcast.45) | data formatting | bytes 4194304 | tf_op jit(solution)/shard_map/all_to_all | solution.py:81
  10.9 1.1 %all-to-all-done.1 = bf16[64,4,512]{2,0,1:T(8,128)(2,1)S(1)} async-done(((bf16[64,4,512]{2,0,1:T(8,128)(2,1)}), bf16[64,4,512]{2,0,1:T(8,128)(2,1)S(1)}, u32[]{:S(2)}, u32[]{:S(2)}) %all-to-all-start.1) | async-done | bytes 262176 | tf_op jit(solution)/shard_map/all_to_all | solution.py:87
  12.0 3.6 %all-to-all-start = ((bf16[64,4,4096]{2,0,1:T(8,128)(2,1)}), bf16[64,4,4096]{2,0,1:T(8,128)(2,1)S(1)}, u32[]{:S(2)}, u32[]{:S(2)}) async-start(bf16[64,4,4096]{2,0,1:T(8,128)(2,1)} %bitcast.30), calls=%async_computation | async-start | bytes 4194304 | tf_op jit(solution)/shard_map/all_to_all | solution.py:81
  15.6 1.3 %collective-permute-start.4 = (bf16[128,512]{1,0:T(8,128)(2,1)S(1)}, bf16[128,512]{1,0:T(8,128)(2,1)S(1)}, u32[]{:S(2)}, u32[]{:S(2)}) collective-permute-start(bf16[128,512]{1,0:T(8,128)(2,1)S(1)} %bitcast.49), channel_id=1, source_target_pairs={{16,0},{20,4},{24,8},{28,12},{17,1},{21,5},{25,9},{29,13},{18,2},{... | collective-permute-start | bytes 393224 | tf_op jit(solution)/shard_map/ppermute | solution.py:18
  16.9 0.7 collective-permute-start.5
  17.6 0.1 clamp_add_fusion
  17.7 0.8 copy.17.start_ref
  18.5 0.6 pad_add_fusion.blocks_ref
  19.1 9.8 %collective-permute-start = (bf16[128,512]{1,0:T(8,128)(2,1)S(1)}, bf16[128,512]{1,0:T(8,128)(2,1)S(1)}, u32[]{:S(2)}, u32[]{:S(2)}) collective-permute-start(bf16[128,512]{1,0:T(8,128)(2,1)S(1)} %bitcast.35), channel_id=1, source_target_pairs={{0,16},{4,20},{8,24},{12,28},{1,17},{5,21},{9,25},{13,29},{2,18},{... | collective-permute-start | bytes 393224 | tf_op jit(solution)/shard_map/ppermute | solution.py:18
  28.8 1.9 %collective-permute-start.1 = (bf16[128,512]{1,0:T(8,128)(2,1)S(1)}, bf16[128,512]{1,0:T(8,128)(2,1)S(1)}, u32[]{:S(2)}, u32[]{:S(2)}) collective-permute-start(bf16[128,512]{1,0:T(8,128)(2,1)S(1)} %bitcast.36), channel_id=1, source_target_pairs={{0,12},{4,16},{8,20},{12,24},{16,28},{1,13},{5,17},{9,21},{13,25},... | collective-permute-start | bytes 393224 | tf_op jit(solution)/shard_map/ppermute | solution.py:18
  30.8 1.8 %collective-permute-start.2 = (bf16[128,512]{1,0:T(8,128)(2,1)S(1)}, bf16[128,512]{1,0:T(8,128)(2,1)S(1)}, u32[]{:S(2)}, u32[]{:S(2)}) collective-permute-start(bf16[128,512]{1,0:T(8,128)(2,1)S(1)} %bitcast.37), channel_id=1, source_target_pairs={{0,8},{4,12},{8,16},{12,20},{16,24},{20,28},{1,9},{5,13},{9,17},{1... | collective-permute-start | bytes 393224 | tf_op jit(solution)/shard_map/ppermute | solution.py:18
  32.6 0.0 collective-permute-done.4
  32.6 1.3 %collective-permute-start.6 = (bf16[128,512]{1,0:T(8,128)(2,1)S(1)}, bf16[128,512]{1,0:T(8,128)(2,1)S(1)}, u32[]{:S(2)}, u32[]{:S(2)}) collective-permute-start(bf16[128,512]{1,0:T(8,128)(2,1)S(1)} %bitcast.50), channel_id=1, source_target_pairs={{12,0},{16,4},{20,8},{24,12},{28,16},{13,1},{17,5},{21,9},{25,13},... | collective-permute-start | bytes 393224 | tf_op jit(solution)/shard_map/ppermute | solution.py:18
  33.9 0.0 collective-permute-done.5
  33.9 0.7 collective-permute-start.7
  34.6 0.1 select_dynamic-update-slice_fusion.3
  34.7 5.7 %collective-permute-done.6 = bf16[128,512]{1,0:T(8,128)(2,1)S(1)} collective-permute-done((bf16[128,512]{1,0:T(8,128)(2,1)S(1)}, bf16[128,512]{1,0:T(8,128)(2,1)S(1)}, u32[]{:S(2)}, u32[]{:S(2)}) %collective-permute-start.6) | collective-permute-done | bytes 131104 | tf_op jit(solution)/shard_map/ppermute | solution.py:18
  40.4 1.3 %collective-permute-start.8 = (bf16[128,512]{1,0:T(8,128)(2,1)S(1)}, bf16[128,512]{1,0:T(8,128)(2,1)S(1)}, u32[]{:S(2)}, u32[]{:S(2)}) collective-permute-start(bf16[128,512]{1,0:T(8,128)(2,1)S(1)} %bitcast.51), channel_id=1, source_target_pairs={{8,0},{12,4},{16,8},{20,12},{24,16},{28,20},{9,1},{13,5},{17,9},{2... | collective-permute-start | bytes 393224 | tf_op jit(solution)/shard_map/ppermute | solution.py:18
  41.7 0.0 collective-permute-done.7
  41.7 0.7 collective-permute-start.9
  42.3 0.1 select_dynamic-update-slice_fusion.2
  42.4 4.8 %collective-permute-done.8 = bf16[128,512]{1,0:T(8,128)(2,1)S(1)} collective-permute-done((bf16[128,512]{1,0:T(8,128)(2,1)S(1)}, bf16[128,512]{1,0:T(8,128)(2,1)S(1)}, u32[]{:S(2)}, u32[]{:S(2)}) %collective-permute-start.8) | collective-permute-done | bytes 131104 | tf_op jit(solution)/shard_map/ppermute | solution.py:18
  47.2 6.9 %collective-permute-start.3 = (bf16[128,512]{1,0:T(8,128)(2,1)S(1)}, bf16[128,512]{1,0:T(8,128)(2,1)S(1)}, u32[]{:S(2)}, u32[]{:S(2)}) collective-permute-start(bf16[128,512]{1,0:T(8,128)(2,1)S(1)} %bitcast.42), channel_id=1, source_target_pairs={{0,4},{4,8},{8,12},{12,16},{16,20},{20,24},{24,28},{1,5},{5,9},{9,... | collective-permute-start | bytes 393224 | tf_op jit(solution)/shard_map/ppermute | solution.py:18
  54.2 0.0 collective-permute-done.9
  54.2 1.3 %collective-permute-start.10 = (bf16[128,512]{1,0:T(8,128)(2,1)S(1)}, bf16[128,512]{1,0:T(8,128)(2,1)S(1)}, u32[]{:S(2)}, u32[]{:S(2)}) collective-permute-start(bf16[128,512]{1,0:T(8,128)(2,1)S(1)} %bitcast.52), channel_id=1, source_target_pairs={{4,0},{8,4},{12,8},{16,12},{20,16},{24,20},{28,24},{5,1},{9,5},{13... | collective-permute-start | bytes 393224 | tf_op jit(solution)/shard_map/ppermute | solution.py:18
  55.5 0.1 select_dynamic-update-slice_fusion.1
  55.5 0.0 collective-permute-done
  55.6 0.0 collective-permute-done.1
  55.6 0.0 collective-permute-done.2
  55.6 2.4 %collective-permute-done.3 = bf16[128,512]{1,0:T(8,128)(2,1)S(1)} collective-permute-done((bf16[128,512]{1,0:T(8,128)(2,1)S(1)}, bf16[128,512]{1,0:T(8,128)(2,1)S(1)}, u32[]{:S(2)}, u32[]{:S(2)}) %collective-permute-start.3) | collective-permute-done | bytes 131104 | tf_op jit(solution)/shard_map/ppermute | solution.py:18
  58.1 3.0 %collective-permute-done.10 = bf16[128,512]{1,0:T(8,128)(2,1)S(1)} collective-permute-done((bf16[128,512]{1,0:T(8,128)(2,1)S(1)}, bf16[128,512]{1,0:T(8,128)(2,1)S(1)}, u32[]{:S(2)}, u32[]{:S(2)}) %collective-permute-start.10) | collective-permute-done | bytes 131104 | tf_op jit(solution)/shard_map/ppermute | solution.py:18
  61.1 1.2 %pad_maximum_fusion.k_ref.v_ref = bf16[2,640,512]{2,1,0:T(8,128)(2,1)} fusion(bf16[1,640,512]{2,1,0:T(8,128)(2,1)S(1)} %bitcast.48, bf16[1,640,512]{2,1,0:T(8,128)(2,1)S(1)} %bitcast.47), kind=kLoop, calls=%fused_computation.1 | loop fusion | flops 655360 | bytes 2621440 | tf_op jit(solution)/shard_map/stack | solution.py:117
  62.3 0.0 all-to-all-done
  62.3 0.0 copy-start
  62.3 1.3 %copy-done = bf16[64,4,4096]{2,0,1:T(8,128)(2,1)} copy-done((bf16[64,4,4096]{2,0,1:T(8,128)(2,1)}, bf16[64,4,4096]{2,0,1:T(8,128)(2,1)S(1)}, u32[]{:S(2)}) %copy-start) | copy-done | bytes 2097176
  63.6 8.9 %shard_map.46 = bf16[256,4096]{1,0:T(8,128)(2,1)} custom-call(s32[4]{0:T(128)} %pad_add_fusion.blocks_ref, bf16[256,4096]{1,0:T(8,128)(2,1)} %bitcast.31, s32[2,128,1]{2,1,0:T(8,128)} %copy.17.start_ref, bf16[2,640,512]{2,1,0:T(8,128)(2,1)} %pad_maximum_fusion.k_ref.v_ref, bf16[2,640,512]{2,1,0:T(8,128)(2,1)} %pad_maximum_fusion.k_ref.v_ref), custom_call_target="tpu_custom_call" | custom-call | tf_op jit(solution)/shard_map/pallas_call | solution.py:137
  72.5 29.3 %all_to_all.53 = bf16[4,64,4096]{2,1,0:T(8,128)(2,1)S(1)} all-to-all(bf16[4,64,4096]{2,1,0:T(8,128)(2,1)} %bitcast.32), channel_id=1, replica_groups=mesh['seq'=8,'kvh'=4] {'kvh'}, dimensions={0} | all-to-all | bytes 4194304 | tf_op jit(solution)/shard_map/all_to_all | solution.py:156
  101.8 1.5 %copy.22 = bf16[4,8,8,4096]{3,2,0,1:T(8,128)(2,1)} copy(bf16[4,8,8,4096]{3,2,1,0:T(8,128)(2,1)S(1)} %bitcast.33) | data formatting | bytes 4194304 | tf_op jit(solution)/shard_map/all_to_all | solution.py:156
  (7 shorter events, 0.1 us)
Async XLA Ops:
  1.7 10.3 %all-to-all-start.1 = ((bf16[64,4,512]{2,0,1:T(8,128)(2,1)}), bf16[64,4,512]{2,0,1:T(8,128)(2,1)S(1)}, u32[]{:S(2)}, u32[]{:S(2)}) async-start(bf16[64,4,512]{2,0,1:T(8,128)(2,1)} %pad_maximum_fusion.1), calls=%async_computation.1 | async-start | bytes 524288 | tf_op jit(solution)/shard_map/all_to_all | solution.py:87
  12.0 50.3 %all-to-all-start = ((bf16[64,4,4096]{2,0,1:T(8,128)(2,1)}), bf16[64,4,4096]{2,0,1:T(8,128)(2,1)S(1)}, u32[]{:S(2)}, u32[]{:S(2)}) async-start(bf16[64,4,4096]{2,0,1:T(8,128)(2,1)} %bitcast.30), calls=%async_computation | async-start | bytes 4194304 | tf_op jit(solution)/shard_map/all_to_all | solution.py:81
  15.6 17.0 %collective-permute-start.4 = (bf16[128,512]{1,0:T(8,128)(2,1)S(1)}, bf16[128,512]{1,0:T(8,128)(2,1)S(1)}, u32[]{:S(2)}, u32[]{:S(2)}) collective-permute-start(bf16[128,512]{1,0:T(8,128)(2,1)S(1)} %bitcast.49), channel_id=1, source_target_pairs={{16,0},{20,4},{24,8},{28,12},{17,1},{21,5},{25,9},{29,13},{18,2},{... | collective-permute-start | bytes 393224 | tf_op jit(solution)/shard_map/ppermute | solution.py:18
  16.9 17.0 %collective-permute-start.5 = (bf16[128,512]{1,0:T(8,128)(2,1)S(1)}, bf16[128,512]{1,0:T(8,128)(2,1)S(1)}, u32[]{:S(2)}, u32[]{:S(2)}) collective-permute-start(bf16[128,512]{1,0:T(8,128)(2,1)S(1)} %bitcast.34), channel_id=1, source_target_pairs={{16,28},{20,24},{24,20},{28,16},{17,29},{21,25},{25,21},{29,17},{1... | collective-permute-start | bytes 393224 | tf_op jit(solution)/shard_map/ppermute | solution.py:110
  19.1 36.5 %collective-permute-start = (bf16[128,512]{1,0:T(8,128)(2,1)S(1)}, bf16[128,512]{1,0:T(8,128)(2,1)S(1)}, u32[]{:S(2)}, u32[]{:S(2)}) collective-permute-start(bf16[128,512]{1,0:T(8,128)(2,1)S(1)} %bitcast.35), channel_id=1, source_target_pairs={{0,16},{4,20},{8,24},{12,28},{1,17},{5,21},{9,25},{13,29},{2,18},{... | collective-permute-start | bytes 393224 | tf_op jit(solution)/shard_map/ppermute | solution.py:18
  28.8 26.7 %collective-permute-start.1 = (bf16[128,512]{1,0:T(8,128)(2,1)S(1)}, bf16[128,512]{1,0:T(8,128)(2,1)S(1)}, u32[]{:S(2)}, u32[]{:S(2)}) collective-permute-start(bf16[128,512]{1,0:T(8,128)(2,1)S(1)} %bitcast.36), channel_id=1, source_target_pairs={{0,12},{4,16},{8,20},{12,24},{16,28},{1,13},{5,17},{9,21},{13,25},... | collective-permute-start | bytes 393224 | tf_op jit(solution)/shard_map/ppermute | solution.py:18
  30.8 24.8 %collective-permute-start.2 = (bf16[128,512]{1,0:T(8,128)(2,1)S(1)}, bf16[128,512]{1,0:T(8,128)(2,1)S(1)}, u32[]{:S(2)}, u32[]{:S(2)}) collective-permute-start(bf16[128,512]{1,0:T(8,128)(2,1)S(1)} %bitcast.37), channel_id=1, source_target_pairs={{0,8},{4,12},{8,16},{12,20},{16,24},{20,28},{1,9},{5,13},{9,17},{1... | collective-permute-start | bytes 393224 | tf_op jit(solution)/shard_map/ppermute | solution.py:18
  32.6 7.8 %collective-permute-start.6 = (bf16[128,512]{1,0:T(8,128)(2,1)S(1)}, bf16[128,512]{1,0:T(8,128)(2,1)S(1)}, u32[]{:S(2)}, u32[]{:S(2)}) collective-permute-start(bf16[128,512]{1,0:T(8,128)(2,1)S(1)} %bitcast.50), channel_id=1, source_target_pairs={{12,0},{16,4},{20,8},{24,12},{28,16},{13,1},{17,5},{21,9},{25,13},... | collective-permute-start | bytes 393224 | tf_op jit(solution)/shard_map/ppermute | solution.py:18
  33.9 7.7 %collective-permute-start.7 = (bf16[128,512]{1,0:T(8,128)(2,1)S(1)}, bf16[128,512]{1,0:T(8,128)(2,1)S(1)}, u32[]{:S(2)}, u32[]{:S(2)}) collective-permute-start(bf16[128,512]{1,0:T(8,128)(2,1)S(1)} %bitcast.38), channel_id=1, source_target_pairs={{20,28},{28,20},{21,29},{29,21},{22,30},{30,22},{23,31},{31,23}} | collective-permute-start | bytes 393224 | tf_op jit(solution)/shard_map/ppermute | solution.py:110
  40.4 6.8 %collective-permute-start.8 = (bf16[128,512]{1,0:T(8,128)(2,1)S(1)}, bf16[128,512]{1,0:T(8,128)(2,1)S(1)}, u32[]{:S(2)}, u32[]{:S(2)}) collective-permute-start(bf16[128,512]{1,0:T(8,128)(2,1)S(1)} %bitcast.51), channel_id=1, source_target_pairs={{8,0},{12,4},{16,8},{20,12},{24,16},{28,20},{9,1},{13,5},{17,9},{2... | collective-permute-start | bytes 393224 | tf_op jit(solution)/shard_map/ppermute | solution.py:18
  41.7 12.5 %collective-permute-start.9 = (bf16[128,512]{1,0:T(8,128)(2,1)S(1)}, bf16[128,512]{1,0:T(8,128)(2,1)S(1)}, u32[]{:S(2)}, u32[]{:S(2)}) collective-permute-start(bf16[128,512]{1,0:T(8,128)(2,1)S(1)} %bitcast.40), channel_id=1, source_target_pairs={{24,28},{28,24},{25,29},{29,25},{26,30},{30,26},{27,31},{31,27}} | collective-permute-start | bytes 393224 | tf_op jit(solution)/shard_map/ppermute | solution.py:110
  47.2 10.8 %collective-permute-start.3 = (bf16[128,512]{1,0:T(8,128)(2,1)S(1)}, bf16[128,512]{1,0:T(8,128)(2,1)S(1)}, u32[]{:S(2)}, u32[]{:S(2)}) collective-permute-start(bf16[128,512]{1,0:T(8,128)(2,1)S(1)} %bitcast.42), channel_id=1, source_target_pairs={{0,4},{4,8},{8,12},{12,16},{16,20},{20,24},{24,28},{1,5},{5,9},{9,... | collective-permute-start | bytes 393224 | tf_op jit(solution)/shard_map/ppermute | solution.py:18
  54.2 6.9 %collective-permute-start.10 = (bf16[128,512]{1,0:T(8,128)(2,1)S(1)}, bf16[128,512]{1,0:T(8,128)(2,1)S(1)}, u32[]{:S(2)}, u32[]{:S(2)}) collective-permute-start(bf16[128,512]{1,0:T(8,128)(2,1)S(1)} %bitcast.52), channel_id=1, source_target_pairs={{4,0},{8,4},{12,8},{16,12},{20,16},{24,20},{28,24},{5,1},{9,5},{13... | collective-permute-start | bytes 393224 | tf_op jit(solution)/shard_map/ppermute | solution.py:18
  62.3 1.3 %copy-start = (bf16[64,4,4096]{2,0,1:T(8,128)(2,1)}, bf16[64,4,4096]{2,0,1:T(8,128)(2,1)S(1)}, u32[]{:S(2)}) copy-start(bf16[64,4,4096]{2,0,1:T(8,128)(2,1)S(1)} %all-to-all-done) | copy-start | bytes 6291460

commit v4 on v3

--- a/solution.py
+++ b/solution.py
@@ -25,16 +25,12 @@
 
 
 def attend_kernel(
-    blocks_ref, q_ref, start_ref, k_ref, v_ref, out_ref, kt_buf, v_buf,
+    blocks_ref, q_ref, start_ref, kt_buf, v_buf, out_ref,
     *, half_rows, group_size, pad_rows, window
 ):
     side = pl.program_id(0)
     block_id = blocks_ref[side]
     needed = blocks_ref[2 + side]
-    kt_buf[...] = k_ref[...].T
-    v_buf[:, :DH] = v_ref[...]
-    lane = lax.broadcasted_iota(jnp.int32, (window, DH), 1)
-    v_buf[:, DH:] = jnp.where(lane == 0, 1.0, 0.0).astype(v_buf.dtype)
     scale = 1.0 / math.sqrt(DH)
     row_start = start_ref[...]
 
@@ -118,6 +114,10 @@
         [jnp.concatenate(low_side[::-1], axis=0), jnp.concatenate(high_side[::-1], axis=0)]
     )
 
+    keys_t = windows[:, :, :kv_feat].transpose(0, 2, 1)
+    values = windows[:, :, kv_feat:].reshape(2, window, kv_heads, DH)
+    ones = jnp.zeros_like(values).at[..., 0].set(1)
+    values_ext = jnp.concatenate([values, ones], axis=3).reshape(2, window, kv_heads * 2 * DH)
     doc_ends = jnp.cumsum(doc_lengths)
     block_ids = jnp.stack([my_shard, 2 * shards - 1 - my_shard]).astype(jnp.int32)
     positions = block_ids[:, None] * half_rows + jnp.arange(half_rows, dtype=jnp.int32)[None, :]
@@ -143,16 +143,12 @@
             in_specs=[
                 pl.BlockSpec((half_rows, q_cols), lambda s, h, b: (s, h)),
                 pl.BlockSpec((None, half_rows, 1), lambda s, h, b: (s, 0, 0)),
-                pl.BlockSpec((None, window, DH), lambda s, h, b: (s, 0, h)),
-                pl.BlockSpec((None, window, DH), lambda s, h, b, n=kv_heads: (s, 0, n + h)),
+                pl.BlockSpec((None, DH, window), lambda s, h, b: (s, h, 0)),
+                pl.BlockSpec((None, window, 2 * DH), lambda s, h, b: (s, 0, h)),
             ],
             out_specs=pl.BlockSpec((half_rows, q_cols), lambda s, h, b: (s, h)),
-            scratch_shapes=[
-                pltpu.VMEM((DH, window), kv_slab.dtype),
-                pltpu.VMEM((window, 2 * DH), kv_slab.dtype),
-            ],
         ),
-    )(block_ids, head_queries, starts, windows, windows)
+    )(block_ids, head_queries, starts, keys_t, values_ext)
     return lax.all_to_all(merged, "kvh", split_axis=0, concat_axis=1, tiled=True)
 
 

time: 105 us -> 108 us (1.029)
  the two profiles are of different devices: /device:TPU:0 before, /device:TPU:24 now
where the time goes in v4:
time: 108 us
  starting transfers between devices  35 us (32%)
  blocking collectives  29.3 us (27%)
  waiting for transfers between devices  14.1 us (13%)
  local copies, waits for them, and re-layouts  12 us (11%)
  Pallas kernels  11.8 us (11%)
  other arithmetic  5.21 us (5%)
    all_to_all x1, blocking collectives, on_device(): lax.all_to_all(merged, 'kvh', split_axis=0, concat_axis=1, tiled=True)  29.3 us
    ppermute x8, starting transfers between devices, shifted(): return lax.ppermute(block, axis, route)  17.4 us
    pallas_call x1, Pallas kernels, on_device(): pl.pallas_call(kernel, out_shape=jax.ShapeDtypeStruct(head_queries.shape,...  11.8 us
    ppermute x3, starting transfers between devices, on_device(): from_mirror = lax.ppermute(first_half, 'seq', mirror) if mirror else blank  10.6 us
    ppermute x8, waiting for transfers between devices, shifted(): return lax.ppermute(block, axis, route)  10.1 us
    all_to_all x1, waiting for transfers between devices, on_device(): lax.all_to_all(kv_local, 'kvh', split_axis=1, concat_axis=0, tiled=True)  3.93 us
    all_to_all x1, starting transfers between devices, on_device(): lax.all_to_all(queries, 'kvh', split_axis=1, concat_axis=0, tiled=True)  3.61 us
    all_to_all x1, starting transfers between devices, on_device(): lax.all_to_all(kv_local, 'kvh', split_axis=1, concat_axis=0, tiled=True)  3.4 us
  transfers between devices with their start and end apart: 13, of which 4 were waited for; matrix products, arithmetic and copies ran while one was open for 11% of the time, Pallas kernels for 0%

profile of v4, /device:TPU:24, one launch (start us, length us, event | category | flops | bytes accessed | tf_op | source)
XLA Modules:
  0.0 107.6 jit_solution(1234080126119246670)
XLA Ops:
  0.0 0.0 copy-start.2
  0.0 0.0 copy-start.1
  0.0 1.1 %reshape.119 = bf16[64,4,256]{2,1,0:T(4,128)(2,1)S(1)} reshape(bf16[64,1024]{1,0:T(8,128)(2,1)} %param.8) | data formatting | bytes 262144 | tf_op jit(solution)/shard_map/reshape | solution.py:80
  1.1 1.0 reshape.118
  2.1 0.1 pad_maximum_fusion.2
  2.2 0.7 copy.77
  3.0 3.4 %all-to-all-start.1 = ((bf16[64,4,512]{2,0,1:T(8,128)(2,1)}), bf16[64,4,512]{2,0,1:T(8,128)(2,1)S(1)}, u32[]{:S(2)}, u32[]{:S(2)}) async-start(bf16[64,4,512]{2,0,1:T(8,128)(2,1)} %copy.77), calls=%async_computation.1 | async-start | bytes 524288 | tf_op jit(solution)/shard_map/all_to_all | solution.py:83
  6.4 0.1 add_multiply_fusion
  6.5 0.1 add_bitcast_fusion
  6.6 0.0 copy-done.2
  6.6 0.2 reduce-window.8
  6.7 0.1 select_reduce_fusion
  6.8 0.1 slice.45
  6.9 0.0 copy-done.1
  6.9 1.5 %copy.101 = bf16[8,4,8,4096]{3,2,0,1:T(8,128)(2,1)} copy(bf16[8,4,8,4096]{3,2,1,0:T(8,128)(2,1)S(1)} %bitcast.33) | data formatting | bytes 4194304 | tf_op jit(solution)/shard_map/all_to_all | solution.py:77
  8.5 3.9 %all-to-all-done.1 = bf16[64,4,512]{2,0,1:T(8,128)(2,1)S(1)} async-done(((bf16[64,4,512]{2,0,1:T(8,128)(2,1)}), bf16[64,4,512]{2,0,1:T(8,128)(2,1)S(1)}, u32[]{:S(2)}, u32[]{:S(2)}) %all-to-all-start.1) | async-done | bytes 262176 | tf_op jit(solution)/shard_map/all_to_all | solution.py:83
  12.4 3.6 %all-to-all-start = ((bf16[64,4,4096]{2,0,1:T(8,128)(2,1)}), bf16[64,4,4096]{2,0,1:T(8,128)(2,1)S(1)}, u32[]{:S(2)}, u32[]{:S(2)}) async-start(bf16[64,4,4096]{2,0,1:T(8,128)(2,1)} %bitcast.30), calls=%async_computation | async-start | bytes 4194304 | tf_op jit(solution)/shard_map/all_to_all | solution.py:77
  16.1 0.1 copy.83
  16.2 2.2 %collective-permute-start.4 = (bf16[128,512]{0,1:T(8,128)(2,1)S(1)}, bf16[128,512]{0,1:T(8,128)(2,1)S(1)}, u32[]{:S(2)}, u32[]{:S(2)}) collective-permute-start(bf16[128,512]{0,1:T(8,128)(2,1)S(1)} %copy.83), channel_id=1, source_target_pairs={{16,0},{20,4},{24,8},{28,12},{17,1},{21,5},{25,9},{29,13},{18,2},{... | collective-permute-start | bytes 393224 | tf_op jit(solution)/shard_map/ppermute | solution.py:18
  18.4 0.1 copy.78
  18.6 3.3 %collective-permute-start.5 = (bf16[128,512]{0,1:T(8,128)(2,1)S(1)}, bf16[128,512]{0,1:T(8,128)(2,1)S(1)}, u32[]{:S(2)}, u32[]{:S(2)}) collective-permute-start(bf16[128,512]{0,1:T(8,128)(2,1)S(1)} %copy.78), channel_id=1, source_target_pairs={{16,28},{20,24},{24,20},{28,16},{17,29},{21,25},{25,21},{29,17},{1... | collective-permute-start | bytes 393224 | tf_op jit(solution)/shard_map/ppermute | solution.py:106
  21.9 0.1 clamp_add_fusion
  22.0 0.8 copy.96.start_ref
  22.7 0.6 pad_add_fusion.blocks_ref
  23.3 1.3 %collective-permute-start.6 = (bf16[128,512]{0,1:T(8,128)(2,1)S(1)}, bf16[128,512]{0,1:T(8,128)(2,1)S(1)}, u32[]{:S(2)}, u32[]{:S(2)}) collective-permute-start(bf16[128,512]{0,1:T(8,128)(2,1)S(1)} %copy.83), channel_id=1, source_target_pairs={{12,0},{16,4},{20,8},{24,12},{28,16},{13,1},{17,5},{21,9},{25,13},... | collective-permute-start | bytes 393224 | tf_op jit(solution)/shard_map/ppermute | solution.py:18
  24.6 0.7 collective-permute-start.7
  25.3 4.1 %collective-permute-start.8 = (bf16[128,512]{0,1:T(8,128)(2,1)S(1)}, bf16[128,512]{0,1:T(8,128)(2,1)S(1)}, u32[]{:S(2)}, u32[]{:S(2)}) collective-permute-start(bf16[128,512]{0,1:T(8,128)(2,1)S(1)} %copy.83), channel_id=1, source_target_pairs={{8,0},{12,4},{16,8},{20,12},{24,16},{28,20},{9,1},{13,5},{17,9},{2... | collective-permute-start | bytes 393224 | tf_op jit(solution)/shard_map/ppermute | solution.py:18
  29.4 0.0 collective-permute-done.4
  29.4 6.6 %collective-permute-start.9 = (bf16[128,512]{0,1:T(8,128)(2,1)S(1)}, bf16[128,512]{0,1:T(8,128)(2,1)S(1)}, u32[]{:S(2)}, u32[]{:S(2)}) collective-permute-start(bf16[128,512]{0,1:T(8,128)(2,1)S(1)} %copy.78), channel_id=1, source_target_pairs={{24,28},{28,24},{25,29},{29,25},{26,30},{30,26},{27,31},{31,27}} | collective-permute-start | bytes 393224 | tf_op jit(solution)/shard_map/ppermute | solution.py:106
  36.1 0.0 collective-permute-done.5
  36.1 1.9 %collective-permute-start.10 = (bf16[128,512]{0,1:T(8,128)(2,1)S(1)}, bf16[128,512]{0,1:T(8,128)(2,1)S(1)}, u32[]{:S(2)}, u32[]{:S(2)}) collective-permute-start(bf16[128,512]{0,1:T(8,128)(2,1)S(1)} %copy.83), channel_id=1, source_target_pairs={{4,0},{8,4},{12,8},{16,12},{20,16},{24,20},{28,24},{5,1},{9,5},{13... | collective-permute-start | bytes 393224 | tf_op jit(solution)/shard_map/ppermute | solution.py:18
  38.0 0.1 select_dynamic-update-slice_fusion.3
  38.1 0.0 collective-permute-done.6
  38.1 1.3 %collective-permute-start = (bf16[128,512]{0,1:T(8,128)(2,1)S(1)}, bf16[128,512]{0,1:T(8,128)(2,1)S(1)}, u32[]{:S(2)}, u32[]{:S(2)}) collective-permute-start(bf16[128,512]{0,1:T(8,128)(2,1)S(1)} %copy.78), channel_id=1, source_target_pairs={{0,16},{4,20},{8,24},{12,28},{1,17},{5,21},{9,25},{13,29},{2,18},{... | collective-permute-start | bytes 393224 | tf_op jit(solution)/shard_map/ppermute | solution.py:18
  39.4 0.0 collective-permute-done.7
  39.4 1.3 %collective-permute-start.1 = (bf16[128,512]{0,1:T(8,128)(2,1)S(1)}, bf16[128,512]{0,1:T(8,128)(2,1)S(1)}, u32[]{:S(2)}, u32[]{:S(2)}) collective-permute-start(bf16[128,512]{0,1:T(8,128)(2,1)S(1)} %copy.78), channel_id=1, source_target_pairs={{0,12},{4,16},{8,20},{12,24},{16,28},{1,13},{5,17},{9,21},{13,25},... | collective-permute-start | bytes 393224 | tf_op jit(solution)/shard_map/ppermute | solution.py:18
  40.7 0.1 select_dynamic-update-slice_fusion.2
  40.8 0.0 collective-permute-done.8
  40.8 1.3 %collective-permute-start.2 = (bf16[128,512]{0,1:T(8,128)(2,1)S(1)}, bf16[128,512]{0,1:T(8,128)(2,1)S(1)}, u32[]{:S(2)}, u32[]{:S(2)}) collective-permute-start(bf16[128,512]{0,1:T(8,128)(2,1)S(1)} %copy.78), channel_id=1, source_target_pairs={{0,8},{4,12},{8,16},{12,20},{16,24},{20,28},{1,9},{5,13},{9,17},{1... | collective-permute-start | bytes 393224 | tf_op jit(solution)/shard_map/ppermute | solution.py:18
  42.1 0.0 collective-permute-done.9
  42.1 3.9 %collective-permute-start.3 = (bf16[128,512]{0,1:T(8,128)(2,1)S(1)}, bf16[128,512]{0,1:T(8,128)(2,1)S(1)}, u32[]{:S(2)}, u32[]{:S(2)}) collective-permute-start(bf16[128,512]{0,1:T(8,128)(2,1)S(1)} %copy.78), channel_id=1, source_target_pairs={{0,4},{4,8},{8,12},{12,16},{16,20},{20,24},{24,28},{1,5},{5,9},{9,... | collective-permute-start | bytes 393224 | tf_op jit(solution)/shard_map/ppermute | solution.py:18
  46.0 0.1 select_dynamic-update-slice_fusion.1
  46.1 0.5 collective-permute-done
  46.6 5.2 %collective-permute-done.1 = bf16[128,512]{0,1:T(8,128)(2,1)S(1)} collective-permute-done((bf16[128,512]{0,1:T(8,128)(2,1)S(1)}, bf16[128,512]{0,1:T(8,128)(2,1)S(1)}, u32[]{:S(2)}, u32[]{:S(2)}) %collective-permute-start.1) | collective-permute-done | bytes 131104 | tf_op jit(solution)/shard_map/ppermute | solution.py:18
  51.9 0.0 collective-permute-done.2
  51.9 4.4 %collective-permute-done.3 = bf16[128,512]{0,1:T(8,128)(2,1)S(1)} collective-permute-done((bf16[128,512]{0,1:T(8,128)(2,1)S(1)}, bf16[128,512]{0,1:T(8,128)(2,1)S(1)}, u32[]{:S(2)}, u32[]{:S(2)}) %collective-permute-start.3) | collective-permute-done | bytes 131104 | tf_op jit(solution)/shard_map/ppermute | solution.py:18
  56.4 0.0 collective-permute-done.10
  56.4 0.1 select_dynamic-update-slice_fusion
  56.6 0.9 pad_maximum_fusion.1
  57.5 1.8 %copy.95 = bf16[2,640,2,128]{3,2,1,0:T(2,128)(2,1)} copy(bf16[2,640,2,128]{1,3,2,0:T(8,128)(2,1)S(1)} %bitcast.32) | data formatting | bytes 1310720 | tf_op jit(solution)/shard_map/reshape | solution.py:118
  59.3 2.7 %pad_maximum_fusion = bf16[2,640,2,256]{3,2,1,0:T(2,128)(2,1)S(1)} fusion(bf16[2,640,2,128]{3,2,1,0:T(2,128)(2,1)} %constant.84.clone.1, bf16[2,640,2,128]{3,2,1,0:T(2,128)(2,1)} %copy.95), kind=kLoop, calls=%fused_computation.3 | loop fusion | flops 2621440 | bytes 2621440 | tf_op jit(solution)/shard_map/concatenate | solution.py:120
  62.0 1.7 %reshape.121.v_buf = bf16[2,640,512]{2,1,0:T(8,128)(2,1)} reshape(bf16[2,640,2,256]{3,2,1,0:T(2,128)(2,1)S(1)} %pad_maximum_fusion) | data formatting | bytes 2621440 | tf_op jit(solution)/shard_map/reshape | solution.py:120
  63.7 0.0 all-to-all-done
  63.7 0.0 copy-start
  63.7 1.3 %copy-done = bf16[64,4,4096]{2,0,1:T(8,128)(2,1)} copy-done((bf16[64,4,4096]{2,0,1:T(8,128)(2,1)}, bf16[64,4,4096]{2,0,1:T(8,128)(2,1)S(1)}, u32[]{:S(2)}) %copy-start) | copy-done | bytes 2097176
  65.0 11.8 %shard_map.46 = bf16[256,4096]{1,0:T(8,128)(2,1)} custom-call(s32[4]{0:T(128)} %pad_add_fusion.blocks_ref, bf16[256,4096]{1,0:T(8,128)(2,1)} %bitcast.28, s32[2,128,1]{2,1,0:T(8,128)} %copy.96.start_ref, bf16[2,256,640]{2,1,0:T(8,128)(2,1)} %get-tuple-element.18.kt_buf, bf16[2,640,512]{2,1,0:T(8,128)(2,1)} %reshape.121.v_buf), custom_call_target="tpu_custom_call" | custom-call | tf_op jit(solution)/shard_map/pallas_call | solution.py:137
  76.8 29.3 %all_to_all.53 = bf16[4,64,4096]{2,1,0:T(8,128)(2,1)S(1)} all-to-all(bf16[4,64,4096]{2,1,0:T(8,128)(2,1)} %bitcast.29), channel_id=1, replica_groups=mesh['seq'=8,'kvh'=4] {'kvh'}, dimensions={0} | all-to-all | bytes 4194304 | tf_op jit(solution)/shard_map/all_to_all | solution.py:152
  106.1 1.5 %copy.99 = bf16[4,8,8,4096]{3,2,0,1:T(8,128)(2,1)} copy(bf16[4,8,8,4096]{3,2,1,0:T(8,128)(2,1)S(1)} %bitcast.31) | data formatting | bytes 4194304 | tf_op jit(solution)/shard_map/all_to_all | solution.py:152
  (6 shorter events, 0.2 us)
Async XLA Ops:
  0.0 6.6 %copy-start.2 = (s32[8]{0:T(128)S(1)}, s32[8]{0:T(128)}, u32[]{:S(2)}) copy-start(s32[8]{0:T(128)} %param.9) | copy-start | bytes 100
  0.0 6.9 %copy-start.1 = (bf16[64,16384]{1,0:T(8,128)(2,1)S(1)}, bf16[64,16384]{1,0:T(8,128)(2,1)}, u32[]{:S(2)}) copy-start(bf16[64,16384]{1,0:T(8,128)(2,1)} %param.6) | copy-start | bytes 6291460
  3.0 9.4 %all-to-all-start.1 = ((bf16[64,4,512]{2,0,1:T(8,128)(2,1)}), bf16[64,4,512]{2,0,1:T(8,128)(2,1)S(1)}, u32[]{:S(2)}, u32[]{:S(2)}) async-start(bf16[64,4,512]{2,0,1:T(8,128)(2,1)} %copy.77), calls=%async_computation.1 | async-start | bytes 524288 | tf_op jit(solution)/shard_map/all_to_all | solution.py:83
  12.4 51.3 %all-to-all-start = ((bf16[64,4,4096]{2,0,1:T(8,128)(2,1)}), bf16[64,4,4096]{2,0,1:T(8,128)(2,1)S(1)}, u32[]{:S(2)}, u32[]{:S(2)}) async-start(bf16[64,4,4096]{2,0,1:T(8,128)(2,1)} %bitcast.30), calls=%async_computation | async-start | bytes 4194304 | tf_op jit(solution)/shard_map/all_to_all | solution.py:77
  16.2 13.3 %collective-permute-start.4 = (bf16[128,512]{0,1:T(8,128)(2,1)S(1)}, bf16[128,512]{0,1:T(8,128)(2,1)S(1)}, u32[]{:S(2)}, u32[]{:S(2)}) collective-permute-start(bf16[128,512]{0,1:T(8,128)(2,1)S(1)} %copy.83), channel_id=1, source_target_pairs={{16,0},{20,4},{24,8},{28,12},{17,1},{21,5},{25,9},{29,13},{18,2},{... | collective-permute-start | bytes 393224 | tf_op jit(solution)/shard_map/ppermute | solution.py:18
  18.6 17.5 %collective-permute-start.5 = (bf16[128,512]{0,1:T(8,128)(2,1)S(1)}, bf16[128,512]{0,1:T(8,128)(2,1)S(1)}, u32[]{:S(2)}, u32[]{:S(2)}) collective-permute-start(bf16[128,512]{0,1:T(8,128)(2,1)S(1)} %copy.78), channel_id=1, source_target_pairs={{16,28},{20,24},{24,20},{28,16},{17,29},{21,25},{25,21},{29,17},{1... | collective-permute-start | bytes 393224 | tf_op jit(solution)/shard_map/ppermute | solution.py:106
  23.3 14.7 %collective-permute-start.6 = (bf16[128,512]{0,1:T(8,128)(2,1)S(1)}, bf16[128,512]{0,1:T(8,128)(2,1)S(1)}, u32[]{:S(2)}, u32[]{:S(2)}) collective-permute-start(bf16[128,512]{0,1:T(8,128)(2,1)S(1)} %copy.83), channel_id=1, source_target_pairs={{12,0},{16,4},{20,8},{24,12},{28,16},{13,1},{17,5},{21,9},{25,13},... | collective-permute-start | bytes 393224 | tf_op jit(solution)/shard_map/ppermute | solution.py:18
  24.6 14.8 %collective-permute-start.7 = (bf16[128,512]{0,1:T(8,128)(2,1)S(1)}, bf16[128,512]{0,1:T(8,128)(2,1)S(1)}, u32[]{:S(2)}, u32[]{:S(2)}) collective-permute-start(bf16[128,512]{0,1:T(8,128)(2,1)S(1)} %copy.78), channel_id=1, source_target_pairs={{20,28},{28,20},{21,29},{29,21},{22,30},{30,22},{23,31},{31,23}} | collective-permute-start | bytes 393224 | tf_op jit(solution)/shard_map/ppermute | solution.py:106
  25.3 15.5 %collective-permute-start.8 = (bf16[128,512]{0,1:T(8,128)(2,1)S(1)}, bf16[128,512]{0,1:T(8,128)(2,1)S(1)}, u32[]{:S(2)}, u32[]{:S(2)}) collective-permute-start(bf16[128,512]{0,1:T(8,128)(2,1)S(1)} %copy.83), channel_id=1, source_target_pairs={{8,0},{12,4},{16,8},{20,12},{24,16},{28,20},{9,1},{13,5},{17,9},{2... | collective-permute-start | bytes 393224 | tf_op jit(solution)/shard_map/ppermute | solution.py:18
  29.4 12.7 %collective-permute-start.9 = (bf16[128,512]{0,1:T(8,128)(2,1)S(1)}, bf16[128,512]{0,1:T(8,128)(2,1)S(1)}, u32[]{:S(2)}, u32[]{:S(2)}) collective-permute-start(bf16[128,512]{0,1:T(8,128)(2,1)S(1)} %copy.78), channel_id=1, source_target_pairs={{24,28},{28,24},{25,29},{29,25},{26,30},{30,26},{27,31},{31,27}} | collective-permute-start | bytes 393224 | tf_op jit(solution)/shard_map/ppermute | solution.py:106
  36.1 20.3 %collective-permute-start.10 = (bf16[128,512]{0,1:T(8,128)(2,1)S(1)}, bf16[128,512]{0,1:T(8,128)(2,1)S(1)}, u32[]{:S(2)}, u32[]{:S(2)}) collective-permute-start(bf16[128,512]{0,1:T(8,128)(2,1)S(1)} %copy.83), channel_id=1, source_target_pairs={{4,0},{8,4},{12,8},{16,12},{20,16},{24,20},{28,24},{5,1},{9,5},{13... | collective-permute-start | bytes 393224 | tf_op jit(solution)/shard_map/ppermute | solution.py:18
  38.1 8.5 %collective-permute-start = (bf16[128,512]{0,1:T(8,128)(2,1)S(1)}, bf16[128,512]{0,1:T(8,128)(2,1)S(1)}, u32[]{:S(2)}, u32[]{:S(2)}) collective-permute-start(bf16[128,512]{0,1:T(8,128)(2,1)S(1)} %copy.78), channel_id=1, source_target_pairs={{0,16},{4,20},{8,24},{12,28},{1,17},{5,21},{9,25},{13,29},{2,18},{... | collective-permute-start | bytes 393224 | tf_op jit(solution)/shard_map/ppermute | solution.py:18
  39.4 12.4 %collective-permute-start.1 = (bf16[128,512]{0,1:T(8,128)(2,1)S(1)}, bf16[128,512]{0,1:T(8,128)(2,1)S(1)}, u32[]{:S(2)}, u32[]{:S(2)}) collective-permute-start(bf16[128,512]{0,1:T(8,128)(2,1)S(1)} %copy.78), channel_id=1, source_target_pairs={{0,12},{4,16},{8,20},{12,24},{16,28},{1,13},{5,17},{9,21},{13,25},... | collective-permute-start | bytes 393224 | tf_op jit(solution)/shard_map/ppermute | solution.py:18
  40.8 11.1 %collective-permute-start.2 = (bf16[128,512]{0,1:T(8,128)(2,1)S(1)}, bf16[128,512]{0,1:T(8,128)(2,1)S(1)}, u32[]{:S(2)}, u32[]{:S(2)}) collective-permute-start(bf16[128,512]{0,1:T(8,128)(2,1)S(1)} %copy.78), channel_id=1, source_target_pairs={{0,8},{4,12},{8,16},{12,20},{16,24},{20,28},{1,9},{5,13},{9,17},{1... | collective-permute-start | bytes 393224 | tf_op jit(solution)/shard_map/ppermute | solution.py:18
  42.1 14.3 %collective-permute-start.3 = (bf16[128,512]{0,1:T(8,128)(2,1)S(1)}, bf16[128,512]{0,1:T(8,128)(2,1)S(1)}, u32[]{:S(2)}, u32[]{:S(2)}) collective-permute-start(bf16[128,512]{0,1:T(8,128)(2,1)S(1)} %copy.78), channel_id=1, source_target_pairs={{0,4},{4,8},{8,12},{12,16},{16,20},{20,24},{24,28},{1,5},{5,9},{9,... | collective-permute-start | bytes 393224 | tf_op jit(solution)/shard_map/ppermute | solution.py:18
  63.7 1.3 %copy-start = (bf16[64,4,4096]{2,0,1:T(8,128)(2,1)}, bf16[64,4,4096]{2,0,1:T(8,128)(2,1)S(1)}, u32[]{:S(2)}) copy-start(bf16[64,4,4096]{2,0,1:T(8,128)(2,1)S(1)} %all-to-all-done) | copy-start | bytes 6291460

commit v5 on v3

--- a/solution.py
+++ b/solution.py
@@ -25,14 +25,27 @@
 
 
 def attend_kernel(
-    blocks_ref, q_ref, start_ref, k_ref, v_ref, out_ref, kt_buf, v_buf,
-    *, half_rows, group_size, pad_rows, window
+    blocks_ref, q_ref, start_ref, *refs, half_rows, group_size, pad_rows, window, kv_feat
 ):
+    pieces = window // half_rows
+    low_refs = refs[:pieces]
+    high_refs = refs[pieces : 2 * pieces]
+    out_ref, kt_buf, v_buf = refs[2 * pieces :]
     side = pl.program_id(0)
+    head = pl.program_id(1)
     block_id = blocks_ref[side]
     needed = blocks_ref[2 + side]
-    kt_buf[...] = k_ref[...].T
-    v_buf[:, :DH] = v_ref[...]
+    k_lanes = pl.ds(pl.multiple_of(head * DH, DH), DH)
+    v_lanes = pl.ds(pl.multiple_of(kv_feat + head * DH, DH), DH)
+    for piece_no in range(pieces):
+        keys_at = slice(piece_no * half_rows, (piece_no + 1) * half_rows)
+        for side_no, piece_refs in enumerate((low_refs, high_refs)):
+
+            @pl.when(side == side_no)
+            def _(piece_ref=piece_refs[piece_no], keys_at=keys_at):
+                kt_buf[:, keys_at] = piece_ref[:, k_lanes].T
+                v_buf[keys_at, :DH] = piece_ref[:, v_lanes]
+
     lane = lax.broadcasted_iota(jnp.int32, (window, DH), 1)
     v_buf[:, DH:] = jnp.where(lane == 0, 1.0, 0.0).astype(v_buf.dtype)
     scale = 1.0 / math.sqrt(DH)
@@ -114,9 +127,7 @@
         )
         low_side.append(from_low)
         high_side.append(high_pick)
-    windows = jnp.stack(
-        [jnp.concatenate(low_side[::-1], axis=0), jnp.concatenate(high_side[::-1], axis=0)]
-    )
+    pieces = low_side[::-1] + high_side[::-1]
 
     doc_ends = jnp.cumsum(doc_lengths)
     block_ids = jnp.stack([my_shard, 2 * shards - 1 - my_shard]).astype(jnp.int32)
@@ -132,6 +143,7 @@
         group_size=group_size,
         pad_rows=pad_rows,
         window=window,
+        kv_feat=kv_feat,
     )
     q_cols = group_size * DH
     merged = pl.pallas_call(
@@ -143,16 +155,15 @@
             in_specs=[
                 pl.BlockSpec((half_rows, q_cols), lambda s, h, b: (s, h)),
                 pl.BlockSpec((None, half_rows, 1), lambda s, h, b: (s, 0, 0)),
-                pl.BlockSpec((None, window, DH), lambda s, h, b: (s, 0, h)),
-                pl.BlockSpec((None, window, DH), lambda s, h, b, n=kv_heads: (s, 0, n + h)),
-            ],
+            ]
+            + [pl.BlockSpec((half_rows, 2 * kv_feat), lambda s, h, b: (0, 0))] * len(pieces),
             out_specs=pl.BlockSpec((half_rows, q_cols), lambda s, h, b: (s, h)),
             scratch_shapes=[
                 pltpu.VMEM((DH, window), kv_slab.dtype),
                 pltpu.VMEM((window, 2 * DH), kv_slab.dtype),
             ],
         ),
-    )(block_ids, head_queries, starts, windows, windows)
+    )(block_ids, head_queries, starts, *pieces)
     return lax.all_to_all(merged, "kvh", split_axis=0, concat_axis=1, tiled=True)
 
 

time: 105 us -> 101 us (0.962)
  the two profiles are of different devices: /device:TPU:0 before, /device:TPU:16 now
where the time goes in v5:
time: 101 us
  starting transfers between devices  32.4 us (32%)
  blocking collectives  29.3 us (29%)
  waiting for transfers between devices  14.2 us (14%)
  Pallas kernels  14.1 us (14%)
  local copies, waits for them, and re-layouts  8.51 us (8%)
  other arithmetic  2.69 us (3%)
    all_to_all x1, blocking collectives, on_device(): lax.all_to_all(merged, 'kvh', split_axis=0, concat_axis=1, tiled=True)  29.3 us
    ppermute x8, starting transfers between devices, shifted(): return lax.ppermute(block, axis, route)  19.1 us
    pallas_call x1, Pallas kernels, on_device(): pl.pallas_call(kernel, out_shape=jax.ShapeDtypeStruct(head_queries.shape,...  14.1 us
    ppermute x8, waiting for transfers between devices, shifted(): return lax.ppermute(block, axis, route)  11.3 us
    ppermute x3, starting transfers between devices, on_device(): from_mirror = lax.ppermute(first_half, 'seq', mirror) if mirror else blank  6.15 us
    all_to_all x1, starting transfers between devices, on_device(): lax.all_to_all(queries, 'kvh', split_axis=1, concat_axis=0, tiled=True)  3.74 us
    all_to_all x1, starting transfers between devices, on_device(): lax.all_to_all(kv_local, 'kvh', split_axis=1, concat_axis=0, tiled=True)  3.4 us
    all_to_all x1, local copies, waits for them, and re-layouts, on_device(): lax.all_to_all(queries, 'kvh', split_axis=1, concat_axis=0, tiled=True)  3.13 us
  transfers between devices with their start and end apart: 13, of which 5 were waited for; matrix products, arithmetic and copies ran while one was open for 6% of the time, Pallas kernels for 0%

profile of v5, /device:TPU:16, one launch (start us, length us, event | category | flops | bytes accessed | tf_op | source)
XLA Modules:
  0.0 101.4 jit_solution(15342077532896097509)
XLA Ops:
  0.0 1.0 copy_bitcast_fusion.1
  1.0 0.7 pad_maximum_fusion
  1.7 3.4 %all-to-all-start.1 = ((bf16[64,4,512]{2,0,1:T(8,128)(2,1)}), bf16[64,4,512]{2,0,1:T(8,128)(2,1)S(1)}, u32[]{:S(2)}, u32[]{:S(2)}) async-start(bf16[64,4,512]{2,0,1:T(8,128)(2,1)} %pad_maximum_fusion), calls=%async_computation.1 | async-start | bytes 524288 | tf_op jit(solution)/shard_map/all_to_all | solution.py:100
  5.1 3.1 %copy.26 = bf16[8,4,8,4096]{3,2,0,1:T(8,128)(2,1)} copy(bf16[8,4,8,4096]{3,2,1,0:T(8,128)(2,1)} %bitcast.37) | data formatting | bytes 4194304 | tf_op jit(solution)/shard_map/all_to_all | solution.py:94
  8.2 2.9 %all-to-all-done.1 = bf16[64,4,512]{2,0,1:T(8,128)(2,1)S(1)} async-done(((bf16[64,4,512]{2,0,1:T(8,128)(2,1)}), bf16[64,4,512]{2,0,1:T(8,128)(2,1)S(1)}, u32[]{:S(2)}, u32[]{:S(2)}) %all-to-all-start.1) | async-done | bytes 262176 | tf_op jit(solution)/shard_map/all_to_all | solution.py:100
  11.1 0.0 copy-start.6
  11.1 3.7 %all-to-all-start = ((bf16[64,4,4096]{2,0,1:T(8,128)(2,1)}), bf16[64,4,4096]{2,0,1:T(8,128)(2,1)S(1)}, u32[]{:S(2)}, u32[]{:S(2)}) async-start(bf16[64,4,4096]{2,0,1:T(8,128)(2,1)} %bitcast.35), calls=%async_computation | async-start | bytes 4194304 | tf_op jit(solution)/shard_map/all_to_all | solution.py:94
  14.9 0.1 add_multiply_fusion
  15.0 0.0 copy-start.1
  15.0 0.0 copy-start.2
  15.0 3.3 %collective-permute-start.10 = (bf16[128,512]{1,0:T(8,128)(2,1)S(1)}, bf16[128,512]{1,0:T(8,128)(2,1)S(1)}, u32[]{:S(2)}, u32[]{:S(2)}) collective-permute-start(bf16[128,512]{1,0:T(8,128)(2,1)S(1)} %bitcast.47), channel_id=1, source_target_pairs={{4,0},{8,4},{12,8},{16,12},{20,16},{24,20},{28,24},{5,1},{9,5},{13... | collective-permute-start | bytes 393224 | tf_op jit(solution)/shard_map/ppermute | solution.py:18
  18.3 1.3 %collective-permute-start.4 = (bf16[128,512]{1,0:T(8,128)(2,1)S(1)}, bf16[128,512]{1,0:T(8,128)(2,1)S(1)}, u32[]{:S(2)}, u32[]{:S(2)}) collective-permute-start(bf16[128,512]{1,0:T(8,128)(2,1)S(1)} %bitcast.48), channel_id=1, source_target_pairs={{16,0},{20,4},{24,8},{28,12},{17,1},{21,5},{25,9},{29,13},{18,2},{... | collective-permute-start | bytes 393224 | tf_op jit(solution)/shard_map/ppermute | solution.py:18
  19.6 0.1 add_bitcast_fusion
  19.7 0.0 copy-done.6
  19.7 0.2 reduce-window.8
  19.8 0.1 select_reduce_fusion
  19.9 0.1 slice.15
  20.0 1.9 %collective-permute-start.6 = (bf16[128,512]{1,0:T(8,128)(2,1)S(1)}, bf16[128,512]{1,0:T(8,128)(2,1)S(1)}, u32[]{:S(2)}, u32[]{:S(2)}) collective-permute-start(bf16[128,512]{1,0:T(8,128)(2,1)S(1)} %bitcast.49), channel_id=1, source_target_pairs={{12,0},{16,4},{20,8},{24,12},{28,16},{13,1},{17,5},{21,9},{25,13},... | collective-permute-start | bytes 393224 | tf_op jit(solution)/shard_map/ppermute | solution.py:18
  21.9 4.8 %collective-permute-start.5 = (bf16[128,512]{1,0:T(8,128)(2,1)S(1)}, bf16[128,512]{1,0:T(8,128)(2,1)S(1)}, u32[]{:S(2)}, u32[]{:S(2)}) collective-permute-start(bf16[128,512]{1,0:T(8,128)(2,1)S(1)} %bitcast.38), channel_id=1, source_target_pairs={{16,28},{20,24},{24,20},{28,16},{17,29},{21,25},{25,21},{29,17},{1... | collective-permute-start | bytes 393224 | tf_op jit(solution)/shard_map/ppermute | solution.py:123
  26.8 0.7 collective-permute-start.7
  27.5 0.0 collective-permute-done.10
  27.5 1.9 %collective-permute-start.8 = (bf16[128,512]{1,0:T(8,128)(2,1)S(1)}, bf16[128,512]{1,0:T(8,128)(2,1)S(1)}, u32[]{:S(2)}, u32[]{:S(2)}) collective-permute-start(bf16[128,512]{1,0:T(8,128)(2,1)S(1)} %bitcast.50), channel_id=1, source_target_pairs={{8,0},{12,4},{16,8},{20,12},{24,16},{28,20},{9,1},{13,5},{17,9},{2... | collective-permute-start | bytes 393224 | tf_op jit(solution)/shard_map/ppermute | solution.py:18
  29.4 1.1 %collective-permute-done.4 = bf16[128,512]{1,0:T(8,128)(2,1)S(1)} collective-permute-done((bf16[128,512]{1,0:T(8,128)(2,1)S(1)}, bf16[128,512]{1,0:T(8,128)(2,1)S(1)}, u32[]{:S(2)}, u32[]{:S(2)}) %collective-permute-start.4) | collective-permute-done | bytes 131104 | tf_op jit(solution)/shard_map/ppermute | solution.py:18
  30.5 0.7 collective-permute-start.9
  31.2 0.1 clamp_add_fusion
  31.3 0.8 copy.17.start_ref
  32.1 0.6 pad_add_fusion.blocks_ref
  32.7 0.0 collective-permute-done.5
  32.7 1.3 %collective-permute-start = (bf16[128,512]{1,0:T(8,128)(2,1)S(1)}, bf16[128,512]{1,0:T(8,128)(2,1)S(1)}, u32[]{:S(2)}, u32[]{:S(2)}) collective-permute-start(bf16[128,512]{1,0:T(8,128)(2,1)S(1)} %bitcast.41), channel_id=1, source_target_pairs={{0,16},{4,20},{8,24},{12,28},{1,17},{5,21},{9,25},{13,29},{2,18},{... | collective-permute-start | bytes 393224 | tf_op jit(solution)/shard_map/ppermute | solution.py:18
  34.0 0.0 collective-permute-done.6
  34.0 5.5 %collective-permute-start.1 = (bf16[128,512]{1,0:T(8,128)(2,1)S(1)}, bf16[128,512]{1,0:T(8,128)(2,1)S(1)}, u32[]{:S(2)}, u32[]{:S(2)}) collective-permute-start(bf16[128,512]{1,0:T(8,128)(2,1)S(1)} %bitcast.42), channel_id=1, source_target_pairs={{0,12},{4,16},{8,20},{12,24},{16,28},{1,13},{5,17},{9,21},{13,25},... | collective-permute-start | bytes 393224 | tf_op jit(solution)/shard_map/ppermute | solution.py:18
  39.5 0.0 collective-permute-done.7
  39.5 1.9 %collective-permute-start.2 = (bf16[128,512]{1,0:T(8,128)(2,1)S(1)}, bf16[128,512]{1,0:T(8,128)(2,1)S(1)}, u32[]{:S(2)}, u32[]{:S(2)}) collective-permute-start(bf16[128,512]{1,0:T(8,128)(2,1)S(1)} %bitcast.43), channel_id=1, source_target_pairs={{0,8},{4,12},{8,16},{12,20},{16,24},{20,28},{1,9},{5,13},{9,17},{1... | collective-permute-start | bytes 393224 | tf_op jit(solution)/shard_map/ppermute | solution.py:18
  41.5 0.0 collective-permute-done.8
  41.5 1.9 %collective-permute-start.3 = (bf16[128,512]{1,0:T(8,128)(2,1)S(1)}, bf16[128,512]{1,0:T(8,128)(2,1)}, u32[]{:S(2)}, u32[]{:S(2)}) collective-permute-start(bf16[128,512]{1,0:T(8,128)(2,1)S(1)} %bitcast.44), channel_id=1, source_target_pairs={{0,4},{4,8},{8,12},{12,16},{16,20},{20,24},{24,28},{1,5},{5,9},{9,... | collective-permute-start | bytes 393224 | tf_op jit(solution)/shard_map/ppermute | solution.py:18
  43.4 0.0 collective-permute-done.9
  43.4 0.9 select_select_fusion
  44.3 0.0 collective-permute-done.refs_0_
  44.3 0.0 copy-start.3
  44.3 0.9 collective-permute-done.1.refs_1_
  45.2 0.0 copy-start.4
  45.2 3.7 %collective-permute-done.2.refs_2_ = bf16[128,512]{1,0:T(8,128)(2,1)S(1)} collective-permute-done((bf16[128,512]{1,0:T(8,128)(2,1)S(1)}, bf16[128,512]{1,0:T(8,128)(2,1)S(1)}, u32[]{:S(2)}, u32[]{:S(2)}) %collective-permute-start.2) | collective-permute-done | bytes 131104 | tf_op jit(solution)/shard_map/ppermute | solution.py:18
  48.9 0.0 copy-start.5
  48.9 0.7 copy-done.5
  49.6 5.5 %collective-permute-done.3.refs_3_ = bf16[128,512]{1,0:T(8,128)(2,1)} collective-permute-done((bf16[128,512]{1,0:T(8,128)(2,1)S(1)}, bf16[128,512]{1,0:T(8,128)(2,1)}, u32[]{:S(2)}, u32[]{:S(2)}) %collective-permute-start.3) | collective-permute-done | bytes 131104 | tf_op jit(solution)/shard_map/ppermute | solution.py:18
  55.1 0.0 all-to-all-done
  55.1 0.0 copy-start
  55.1 0.0 copy-done.1
  55.1 0.0 copy-done.2
  55.1 0.0 copy-done.3
  55.1 0.0 copy-done.4
  55.1 1.3 %copy-done = bf16[64,4,4096]{2,0,1:T(8,128)(2,1)} copy-done((bf16[64,4,4096]{2,0,1:T(8,128)(2,1)}, bf16[64,4,4096]{2,0,1:T(8,128)(2,1)S(1)}, u32[]{:S(2)}) %copy-start) | copy-done | bytes 2097176
  56.4 14.1 %shard_map.46 = bf16[256,4096]{1,0:T(8,128)(2,1)} custom-call(s32[4]{0:T(128)} %pad_add_fusion.blocks_ref, bf16[256,4096]{1,0:T(8,128)(2,1)} %bitcast.33, s32[2,128,1]{2,1,0:T(8,128)} %copy.17.start_ref, bf16[128,512]{1,0:T(8,128)(2,1)} %copy-done.3, bf16[128,512]{1,0:T(8,128)(2,1)} %copy-done.4, bf16[128,512]{1,0:T(8,128)(2,1)} %copy-done.5, ...), custom_call_target="tpu_custom_call" | custom-call | tf_op jit(solution)/shard_map/pallas_call | solution.py:149
  70.5 29.3 %all_to_all.53 = bf16[4,64,4096]{2,1,0:T(8,128)(2,1)S(1)} all-to-all(bf16[4,64,4096]{2,1,0:T(8,128)(2,1)} %bitcast.34), channel_id=1, replica_groups=mesh['seq'=8,'kvh'=4] {'kvh'}, dimensions={0} | all-to-all | bytes 4194304 | tf_op jit(solution)/shard_map/all_to_all | solution.py:167
  99.8 1.5 %copy.22 = bf16[4,8,8,4096]{3,2,0,1:T(8,128)(2,1)} copy(bf16[4,8,8,4096]{3,2,1,0:T(8,128)(2,1)S(1)} %bitcast.36) | data formatting | bytes 4194304 | tf_op jit(solution)/shard_map/all_to_all | solution.py:167
  (1 shorter events, 0.0 us)
Async XLA Ops:
  1.7 9.4 %all-to-all-start.1 = ((bf16[64,4,512]{2,0,1:T(8,128)(2,1)}), bf16[64,4,512]{2,0,1:T(8,128)(2,1)S(1)}, u32[]{:S(2)}, u32[]{:S(2)}) async-start(bf16[64,4,512]{2,0,1:T(8,128)(2,1)} %pad_maximum_fusion), calls=%async_computation.1 | async-start | bytes 524288 | tf_op jit(solution)/shard_map/all_to_all | solution.py:100
  11.1 8.5 %copy-start.6 = (s32[8]{0:T(128)S(1)}, s32[8]{0:T(128)}, u32[]{:S(2)}) copy-start(s32[8]{0:T(128)} %param.7) | copy-start | bytes 100
  11.1 44.0 %all-to-all-start = ((bf16[64,4,4096]{2,0,1:T(8,128)(2,1)}), bf16[64,4,4096]{2,0,1:T(8,128)(2,1)S(1)}, u32[]{:S(2)}, u32[]{:S(2)}) async-start(bf16[64,4,4096]{2,0,1:T(8,128)(2,1)} %bitcast.35), calls=%async_computation | async-start | bytes 4194304 | tf_op jit(solution)/shard_map/all_to_all | solution.py:94
  15.0 40.1 %copy-start.1 = (bf16[2,64,1,512]{3,1,0,2:T(8,128)(2,1)}, bf16[2,64,1,512]{3,1,0,2:T(8,128)(2,1)S(1)}, u32[]{:S(2)}) copy-start(bf16[2,64,1,512]{3,1,0,2:T(8,128)(2,1)S(1)} %get-tuple-element.6) | copy-start | bytes 393220
  15.0 40.1 %copy-start.2 = (bf16[2,64,1,512]{3,1,0,2:T(8,128)(2,1)}, bf16[2,64,1,512]{3,1,0,2:T(8,128)(2,1)S(1)}, u32[]{:S(2)}) copy-start(bf16[2,64,1,512]{3,1,0,2:T(8,128)(2,1)S(1)} %get-tuple-element.5) | copy-start | bytes 393220
  15.0 12.5 %collective-permute-start.10 = (bf16[128,512]{1,0:T(8,128)(2,1)S(1)}, bf16[128,512]{1,0:T(8,128)(2,1)S(1)}, u32[]{:S(2)}, u32[]{:S(2)}) collective-permute-start(bf16[128,512]{1,0:T(8,128)(2,1)S(1)} %bitcast.47), channel_id=1, source_target_pairs={{4,0},{8,4},{12,8},{16,12},{20,16},{24,20},{28,24},{5,1},{9,5},{13... | collective-permute-start | bytes 393224 | tf_op jit(solution)/shard_map/ppermute | solution.py:18
  18.3 12.2 %collective-permute-start.4 = (bf16[128,512]{1,0:T(8,128)(2,1)S(1)}, bf16[128,512]{1,0:T(8,128)(2,1)S(1)}, u32[]{:S(2)}, u32[]{:S(2)}) collective-permute-start(bf16[128,512]{1,0:T(8,128)(2,1)S(1)} %bitcast.48), channel_id=1, source_target_pairs={{16,0},{20,4},{24,8},{28,12},{17,1},{21,5},{25,9},{29,13},{18,2},{... | collective-permute-start | bytes 393224 | tf_op jit(solution)/shard_map/ppermute | solution.py:18
  20.0 13.9 %collective-permute-start.6 = (bf16[128,512]{1,0:T(8,128)(2,1)S(1)}, bf16[128,512]{1,0:T(8,128)(2,1)S(1)}, u32[]{:S(2)}, u32[]{:S(2)}) collective-permute-start(bf16[128,512]{1,0:T(8,128)(2,1)S(1)} %bitcast.49), channel_id=1, source_target_pairs={{12,0},{16,4},{20,8},{24,12},{28,16},{13,1},{17,5},{21,9},{25,13},... | collective-permute-start | bytes 393224 | tf_op jit(solution)/shard_map/ppermute | solution.py:18
  21.9 10.7 %collective-permute-start.5 = (bf16[128,512]{1,0:T(8,128)(2,1)S(1)}, bf16[128,512]{1,0:T(8,128)(2,1)S(1)}, u32[]{:S(2)}, u32[]{:S(2)}) collective-permute-start(bf16[128,512]{1,0:T(8,128)(2,1)S(1)} %bitcast.38), channel_id=1, source_target_pairs={{16,28},{20,24},{24,20},{28,16},{17,29},{21,25},{25,21},{29,17},{1... | collective-permute-start | bytes 393224 | tf_op jit(solution)/shard_map/ppermute | solution.py:123
  26.8 12.8 %collective-permute-start.7 = (bf16[128,512]{1,0:T(8,128)(2,1)S(1)}, bf16[128,512]{1,0:T(8,128)(2,1)S(1)}, u32[]{:S(2)}, u32[]{:S(2)}) collective-permute-start(bf16[128,512]{1,0:T(8,128)(2,1)S(1)} %bitcast.39), channel_id=1, source_target_pairs={{20,28},{28,20},{21,29},{29,21},{22,30},{30,22},{23,31},{31,23}} | collective-permute-start | bytes 393224 | tf_op jit(solution)/shard_map/ppermute | solution.py:123
  27.5 14.0 %collective-permute-start.8 = (bf16[128,512]{1,0:T(8,128)(2,1)S(1)}, bf16[128,512]{1,0:T(8,128)(2,1)S(1)}, u32[]{:S(2)}, u32[]{:S(2)}) collective-permute-start(bf16[128,512]{1,0:T(8,128)(2,1)S(1)} %bitcast.50), channel_id=1, source_target_pairs={{8,0},{12,4},{16,8},{20,12},{24,16},{28,20},{9,1},{13,5},{17,9},{2... | collective-permute-start | bytes 393224 | tf_op jit(solution)/shard_map/ppermute | solution.py:18
  30.5 12.9 %collective-permute-start.9 = (bf16[128,512]{1,0:T(8,128)(2,1)S(1)}, bf16[128,512]{1,0:T(8,128)(2,1)S(1)}, u32[]{:S(2)}, u32[]{:S(2)}) collective-permute-start(bf16[128,512]{1,0:T(8,128)(2,1)S(1)} %bitcast.40), channel_id=1, source_target_pairs={{24,28},{28,24},{25,29},{29,25},{26,30},{30,26},{27,31},{31,27}} | collective-permute-start | bytes 393224 | tf_op jit(solution)/shard_map/ppermute | solution.py:123
  32.7 11.6 %collective-permute-start = (bf16[128,512]{1,0:T(8,128)(2,1)S(1)}, bf16[128,512]{1,0:T(8,128)(2,1)S(1)}, u32[]{:S(2)}, u32[]{:S(2)}) collective-permute-start(bf16[128,512]{1,0:T(8,128)(2,1)S(1)} %bitcast.41), channel_id=1, source_target_pairs={{0,16},{4,20},{8,24},{12,28},{1,17},{5,21},{9,25},{13,29},{2,18},{... | collective-permute-start | bytes 393224 | tf_op jit(solution)/shard_map/ppermute | solution.py:18
  34.0 11.2 %collective-permute-start.1 = (bf16[128,512]{1,0:T(8,128)(2,1)S(1)}, bf16[128,512]{1,0:T(8,128)(2,1)S(1)}, u32[]{:S(2)}, u32[]{:S(2)}) collective-permute-start(bf16[128,512]{1,0:T(8,128)(2,1)S(1)} %bitcast.42), channel_id=1, source_target_pairs={{0,12},{4,16},{8,20},{12,24},{16,28},{1,13},{5,17},{9,21},{13,25},... | collective-permute-start | bytes 393224 | tf_op jit(solution)/shard_map/ppermute | solution.py:18
  39.5 9.4 %collective-permute-start.2 = (bf16[128,512]{1,0:T(8,128)(2,1)S(1)}, bf16[128,512]{1,0:T(8,128)(2,1)S(1)}, u32[]{:S(2)}, u32[]{:S(2)}) collective-permute-start(bf16[128,512]{1,0:T(8,128)(2,1)S(1)} %bitcast.43), channel_id=1, source_target_pairs={{0,8},{4,12},{8,16},{12,20},{16,24},{20,28},{1,9},{5,13},{9,17},{1... | collective-permute-start | bytes 393224 | tf_op jit(solution)/shard_map/ppermute | solution.py:18
  41.5 13.6 %collective-permute-start.3 = (bf16[128,512]{1,0:T(8,128)(2,1)S(1)}, bf16[128,512]{1,0:T(8,128)(2,1)}, u32[]{:S(2)}, u32[]{:S(2)}) collective-permute-start(bf16[128,512]{1,0:T(8,128)(2,1)S(1)} %bitcast.44), channel_id=1, source_target_pairs={{0,4},{4,8},{8,12},{12,16},{16,20},{20,24},{24,28},{1,5},{5,9},{9,... | collective-permute-start | bytes 393224 | tf_op jit(solution)/shard_map/ppermute | solution.py:18
  44.3 10.8 %copy-start.3 = (bf16[128,512]{1,0:T(8,128)(2,1)}, bf16[128,512]{1,0:T(8,128)(2,1)S(1)}, u32[]{:S(2)}) copy-start(bf16[128,512]{1,0:T(8,128)(2,1)S(1)} %collective-permute-done.refs_0_) | copy-start | bytes 393220
  45.2 9.9 %copy-start.4 = (bf16[128,512]{1,0:T(8,128)(2,1)}, bf16[128,512]{1,0:T(8,128)(2,1)S(1)}, u32[]{:S(2)}) copy-start(bf16[128,512]{1,0:T(8,128)(2,1)S(1)} %collective-permute-done.1.refs_1_) | copy-start | bytes 393220
  48.9 0.7 copy-start.5
  55.1 1.3 %copy-start = (bf16[64,4,4096]{2,0,1:T(8,128)(2,1)}, bf16[64,4,4096]{2,0,1:T(8,128)(2,1)S(1)}, u32[]{:S(2)}) copy-start(bf16[64,4,4096]{2,0,1:T(8,128)(2,1)S(1)} %all-to-all-done) | copy-start | bytes 6291460

commit v6 on v5

--- a/solution.py
+++ b/solution.py
@@ -41,7 +41,7 @@
         keys_at = slice(piece_no * half_rows, (piece_no + 1) * half_rows)
         for side_no, piece_refs in enumerate((low_refs, high_refs)):
 
-            @pl.when(side == side_no)
+            @pl.when((side == side_no) & (piece_no >= pieces - needed))
             def _(piece_ref=piece_refs[piece_no], keys_at=keys_at):
                 kt_buf[:, keys_at] = piece_ref[:, k_lanes].T
                 v_buf[keys_at, :DH] = piece_ref[:, v_lanes]

time: 101 us -> 99.5 us (0.985); the launches traced: 101 us -> 98.7 us
  Pallas kernels: 14.1 us -> 11.5 us
    pallas_call x1, Pallas kernels: 14.1 us -> 11.5 us  [on_device(): pl.pallas_call(kernel, out_shape=jax.ShapeDtypeStruct(head_queries.shape,...]
where the time goes in v6:
time: 99.5 us; the launch traced here: 98.7 us
  starting transfers between devices  32.4 us (33%)
  blocking collectives  29.3 us (29%)
  waiting for transfers between devices  14.2 us (14%)
  Pallas kernels  11.5 us (12%)
  local copies, waits for them, and re-layouts  8.51 us (9%)
  other arithmetic  2.69 us (3%)
    all_to_all x1, blocking collectives, on_device(): lax.all_to_all(merged, 'kvh', split_axis=0, concat_axis=1, tiled=True)  29.3 us
    ppermute x8, starting transfers between devices, shifted(): return lax.ppermute(block, axis, route)  19.1 us
    pallas_call x1, Pallas kernels, on_device(): pl.pallas_call(kernel, out_shape=jax.ShapeDtypeStruct(head_queries.shape,...  11.5 us
    ppermute x8, waiting for transfers between devices, shifted(): return lax.ppermute(block, axis, route)  11.3 us
    ppermute x3, starting transfers between devices, on_device(): from_mirror = lax.ppermute(first_half, 'seq', mirror) if mirror else blank  6.15 us
    all_to_all x1, starting transfers between devices, on_device(): lax.all_to_all(queries, 'kvh', split_axis=1, concat_axis=0, tiled=True)  3.74 us
    all_to_all x1, starting transfers between devices, on_device(): lax.all_to_all(kv_local, 'kvh', split_axis=1, concat_axis=0, tiled=True)  3.4 us
    all_to_all x1, local copies, waits for them, and re-layouts, on_device(): lax.all_to_all(queries, 'kvh', split_axis=1, concat_axis=0, tiled=True)  3.13 us
  transfers between devices with their start and end apart: 13, of which 5 were waited for; matrix products, arithmetic and copies ran while one was open for 6% of the time, Pallas kernels for 0%

profile of v6, /device:TPU:16, one launch (start us, length us, event | category | flops | bytes accessed | tf_op | source)
XLA Modules:
  0.0 98.7 jit_solution(18138147587575190744)
XLA Ops:
  0.0 1.0 copy_bitcast_fusion.1
  1.0 0.7 pad_maximum_fusion
  1.7 3.4 %all-to-all-start.1 = ((bf16[64,4,512]{2,0,1:T(8,128)(2,1)}), bf16[64,4,512]{2,0,1:T(8,128)(2,1)S(1)}, u32[]{:S(2)}, u32[]{:S(2)}) async-start(bf16[64,4,512]{2,0,1:T(8,128)(2,1)} %pad_maximum_fusion), calls=%async_computation.1 | async-start | bytes 524288 | tf_op jit(solution)/shard_map/all_to_all | solution.py:100
  5.1 3.1 %copy.26 = bf16[8,4,8,4096]{3,2,0,1:T(8,128)(2,1)} copy(bf16[8,4,8,4096]{3,2,1,0:T(8,128)(2,1)} %bitcast.37) | data formatting | bytes 4194304 | tf_op jit(solution)/shard_map/all_to_all | solution.py:94
  8.2 2.9 %all-to-all-done.1 = bf16[64,4,512]{2,0,1:T(8,128)(2,1)S(1)} async-done(((bf16[64,4,512]{2,0,1:T(8,128)(2,1)}), bf16[64,4,512]{2,0,1:T(8,128)(2,1)S(1)}, u32[]{:S(2)}, u32[]{:S(2)}) %all-to-all-start.1) | async-done | bytes 262176 | tf_op jit(solution)/shard_map/all_to_all | solution.py:100
  11.1 0.0 copy-start.6
  11.1 3.7 %all-to-all-start = ((bf16[64,4,4096]{2,0,1:T(8,128)(2,1)}), bf16[64,4,4096]{2,0,1:T(8,128)(2,1)S(1)}, u32[]{:S(2)}, u32[]{:S(2)}) async-start(bf16[64,4,4096]{2,0,1:T(8,128)(2,1)} %bitcast.35), calls=%async_computation | async-start | bytes 4194304 | tf_op jit(solution)/shard_map/all_to_all | solution.py:94
  14.9 0.1 add_multiply_fusion
  15.0 0.0 copy-start.1
  15.0 0.0 copy-start.2
  15.0 3.3 %collective-permute-start.10 = (bf16[128,512]{1,0:T(8,128)(2,1)S(1)}, bf16[128,512]{1,0:T(8,128)(2,1)S(1)}, u32[]{:S(2)}, u32[]{:S(2)}) collective-permute-start(bf16[128,512]{1,0:T(8,128)(2,1)S(1)} %bitcast.47), channel_id=1, source_target_pairs={{4,0},{8,4},{12,8},{16,12},{20,16},{24,20},{28,24},{5,1},{9,5},{13... | collective-permute-start | bytes 393224 | tf_op jit(solution)/shard_map/ppermute | solution.py:18
  18.3 1.3 %collective-permute-start.4 = (bf16[128,512]{1,0:T(8,128)(2,1)S(1)}, bf16[128,512]{1,0:T(8,128)(2,1)S(1)}, u32[]{:S(2)}, u32[]{:S(2)}) collective-permute-start(bf16[128,512]{1,0:T(8,128)(2,1)S(1)} %bitcast.48), channel_id=1, source_target_pairs={{16,0},{20,4},{24,8},{28,12},{17,1},{21,5},{25,9},{29,13},{18,2},{... | collective-permute-start | bytes 393224 | tf_op jit(solution)/shard_map/ppermute | solution.py:18
  19.6 0.1 add_bitcast_fusion
  19.7 0.0 copy-done.6
  19.7 0.2 reduce-window.8
  19.8 0.1 select_reduce_fusion
  19.9 0.1 slice.15
  20.0 1.9 %collective-permute-start.6 = (bf16[128,512]{1,0:T(8,128)(2,1)S(1)}, bf16[128,512]{1,0:T(8,128)(2,1)S(1)}, u32[]{:S(2)}, u32[]{:S(2)}) collective-permute-start(bf16[128,512]{1,0:T(8,128)(2,1)S(1)} %bitcast.49), channel_id=1, source_target_pairs={{12,0},{16,4},{20,8},{24,12},{28,16},{13,1},{17,5},{21,9},{25,13},... | collective-permute-start | bytes 393224 | tf_op jit(solution)/shard_map/ppermute | solution.py:18
  21.9 4.8 %collective-permute-start.5 = (bf16[128,512]{1,0:T(8,128)(2,1)S(1)}, bf16[128,512]{1,0:T(8,128)(2,1)S(1)}, u32[]{:S(2)}, u32[]{:S(2)}) collective-permute-start(bf16[128,512]{1,0:T(8,128)(2,1)S(1)} %bitcast.38), channel_id=1, source_target_pairs={{16,28},{20,24},{24,20},{28,16},{17,29},{21,25},{25,21},{29,17},{1... | collective-permute-start | bytes 393224 | tf_op jit(solution)/shard_map/ppermute | solution.py:123
  26.8 0.7 collective-permute-start.7
  27.5 0.0 collective-permute-done.10
  27.5 1.9 %collective-permute-start.8 = (bf16[128,512]{1,0:T(8,128)(2,1)S(1)}, bf16[128,512]{1,0:T(8,128)(2,1)S(1)}, u32[]{:S(2)}, u32[]{:S(2)}) collective-permute-start(bf16[128,512]{1,0:T(8,128)(2,1)S(1)} %bitcast.50), channel_id=1, source_target_pairs={{8,0},{12,4},{16,8},{20,12},{24,16},{28,20},{9,1},{13,5},{17,9},{2... | collective-permute-start | bytes 393224 | tf_op jit(solution)/shard_map/ppermute | solution.py:18
  29.4 1.1 %collective-permute-done.4 = bf16[128,512]{1,0:T(8,128)(2,1)S(1)} collective-permute-done((bf16[128,512]{1,0:T(8,128)(2,1)S(1)}, bf16[128,512]{1,0:T(8,128)(2,1)S(1)}, u32[]{:S(2)}, u32[]{:S(2)}) %collective-permute-start.4) | collective-permute-done | bytes 131104 | tf_op jit(solution)/shard_map/ppermute | solution.py:18
  30.5 0.7 collective-permute-start.9
  31.2 0.1 clamp_add_fusion
  31.3 0.8 copy.17.start_ref
  32.1 0.6 pad_add_fusion.blocks_ref
  32.7 0.0 collective-permute-done.5
  32.7 1.3 %collective-permute-start = (bf16[128,512]{1,0:T(8,128)(2,1)S(1)}, bf16[128,512]{1,0:T(8,128)(2,1)S(1)}, u32[]{:S(2)}, u32[]{:S(2)}) collective-permute-start(bf16[128,512]{1,0:T(8,128)(2,1)S(1)} %bitcast.41), channel_id=1, source_target_pairs={{0,16},{4,20},{8,24},{12,28},{1,17},{5,21},{9,25},{13,29},{2,18},{... | collective-permute-start | bytes 393224 | tf_op jit(solution)/shard_map/ppermute | solution.py:18
  34.0 0.0 collective-permute-done.6
  34.0 5.5 %collective-permute-start.1 = (bf16[128,512]{1,0:T(8,128)(2,1)S(1)}, bf16[128,512]{1,0:T(8,128)(2,1)S(1)}, u32[]{:S(2)}, u32[]{:S(2)}) collective-permute-start(bf16[128,512]{1,0:T(8,128)(2,1)S(1)} %bitcast.42), channel_id=1, source_target_pairs={{0,12},{4,16},{8,20},{12,24},{16,28},{1,13},{5,17},{9,21},{13,25},... | collective-permute-start | bytes 393224 | tf_op jit(solution)/shard_map/ppermute | solution.py:18
  39.5 0.0 collective-permute-done.7
  39.5 1.9 %collective-permute-start.2 = (bf16[128,512]{1,0:T(8,128)(2,1)S(1)}, bf16[128,512]{1,0:T(8,128)(2,1)S(1)}, u32[]{:S(2)}, u32[]{:S(2)}) collective-permute-start(bf16[128,512]{1,0:T(8,128)(2,1)S(1)} %bitcast.43), channel_id=1, source_target_pairs={{0,8},{4,12},{8,16},{12,20},{16,24},{20,28},{1,9},{5,13},{9,17},{1... | collective-permute-start | bytes 393224 | tf_op jit(solution)/shard_map/ppermute | solution.py:18
  41.5 0.0 collective-permute-done.8
  41.5 1.9 %collective-permute-start.3 = (bf16[128,512]{1,0:T(8,128)(2,1)S(1)}, bf16[128,512]{1,0:T(8,128)(2,1)}, u32[]{:S(2)}, u32[]{:S(2)}) collective-permute-start(bf16[128,512]{1,0:T(8,128)(2,1)S(1)} %bitcast.44), channel_id=1, source_target_pairs={{0,4},{4,8},{8,12},{12,16},{16,20},{20,24},{24,28},{1,5},{5,9},{9,... | collective-permute-start | bytes 393224 | tf_op jit(solution)/shard_map/ppermute | solution.py:18
  43.4 0.0 collective-permute-done.9
  43.4 0.9 select_select_fusion
  44.3 0.0 collective-permute-done.refs_0_
  44.3 0.0 copy-start.3
  44.3 0.9 collective-permute-done.1.refs_1_
  45.2 0.0 copy-start.4
  45.2 3.7 %collective-permute-done.2.refs_2_ = bf16[128,512]{1,0:T(8,128)(2,1)S(1)} collective-permute-done((bf16[128,512]{1,0:T(8,128)(2,1)S(1)}, bf16[128,512]{1,0:T(8,128)(2,1)S(1)}, u32[]{:S(2)}, u32[]{:S(2)}) %collective-permute-start.2) | collective-permute-done | bytes 131104 | tf_op jit(solution)/shard_map/ppermute | solution.py:18
  48.9 0.0 copy-start.5
  48.9 0.7 copy-done.5
  49.6 5.5 %collective-permute-done.3.refs_3_ = bf16[128,512]{1,0:T(8,128)(2,1)} collective-permute-done((bf16[128,512]{1,0:T(8,128)(2,1)S(1)}, bf16[128,512]{1,0:T(8,128)(2,1)}, u32[]{:S(2)}, u32[]{:S(2)}) %collective-permute-start.3) | collective-permute-done | bytes 131104 | tf_op jit(solution)/shard_map/ppermute | solution.py:18
  55.1 0.0 all-to-all-done
  55.1 0.0 copy-start
  55.1 0.0 copy-done.1
  55.1 0.0 copy-done.2
  55.1 0.0 copy-done.3
  55.1 0.0 copy-done.4
  55.1 1.3 %copy-done = bf16[64,4,4096]{2,0,1:T(8,128)(2,1)} copy-done((bf16[64,4,4096]{2,0,1:T(8,128)(2,1)}, bf16[64,4,4096]{2,0,1:T(8,128)(2,1)S(1)}, u32[]{:S(2)}) %copy-start) | copy-done | bytes 2097176
  56.4 11.5 %shard_map.46 = bf16[256,4096]{1,0:T(8,128)(2,1)} custom-call(s32[4]{0:T(128)} %pad_add_fusion.blocks_ref, bf16[256,4096]{1,0:T(8,128)(2,1)} %bitcast.33, s32[2,128,1]{2,1,0:T(8,128)} %copy.17.start_ref, bf16[128,512]{1,0:T(8,128)(2,1)} %copy-done.3, bf16[128,512]{1,0:T(8,128)(2,1)} %copy-done.4, bf16[128,512]{1,0:T(8,128)(2,1)} %copy-done.5, ...), custom_call_target="tpu_custom_call" | custom-call | tf_op jit(solution)/shard_map/pallas_call | solution.py:149
  67.9 29.3 %all_to_all.53 = bf16[4,64,4096]{2,1,0:T(8,128)(2,1)S(1)} all-to-all(bf16[4,64,4096]{2,1,0:T(8,128)(2,1)} %bitcast.34), channel_id=1, replica_groups=mesh['seq'=8,'kvh'=4] {'kvh'}, dimensions={0} | all-to-all | bytes 4194304 | tf_op jit(solution)/shard_map/all_to_all | solution.py:167
  97.2 1.5 %copy.22 = bf16[4,8,8,4096]{3,2,0,1:T(8,128)(2,1)} copy(bf16[4,8,8,4096]{3,2,1,0:T(8,128)(2,1)S(1)} %bitcast.36) | data formatting | bytes 4194304 | tf_op jit(solution)/shard_map/all_to_all | solution.py:167
  (1 shorter events, 0.0 us)
Async XLA Ops:
  1.7 9.4 %all-to-all-start.1 = ((bf16[64,4,512]{2,0,1:T(8,128)(2,1)}), bf16[64,4,512]{2,0,1:T(8,128)(2,1)S(1)}, u32[]{:S(2)}, u32[]{:S(2)}) async-start(bf16[64,4,512]{2,0,1:T(8,128)(2,1)} %pad_maximum_fusion), calls=%async_computation.1 | async-start | bytes 524288 | tf_op jit(solution)/shard_map/all_to_all | solution.py:100
  11.1 8.5 %copy-start.6 = (s32[8]{0:T(128)S(1)}, s32[8]{0:T(128)}, u32[]{:S(2)}) copy-start(s32[8]{0:T(128)} %param.7) | copy-start | bytes 100
  11.1 44.0 %all-to-all-start = ((bf16[64,4,4096]{2,0,1:T(8,128)(2,1)}), bf16[64,4,4096]{2,0,1:T(8,128)(2,1)S(1)}, u32[]{:S(2)}, u32[]{:S(2)}) async-start(bf16[64,4,4096]{2,0,1:T(8,128)(2,1)} %bitcast.35), calls=%async_computation | async-start | bytes 4194304 | tf_op jit(solution)/shard_map/all_to_all | solution.py:94
  15.0 40.1 %copy-start.1 = (bf16[2,64,1,512]{3,1,0,2:T(8,128)(2,1)}, bf16[2,64,1,512]{3,1,0,2:T(8,128)(2,1)S(1)}, u32[]{:S(2)}) copy-start(bf16[2,64,1,512]{3,1,0,2:T(8,128)(2,1)S(1)} %get-tuple-element.6) | copy-start | bytes 393220
  15.0 40.1 %copy-start.2 = (bf16[2,64,1,512]{3,1,0,2:T(8,128)(2,1)}, bf16[2,64,1,512]{3,1,0,2:T(8,128)(2,1)S(1)}, u32[]{:S(2)}) copy-start(bf16[2,64,1,512]{3,1,0,2:T(8,128)(2,1)S(1)} %get-tuple-element.5) | copy-start | bytes 393220
  15.0 12.5 %collective-permute-start.10 = (bf16[128,512]{1,0:T(8,128)(2,1)S(1)}, bf16[128,512]{1,0:T(8,128)(2,1)S(1)}, u32[]{:S(2)}, u32[]{:S(2)}) collective-permute-start(bf16[128,512]{1,0:T(8,128)(2,1)S(1)} %bitcast.47), channel_id=1, source_target_pairs={{4,0},{8,4},{12,8},{16,12},{20,16},{24,20},{28,24},{5,1},{9,5},{13... | collective-permute-start | bytes 393224 | tf_op jit(solution)/shard_map/ppermute | solution.py:18
  18.3 12.2 %collective-permute-start.4 = (bf16[128,512]{1,0:T(8,128)(2,1)S(1)}, bf16[128,512]{1,0:T(8,128)(2,1)S(1)}, u32[]{:S(2)}, u32[]{:S(2)}) collective-permute-start(bf16[128,512]{1,0:T(8,128)(2,1)S(1)} %bitcast.48), channel_id=1, source_target_pairs={{16,0},{20,4},{24,8},{28,12},{17,1},{21,5},{25,9},{29,13},{18,2},{... | collective-permute-start | bytes 393224 | tf_op jit(solution)/shard_map/ppermute | solution.py:18
  20.0 13.9 %collective-permute-start.6 = (bf16[128,512]{1,0:T(8,128)(2,1)S(1)}, bf16[128,512]{1,0:T(8,128)(2,1)S(1)}, u32[]{:S(2)}, u32[]{:S(2)}) collective-permute-start(bf16[128,512]{1,0:T(8,128)(2,1)S(1)} %bitcast.49), channel_id=1, source_target_pairs={{12,0},{16,4},{20,8},{24,12},{28,16},{13,1},{17,5},{21,9},{25,13},... | collective-permute-start | bytes 393224 | tf_op jit(solution)/shard_map/ppermute | solution.py:18
  21.9 10.7 %collective-permute-start.5 = (bf16[128,512]{1,0:T(8,128)(2,1)S(1)}, bf16[128,512]{1,0:T(8,128)(2,1)S(1)}, u32[]{:S(2)}, u32[]{:S(2)}) collective-permute-start(bf16[128,512]{1,0:T(8,128)(2,1)S(1)} %bitcast.38), channel_id=1, source_target_pairs={{16,28},{20,24},{24,20},{28,16},{17,29},{21,25},{25,21},{29,17},{1... | collective-permute-start | bytes 393224 | tf_op jit(solution)/shard_map/ppermute | solution.py:123
  26.8 12.8 %collective-permute-start.7 = (bf16[128,512]{1,0:T(8,128)(2,1)S(1)}, bf16[128,512]{1,0:T(8,128)(2,1)S(1)}, u32[]{:S(2)}, u32[]{:S(2)}) collective-permute-start(bf16[128,512]{1,0:T(8,128)(2,1)S(1)} %bitcast.39), channel_id=1, source_target_pairs={{20,28},{28,20},{21,29},{29,21},{22,30},{30,22},{23,31},{31,23}} | collective-permute-start | bytes 393224 | tf_op jit(solution)/shard_map/ppermute | solution.py:123
  27.5 14.0 %collective-permute-start.8 = (bf16[128,512]{1,0:T(8,128)(2,1)S(1)}, bf16[128,512]{1,0:T(8,128)(2,1)S(1)}, u32[]{:S(2)}, u32[]{:S(2)}) collective-permute-start(bf16[128,512]{1,0:T(8,128)(2,1)S(1)} %bitcast.50), channel_id=1, source_target_pairs={{8,0},{12,4},{16,8},{20,12},{24,16},{28,20},{9,1},{13,5},{17,9},{2... | collective-permute-start | bytes 393224 | tf_op jit(solution)/shard_map/ppermute | solution.py:18
  30.5 12.9 %collective-permute-start.9 = (bf16[128,512]{1,0:T(8,128)(2,1)S(1)}, bf16[128,512]{1,0:T(8,128)(2,1)S(1)}, u32[]{:S(2)}, u32[]{:S(2)}) collective-permute-start(bf16[128,512]{1,0:T(8,128)(2,1)S(1)} %bitcast.40), channel_id=1, source_target_pairs={{24,28},{28,24},{25,29},{29,25},{26,30},{30,26},{27,31},{31,27}} | collective-permute-start | bytes 393224 | tf_op jit(solution)/shard_map/ppermute | solution.py:123
  32.7 11.6 %collective-permute-start = (bf16[128,512]{1,0:T(8,128)(2,1)S(1)}, bf16[128,512]{1,0:T(8,128)(2,1)S(1)}, u32[]{:S(2)}, u32[]{:S(2)}) collective-permute-start(bf16[128,512]{1,0:T(8,128)(2,1)S(1)} %bitcast.41), channel_id=1, source_target_pairs={{0,16},{4,20},{8,24},{12,28},{1,17},{5,21},{9,25},{13,29},{2,18},{... | collective-permute-start | bytes 393224 | tf_op jit(solution)/shard_map/ppermute | solution.py:18
  34.0 11.2 %collective-permute-start.1 = (bf16[128,512]{1,0:T(8,128)(2,1)S(1)}, bf16[128,512]{1,0:T(8,128)(2,1)S(1)}, u32[]{:S(2)}, u32[]{:S(2)}) collective-permute-start(bf16[128,512]{1,0:T(8,128)(2,1)S(1)} %bitcast.42), channel_id=1, source_target_pairs={{0,12},{4,16},{8,20},{12,24},{16,28},{1,13},{5,17},{9,21},{13,25},... | collective-permute-start | bytes 393224 | tf_op jit(solution)/shard_map/ppermute | solution.py:18
  39.5 9.4 %collective-permute-start.2 = (bf16[128,512]{1,0:T(8,128)(2,1)S(1)}, bf16[128,512]{1,0:T(8,128)(2,1)S(1)}, u32[]{:S(2)}, u32[]{:S(2)}) collective-permute-start(bf16[128,512]{1,0:T(8,128)(2,1)S(1)} %bitcast.43), channel_id=1, source_target_pairs={{0,8},{4,12},{8,16},{12,20},{16,24},{20,28},{1,9},{5,13},{9,17},{1... | collective-permute-start | bytes 393224 | tf_op jit(solution)/shard_map/ppermute | solution.py:18
  41.5 13.6 %collective-permute-start.3 = (bf16[128,512]{1,0:T(8,128)(2,1)S(1)}, bf16[128,512]{1,0:T(8,128)(2,1)}, u32[]{:S(2)}, u32[]{:S(2)}) collective-permute-start(bf16[128,512]{1,0:T(8,128)(2,1)S(1)} %bitcast.44), channel_id=1, source_target_pairs={{0,4},{4,8},{8,12},{12,16},{16,20},{20,24},{24,28},{1,5},{5,9},{9,... | collective-permute-start | bytes 393224 | tf_op jit(solution)/shard_map/ppermute | solution.py:18
  44.3 10.8 %copy-start.3 = (bf16[128,512]{1,0:T(8,128)(2,1)}, bf16[128,512]{1,0:T(8,128)(2,1)S(1)}, u32[]{:S(2)}) copy-start(bf16[128,512]{1,0:T(8,128)(2,1)S(1)} %collective-permute-done.refs_0_) | copy-start | bytes 393220
  45.2 9.9 %copy-start.4 = (bf16[128,512]{1,0:T(8,128)(2,1)}, bf16[128,512]{1,0:T(8,128)(2,1)S(1)}, u32[]{:S(2)}) copy-start(bf16[128,512]{1,0:T(8,128)(2,1)S(1)} %collective-permute-done.1.refs_1_) | copy-start | bytes 393220
  48.9 0.7 copy-start.5
  55.1 1.3 %copy-start = (bf16[64,4,4096]{2,0,1:T(8,128)(2,1)}, bf16[64,4,4096]{2,0,1:T(8,128)(2,1)S(1)}, u32[]{:S(2)}) copy-start(bf16[64,4,4096]{2,0,1:T(8,128)(2,1)S(1)} %all-to-all-done) | copy-start | bytes 6291460

commit v7 on v6

--- a/solution.py
+++ b/solution.py
@@ -29,22 +29,30 @@
 ):
     pieces = window // half_rows
     low_refs = refs[:pieces]
-    high_refs = refs[pieces : 2 * pieces]
-    out_ref, kt_buf, v_buf = refs[2 * pieces :]
+    high_refs = refs[pieces : 3 * pieces - 1]
+    out_ref, kt_buf, v_buf = refs[3 * pieces - 1 :]
     side = pl.program_id(0)
     head = pl.program_id(1)
     block_id = blocks_ref[side]
     needed = blocks_ref[2 + side]
     k_lanes = pl.ds(pl.multiple_of(head * DH, DH), DH)
     v_lanes = pl.ds(pl.multiple_of(kv_feat + head * DH, DH), DH)
+
+    def fill(piece_ref, keys_at):
+        kt_buf[:, keys_at] = piece_ref[:, k_lanes].T
+        v_buf[keys_at, :DH] = piece_ref[:, v_lanes]
+
     for piece_no in range(pieces):
         keys_at = slice(piece_no * half_rows, (piece_no + 1) * half_rows)
-        for side_no, piece_refs in enumerate((low_refs, high_refs)):
-
-            @pl.when((side == side_no) & (piece_no >= pieces - needed))
-            def _(piece_ref=piece_refs[piece_no], keys_at=keys_at):
-                kt_buf[:, keys_at] = piece_ref[:, k_lanes].T
-                v_buf[keys_at, :DH] = piece_ref[:, v_lanes]
+        back = pieces - 1 - piece_no
+        pl.when(side == 0)(functools.partial(fill, low_refs[piece_no], keys_at))
+        if back == 0:
+            pl.when(side == 1)(functools.partial(fill, high_refs[0], keys_at))
+            continue
+        source = blocks_ref[3 + back]
+        choices = (high_refs[2 * back - 1], low_refs[pieces - 1], high_refs[2 * back])
+        for code, piece_ref in enumerate(choices):
+            pl.when((side == 1) & (source == code))(functools.partial(fill, piece_ref, keys_at))
 
     lane = lax.broadcasted_iota(jnp.int32, (window, DH), 1)
     v_buf[:, DH:] = jnp.where(lane == 0, 1.0, 0.0).astype(v_buf.dtype)
@@ -115,6 +123,7 @@
     blank = jnp.zeros_like(first_half)
     low_side = [first_half]
     high_side = [second_half]
+    sources = []
     for back in range(1, lookback + 1):
         from_low = shifted(first_half, "seq", back)
         from_high = shifted(second_half, "seq", -back)
@@ -122,19 +131,18 @@
         mirror = [(t, u) for t, u in mirror if 0 <= u < shards and u != t]
         from_mirror = lax.ppermute(first_half, "seq", mirror) if mirror else blank
         wanted = 2 * shards - 1 - my_shard - back
-        high_pick = jnp.where(
-            wanted >= shards, from_high, jnp.where(wanted == my_shard, first_half, from_mirror)
-        )
+        source = jnp.where(wanted >= shards, 0, jnp.where(wanted == my_shard, 1, 2))
         low_side.append(from_low)
-        high_side.append(high_pick)
-    pieces = low_side[::-1] + high_side[::-1]
+        high_side.append((from_high, from_mirror))
+        sources.append(source)
+    pieces = low_side[::-1] + [second_half] + [p for pair in high_side[1:] for p in pair]
 
     doc_ends = jnp.cumsum(doc_lengths)
     block_ids = jnp.stack([my_shard, 2 * shards - 1 - my_shard]).astype(jnp.int32)
     positions = block_ids[:, None] * half_rows + jnp.arange(half_rows, dtype=jnp.int32)[None, :]
     starts = doc_start(positions.reshape(-1), doc_ends, doc_lengths).astype(jnp.int32)
     needed = 1 + jnp.clip((block_ids * half_rows - starts[::half_rows] + half_rows - 1) // half_rows, 0, lookback)
-    block_ids = jnp.concatenate([block_ids, needed.astype(jnp.int32)])
+    block_ids = jnp.concatenate([block_ids, needed.astype(jnp.int32), jnp.stack(sources).astype(jnp.int32)])
     starts = starts.reshape(2, half_rows, 1)
 
     kernel = functools.partial(

time: 99.5 us -> 101 us (1.015)
  the two profiles are of different devices: /device:TPU:16 before, /device:TPU:0 now
where the time goes in v7:
time: 101 us; the launch traced here: 100 us
  blocking collectives  29.3 us (29%)
  starting transfers between devices  29 us (29%)
  waiting for transfers between devices  20.6 us (20%)
  Pallas kernels  11.5 us (11%)
  local copies, waits for them, and re-layouts  8.57 us (8%)
  other arithmetic  1.24 us (1%)
    all_to_all x1, blocking collectives, on_device(): lax.all_to_all(merged, 'kvh', split_axis=0, concat_axis=1, tiled=True)  29.3 us
    ppermute x8, starting transfers between devices, shifted(): return lax.ppermute(block, axis, route)  19.1 us
    ppermute x8, waiting for transfers between devices, shifted(): return lax.ppermute(block, axis, route)  17.7 us
    pallas_call x1, Pallas kernels, on_device(): pl.pallas_call(kernel, out_shape=jax.ShapeDtypeStruct(head_queries.shape,...  11.5 us
    all_to_all x1, starting transfers between devices, on_device(): lax.all_to_all(kv_local, 'kvh', split_axis=1, concat_axis=0, tiled=True)  4.24 us
    all_to_all x1, starting transfers between devices, on_device(): lax.all_to_all(queries, 'kvh', split_axis=1, concat_axis=0, tiled=True)  3.74 us
    all_to_all x1, local copies, waits for them, and re-layouts, on_device(): lax.all_to_all(queries, 'kvh', split_axis=1, concat_axis=0, tiled=True)  3.13 us
    all_to_all x1, waiting for transfers between devices, on_device(): lax.all_to_all(kv_local, 'kvh', split_axis=1, concat_axis=0, tiled=True)  2.91 us
  transfers between devices with their start and end apart: 13, of which 5 were waited for; matrix products, arithmetic and copies ran while one was open for 5% of the time, Pallas kernels for 0%

profile of v7, /device:TPU:0, one launch (start us, length us, event | category | flops | bytes accessed | tf_op | source)
XLA Modules:
  0.0 100.5 jit_solution(14540567585531107323)
XLA Ops:
  0.0 1.0 copy_bitcast_fusion.1
  1.0 0.7 pad_maximum_fusion
  1.7 4.2 %all-to-all-start.1 = ((bf16[64,4,512]{2,0,1:T(8,128)(2,1)}), bf16[64,4,512]{2,0,1:T(8,128)(2,1)S(1)}, u32[]{:S(2)}, u32[]{:S(2)}) async-start(bf16[64,4,512]{2,0,1:T(8,128)(2,1)} %pad_maximum_fusion), calls=%async_computation.1 | async-start | bytes 524288 | tf_op jit(solution)/shard_map/all_to_all | solution.py:108
  6.0 3.1 %copy.26 = bf16[8,4,8,4096]{3,2,0,1:T(8,128)(2,1)} copy(bf16[8,4,8,4096]{3,2,1,0:T(8,128)(2,1)} %bitcast.37) | data formatting | bytes 4194304 | tf_op jit(solution)/shard_map/all_to_all | solution.py:102
  9.1 2.9 %all-to-all-done.1 = bf16[64,4,512]{2,0,1:T(8,128)(2,1)S(1)} async-done(((bf16[64,4,512]{2,0,1:T(8,128)(2,1)}), bf16[64,4,512]{2,0,1:T(8,128)(2,1)S(1)}, u32[]{:S(2)}, u32[]{:S(2)}) %all-to-all-start.1) | async-done | bytes 262176 | tf_op jit(solution)/shard_map/all_to_all | solution.py:108
  12.0 0.0 copy-start.12
  12.0 3.7 %all-to-all-start = ((bf16[64,4,4096]{2,0,1:T(8,128)(2,1)}), bf16[64,4,4096]{2,0,1:T(8,128)(2,1)S(1)}, u32[]{:S(2)}, u32[]{:S(2)}) async-start(bf16[64,4,4096]{2,0,1:T(8,128)(2,1)} %bitcast.35), calls=%async_computation | async-start | bytes 4194304 | tf_op jit(solution)/shard_map/all_to_all | solution.py:102
  15.8 0.0 copy-start.1
  15.8 0.0 copy-start.2
  15.8 5.1 %collective-permute-start = (bf16[128,512]{1,0:T(8,128)(2,1)S(1)}, bf16[128,512]{1,0:T(8,128)(2,1)S(1)}, u32[]{:S(2)}, u32[]{:S(2)}) collective-permute-start(bf16[128,512]{1,0:T(8,128)(2,1)S(1)} %bitcast.44), channel_id=1, source_target_pairs={{0,16},{4,20},{8,24},{12,28},{1,17},{5,21},{9,25},{13,29},{2,18},{... | collective-permute-start | bytes 393224 | tf_op jit(solution)/shard_map/ppermute | solution.py:18
  20.9 0.1 add_multiply_fusion
  21.0 4.4 %collective-permute-start.1 = (bf16[128,512]{1,0:T(8,128)(2,1)S(1)}, bf16[128,512]{1,0:T(8,128)(2,1)S(1)}, u32[]{:S(2)}, u32[]{:S(2)}) collective-permute-start(bf16[128,512]{1,0:T(8,128)(2,1)S(1)} %bitcast.45), channel_id=1, source_target_pairs={{0,12},{4,16},{8,20},{12,24},{16,28},{1,13},{5,17},{9,21},{13,25},... | collective-permute-start | bytes 393224 | tf_op jit(solution)/shard_map/ppermute | solution.py:18
  25.4 0.7 collective-permute-start.10
  26.1 1.3 %collective-permute-start.2 = (bf16[128,512]{1,0:T(8,128)(2,1)S(1)}, bf16[128,512]{1,0:T(8,128)(2,1)S(1)}, u32[]{:S(2)}, u32[]{:S(2)}) collective-permute-start(bf16[128,512]{1,0:T(8,128)(2,1)S(1)} %bitcast.47), channel_id=1, source_target_pairs={{0,8},{4,12},{8,16},{12,20},{16,24},{20,28},{1,9},{5,13},{9,17},{1... | collective-permute-start | bytes 393224 | tf_op jit(solution)/shard_map/ppermute | solution.py:18
  27.4 3.1 %collective-permute-start.3 = (bf16[128,512]{1,0:T(8,128)(2,1)S(1)}, bf16[128,512]{1,0:T(8,128)(2,1)S(1)}, u32[]{:S(2)}, u32[]{:S(2)}) collective-permute-start(bf16[128,512]{1,0:T(8,128)(2,1)S(1)} %bitcast.48), channel_id=1, source_target_pairs={{0,4},{4,8},{8,12},{12,16},{16,20},{20,24},{24,28},{1,5},{5,9},{9,... | collective-permute-start | bytes 393224 | tf_op jit(solution)/shard_map/ppermute | solution.py:18
  30.5 0.0 collective-permute-done.refs_0_
  30.5 0.0 copy-start.3
  30.5 0.7 collective-permute-start.6
  31.2 0.1 add_bitcast_fusion
  31.2 0.0 copy-done.12
  31.2 0.2 reduce-window.8
  31.4 0.1 select_reduce_fusion
  31.5 0.1 slice.15
  31.6 0.8 copy.17.start_ref
  32.4 0.0 collective-permute-done.1.refs_1_
  32.4 0.0 copy-start.4
  32.4 0.7 collective-permute-start.8
  33.1 0.0 collective-permute-done.10.refs_13_
  33.1 0.0 copy-start.5
  33.1 1.3 %collective-permute-start.4 = (bf16[128,512]{1,0:T(8,128)(2,1)S(1)}, bf16[128,512]{1,0:T(8,128)(2,1)S(1)}, u32[]{:S(2)}, u32[]{:S(2)}) collective-permute-start(bf16[128,512]{1,0:T(8,128)(2,1)S(1)} %bitcast.39), channel_id=1, source_target_pairs={{4,0},{8,4},{12,8},{16,12},{20,16},{24,20},{28,24},{5,1},{9,5},{13... | collective-permute-start | bytes 393224 | tf_op jit(solution)/shard_map/ppermute | solution.py:18
  34.4 0.0 collective-permute-done.2.refs_2_
  34.4 0.0 copy-start.6
  34.4 1.3 %collective-permute-start.5 = (bf16[128,512]{1,0:T(8,128)(2,1)S(1)}, bf16[128,512]{1,0:T(8,128)(2,1)S(1)}, u32[]{:S(2)}, u32[]{:S(2)}) collective-permute-start(bf16[128,512]{1,0:T(8,128)(2,1)S(1)} %bitcast.40), channel_id=1, source_target_pairs={{8,0},{12,4},{16,8},{20,12},{24,16},{28,20},{9,1},{13,5},{17,9},{2... | collective-permute-start | bytes 393224 | tf_op jit(solution)/shard_map/ppermute | solution.py:18
  35.7 0.0 collective-permute-done.3.refs_3_
  35.7 0.0 copy-start.7
  35.7 1.3 %collective-permute-start.7 = (bf16[128,512]{1,0:T(8,128)(2,1)S(1)}, bf16[128,512]{1,0:T(8,128)(2,1)}, u32[]{:S(2)}, u32[]{:S(2)}) collective-permute-start(bf16[128,512]{1,0:T(8,128)(2,1)S(1)} %bitcast.41), channel_id=1, source_target_pairs={{12,0},{16,4},{20,8},{24,12},{28,16},{13,1},{17,5},{21,9},{25,13},... | collective-permute-start | bytes 393224 | tf_op jit(solution)/shard_map/ppermute | solution.py:18
  37.0 0.0 collective-permute-done.6.refs_9_
  37.1 0.0 copy-start.8
  37.1 1.3 %collective-permute-start.9 = (bf16[128,512]{1,0:T(8,128)(2,1)S(1)}, bf16[128,512]{1,0:T(8,128)(2,1)}, u32[]{:S(2)}, u32[]{:S(2)}) collective-permute-start(bf16[128,512]{1,0:T(8,128)(2,1)S(1)} %bitcast.42), channel_id=1, source_target_pairs={{16,0},{20,4},{24,8},{28,12},{17,1},{21,5},{25,9},{29,13},{18,2},{... | collective-permute-start | bytes 393224 | tf_op jit(solution)/shard_map/ppermute | solution.py:18
  38.4 0.1 clamp_add_fusion
  38.5 0.7 concatenate.11.blocks_ref
  39.1 0.0 collective-permute-done.8.refs_11_
  39.1 0.0 copy-start.9
  39.1 1.2 %collective-permute-done.4.refs_6_ = bf16[128,512]{1,0:T(8,128)(2,1)S(1)} collective-permute-done((bf16[128,512]{1,0:T(8,128)(2,1)S(1)}, bf16[128,512]{1,0:T(8,128)(2,1)S(1)}, u32[]{:S(2)}, u32[]{:S(2)}) %collective-permute-start.4) | collective-permute-done | bytes 131104 | tf_op jit(solution)/shard_map/ppermute | solution.py:18
  40.4 4.0 %collective-permute-done.5.refs_8_ = bf16[128,512]{1,0:T(8,128)(2,1)S(1)} collective-permute-done((bf16[128,512]{1,0:T(8,128)(2,1)S(1)}, bf16[128,512]{1,0:T(8,128)(2,1)S(1)}, u32[]{:S(2)}, u32[]{:S(2)}) %collective-permute-start.5) | collective-permute-done | bytes 131104 | tf_op jit(solution)/shard_map/ppermute | solution.py:18
  44.3 2.1 %collective-permute-done.7.refs_10_ = bf16[128,512]{1,0:T(8,128)(2,1)} collective-permute-done((bf16[128,512]{1,0:T(8,128)(2,1)S(1)}, bf16[128,512]{1,0:T(8,128)(2,1)}, u32[]{:S(2)}, u32[]{:S(2)}) %collective-permute-start.7) | collective-permute-done | bytes 131104 | tf_op jit(solution)/shard_map/ppermute | solution.py:18
  46.5 10.3 %collective-permute-done.9.refs_12_ = bf16[128,512]{1,0:T(8,128)(2,1)} collective-permute-done((bf16[128,512]{1,0:T(8,128)(2,1)S(1)}, bf16[128,512]{1,0:T(8,128)(2,1)}, u32[]{:S(2)}, u32[]{:S(2)}) %collective-permute-start.9) | collective-permute-done | bytes 131104 | tf_op jit(solution)/shard_map/ppermute | solution.py:18
  56.8 0.0 all-to-all-done
  56.8 0.7 broadcast_in_dim.21.refs_7_
  57.5 0.0 copy-done.1
  57.5 0.0 copy-done.2
  57.5 0.0 copy-done.3
  57.5 0.0 copy-done.4
  57.5 0.0 copy-done.5
  57.5 0.0 copy-done.6
  57.6 0.0 copy-done.7
  57.6 0.0 copy-done.8
  57.6 0.0 copy-done.9
  57.6 0.0 copy-done.10
  57.6 0.0 copy-done.11
  57.6 0.6 copy-done
  58.2 11.5 %shard_map.46 = bf16[256,4096]{1,0:T(8,128)(2,1)} custom-call(s32[8]{0:T(128)} %concatenate.11.blocks_ref, bf16[256,4096]{1,0:T(8,128)(2,1)} %bitcast.33, s32[2,128,1]{2,1,0:T(8,128)} %copy.17.start_ref, bf16[128,512]{1,0:T(8,128)(2,1)} %copy-done.3, bf16[128,512]{1,0:T(8,128)(2,1)} %copy-done.4, bf16[128,512]{1,0:T(8,128)(2,1)} %copy-done.6, ...), custom_call_target="tpu_custom_call" | custom-call | tf_op jit(solution)/shard_map/pallas_call | solution.py:157
  69.7 29.3 %all_to_all.53 = bf16[4,64,4096]{2,1,0:T(8,128)(2,1)S(1)} all-to-all(bf16[4,64,4096]{2,1,0:T(8,128)(2,1)} %bitcast.34), channel_id=1, replica_groups=mesh['seq'=8,'kvh'=4] {'kvh'}, dimensions={0} | all-to-all | bytes 4194304 | tf_op jit(solution)/shard_map/all_to_all | solution.py:175
  98.9 1.5 %copy.22 = bf16[4,8,8,4096]{3,2,0,1:T(8,128)(2,1)} copy(bf16[4,8,8,4096]{3,2,1,0:T(8,128)(2,1)S(1)} %bitcast.36) | data formatting | bytes 4194304 | tf_op jit(solution)/shard_map/all_to_all | solution.py:175
  (4 shorter events, 0.0 us)
Async XLA Ops:
  1.7 10.3 %all-to-all-start.1 = ((bf16[64,4,512]{2,0,1:T(8,128)(2,1)}), bf16[64,4,512]{2,0,1:T(8,128)(2,1)S(1)}, u32[]{:S(2)}, u32[]{:S(2)}) async-start(bf16[64,4,512]{2,0,1:T(8,128)(2,1)} %pad_maximum_fusion), calls=%async_computation.1 | async-start | bytes 524288 | tf_op jit(solution)/shard_map/all_to_all | solution.py:108
  12.0 19.2 %copy-start.12 = (s32[8]{0:T(128)S(1)}, s32[8]{0:T(128)}, u32[]{:S(2)}) copy-start(s32[8]{0:T(128)} %param.7) | copy-start | bytes 100
  12.0 44.8 %all-to-all-start = ((bf16[64,4,4096]{2,0,1:T(8,128)(2,1)}), bf16[64,4,4096]{2,0,1:T(8,128)(2,1)S(1)}, u32[]{:S(2)}, u32[]{:S(2)}) async-start(bf16[64,4,4096]{2,0,1:T(8,128)(2,1)} %bitcast.35), calls=%async_computation | async-start | bytes 4194304 | tf_op jit(solution)/shard_map/all_to_all | solution.py:102
  15.8 41.7 %copy-start.1 = (bf16[2,64,1,512]{3,1,0,2:T(8,128)(2,1)}, bf16[2,64,1,512]{3,1,0,2:T(8,128)(2,1)S(1)}, u32[]{:S(2)}) copy-start(bf16[2,64,1,512]{3,1,0,2:T(8,128)(2,1)S(1)} %get-tuple-element.5) | copy-start | bytes 393220
  15.8 41.7 %copy-start.2 = (bf16[2,64,1,512]{3,1,0,2:T(8,128)(2,1)}, bf16[2,64,1,512]{3,1,0,2:T(8,128)(2,1)S(1)}, u32[]{:S(2)}) copy-start(bf16[2,64,1,512]{3,1,0,2:T(8,128)(2,1)S(1)} %get-tuple-element.6) | copy-start | bytes 393220
  15.8 14.7 %collective-permute-start = (bf16[128,512]{1,0:T(8,128)(2,1)S(1)}, bf16[128,512]{1,0:T(8,128)(2,1)S(1)}, u32[]{:S(2)}, u32[]{:S(2)}) collective-permute-start(bf16[128,512]{1,0:T(8,128)(2,1)S(1)} %bitcast.44), channel_id=1, source_target_pairs={{0,16},{4,20},{8,24},{12,28},{1,17},{5,21},{9,25},{13,29},{2,18},{... | collective-permute-start | bytes 393224 | tf_op jit(solution)/shard_map/ppermute | solution.py:18
  21.0 11.4 %collective-permute-start.1 = (bf16[128,512]{1,0:T(8,128)(2,1)S(1)}, bf16[128,512]{1,0:T(8,128)(2,1)S(1)}, u32[]{:S(2)}, u32[]{:S(2)}) collective-permute-start(bf16[128,512]{1,0:T(8,128)(2,1)S(1)} %bitcast.45), channel_id=1, source_target_pairs={{0,12},{4,16},{8,20},{12,24},{16,28},{1,13},{5,17},{9,21},{13,25},... | collective-permute-start | bytes 393224 | tf_op jit(solution)/shard_map/ppermute | solution.py:18
  25.4 7.7 %collective-permute-start.10 = (bf16[128,512]{1,0:T(8,128)(2,1)S(1)}, bf16[128,512]{1,0:T(8,128)(2,1)S(1)}, u32[]{:S(2)}, u32[]{:S(2)}) collective-permute-start(bf16[128,512]{1,0:T(8,128)(2,1)S(1)} %bitcast.46), channel_id=1, source_target_pairs={{16,28},{20,24},{24,20},{28,16},{17,29},{21,25},{25,21},{29,17},{1... | collective-permute-start | bytes 393224 | tf_op jit(solution)/shard_map/ppermute | solution.py:132
  26.1 8.3 %collective-permute-start.2 = (bf16[128,512]{1,0:T(8,128)(2,1)S(1)}, bf16[128,512]{1,0:T(8,128)(2,1)S(1)}, u32[]{:S(2)}, u32[]{:S(2)}) collective-permute-start(bf16[128,512]{1,0:T(8,128)(2,1)S(1)} %bitcast.47), channel_id=1, source_target_pairs={{0,8},{4,12},{8,16},{12,20},{16,24},{20,28},{1,9},{5,13},{9,17},{1... | collective-permute-start | bytes 393224 | tf_op jit(solution)/shard_map/ppermute | solution.py:18
  27.4 8.4 %collective-permute-start.3 = (bf16[128,512]{1,0:T(8,128)(2,1)S(1)}, bf16[128,512]{1,0:T(8,128)(2,1)S(1)}, u32[]{:S(2)}, u32[]{:S(2)}) collective-permute-start(bf16[128,512]{1,0:T(8,128)(2,1)S(1)} %bitcast.48), channel_id=1, source_target_pairs={{0,4},{4,8},{8,12},{12,16},{16,20},{20,24},{24,28},{1,5},{5,9},{9,... | collective-permute-start | bytes 393224 | tf_op jit(solution)/shard_map/ppermute | solution.py:18
  30.5 27.0 %copy-start.3 = (bf16[128,512]{1,0:T(8,128)(2,1)}, bf16[128,512]{1,0:T(8,128)(2,1)S(1)}, u32[]{:S(2)}) copy-start(bf16[128,512]{1,0:T(8,128)(2,1)S(1)} %collective-permute-done.refs_0_) | copy-start | bytes 393220
  30.5 6.5 %collective-permute-start.6 = (bf16[128,512]{1,0:T(8,128)(2,1)S(1)}, bf16[128,512]{1,0:T(8,128)(2,1)S(1)}, u32[]{:S(2)}, u32[]{:S(2)}) collective-permute-start(bf16[128,512]{1,0:T(8,128)(2,1)S(1)} %bitcast.49), channel_id=1, source_target_pairs={{24,28},{28,24},{25,29},{29,25},{26,30},{30,26},{27,31},{31,27}} | collective-permute-start | bytes 393224 | tf_op jit(solution)/shard_map/ppermute | solution.py:132
  32.4 25.1 %copy-start.4 = (bf16[128,512]{1,0:T(8,128)(2,1)}, bf16[128,512]{1,0:T(8,128)(2,1)S(1)}, u32[]{:S(2)}) copy-start(bf16[128,512]{1,0:T(8,128)(2,1)S(1)} %collective-permute-done.1.refs_1_) | copy-start | bytes 393220
  32.4 6.7 %collective-permute-start.8 = (bf16[128,512]{1,0:T(8,128)(2,1)S(1)}, bf16[128,512]{1,0:T(8,128)(2,1)S(1)}, u32[]{:S(2)}, u32[]{:S(2)}) collective-permute-start(bf16[128,512]{1,0:T(8,128)(2,1)S(1)} %bitcast.50), channel_id=1, source_target_pairs={{20,28},{28,20},{21,29},{29,21},{22,30},{30,22},{23,31},{31,23}} | collective-permute-start | bytes 393224 | tf_op jit(solution)/shard_map/ppermute | solution.py:132
  33.1 24.5 %copy-start.5 = (bf16[128,512]{1,0:T(8,128)(2,1)}, bf16[128,512]{1,0:T(8,128)(2,1)S(1)}, u32[]{:S(2)}) copy-start(bf16[128,512]{1,0:T(8,128)(2,1)S(1)} %collective-permute-done.10.refs_13_) | copy-start | bytes 393220
  33.1 7.3 %collective-permute-start.4 = (bf16[128,512]{1,0:T(8,128)(2,1)S(1)}, bf16[128,512]{1,0:T(8,128)(2,1)S(1)}, u32[]{:S(2)}, u32[]{:S(2)}) collective-permute-start(bf16[128,512]{1,0:T(8,128)(2,1)S(1)} %bitcast.39), channel_id=1, source_target_pairs={{4,0},{8,4},{12,8},{16,12},{20,16},{24,20},{28,24},{5,1},{9,5},{13... | collective-permute-start | bytes 393224 | tf_op jit(solution)/shard_map/ppermute | solution.py:18
  34.4 23.1 %copy-start.6 = (bf16[128,512]{1,0:T(8,128)(2,1)}, bf16[128,512]{1,0:T(8,128)(2,1)S(1)}, u32[]{:S(2)}) copy-start(bf16[128,512]{1,0:T(8,128)(2,1)S(1)} %collective-permute-done.2.refs_2_) | copy-start | bytes 393220
  34.4 9.9 %collective-permute-start.5 = (bf16[128,512]{1,0:T(8,128)(2,1)S(1)}, bf16[128,512]{1,0:T(8,128)(2,1)S(1)}, u32[]{:S(2)}, u32[]{:S(2)}) collective-permute-start(bf16[128,512]{1,0:T(8,128)(2,1)S(1)} %bitcast.40), channel_id=1, source_target_pairs={{8,0},{12,4},{16,8},{20,12},{24,16},{28,20},{9,1},{13,5},{17,9},{2... | collective-permute-start | bytes 393224 | tf_op jit(solution)/shard_map/ppermute | solution.py:18
  35.7 21.8 %copy-start.7 = (bf16[128,512]{1,0:T(8,128)(2,1)}, bf16[128,512]{1,0:T(8,128)(2,1)S(1)}, u32[]{:S(2)}) copy-start(bf16[128,512]{1,0:T(8,128)(2,1)S(1)} %collective-permute-done.3.refs_3_) | copy-start | bytes 393220
  35.7 10.7 %collective-permute-start.7 = (bf16[128,512]{1,0:T(8,128)(2,1)S(1)}, bf16[128,512]{1,0:T(8,128)(2,1)}, u32[]{:S(2)}, u32[]{:S(2)}) collective-permute-start(bf16[128,512]{1,0:T(8,128)(2,1)S(1)} %bitcast.41), channel_id=1, source_target_pairs={{12,0},{16,4},{20,8},{24,12},{28,16},{13,1},{17,5},{21,9},{25,13},... | collective-permute-start | bytes 393224 | tf_op jit(solution)/shard_map/ppermute | solution.py:18
  37.1 20.5 %copy-start.8 = (bf16[128,512]{1,0:T(8,128)(2,1)}, bf16[128,512]{1,0:T(8,128)(2,1)S(1)}, u32[]{:S(2)}) copy-start(bf16[128,512]{1,0:T(8,128)(2,1)S(1)} %collective-permute-done.6.refs_9_) | copy-start | bytes 393220
  37.1 19.7 %collective-permute-start.9 = (bf16[128,512]{1,0:T(8,128)(2,1)S(1)}, bf16[128,512]{1,0:T(8,128)(2,1)}, u32[]{:S(2)}, u32[]{:S(2)}) collective-permute-start(bf16[128,512]{1,0:T(8,128)(2,1)S(1)} %bitcast.42), channel_id=1, source_target_pairs={{16,0},{20,4},{24,8},{28,12},{17,1},{21,5},{25,9},{29,13},{18,2},{... | collective-permute-start | bytes 393224 | tf_op jit(solution)/shard_map/ppermute | solution.py:18
  39.1 18.4 %copy-start.9 = (bf16[128,512]{1,0:T(8,128)(2,1)}, bf16[128,512]{1,0:T(8,128)(2,1)S(1)}, u32[]{:S(2)}) copy-start(bf16[128,512]{1,0:T(8,128)(2,1)S(1)} %collective-permute-done.8.refs_11_) | copy-start | bytes 393220
  40.4 17.2 %copy-start.10 = (bf16[128,512]{1,0:T(8,128)(2,1)}, bf16[128,512]{1,0:T(8,128)(2,1)S(1)}, u32[]{:S(2)}) copy-start(bf16[128,512]{1,0:T(8,128)(2,1)S(1)} %collective-permute-done.4.refs_6_) | copy-start | bytes 393220
  44.3 13.3 %copy-start.11 = (bf16[128,512]{1,0:T(8,128)(2,1)}, bf16[128,512]{1,0:T(8,128)(2,1)S(1)}, u32[]{:S(2)}) copy-start(bf16[128,512]{1,0:T(8,128)(2,1)S(1)} %collective-permute-done.5.refs_8_) | copy-start | bytes 393220
  56.8 1.4 %copy-start = (bf16[64,4,4096]{2,0,1:T(8,128)(2,1)}, bf16[64,4,4096]{2,0,1:T(8,128)(2,1)S(1)}, u32[]{:S(2)}) copy-start(bf16[64,4,4096]{2,0,1:T(8,128)(2,1)S(1)} %all-to-all-done) | copy-start | bytes 6291460

commit v8 on v5

--- a/solution.py
+++ b/solution.py
@@ -9,7 +9,7 @@
 from jax.sharding import PartitionSpec as P
 
 DH = 128
-BUNCH = 4
+BUNCH = 8
 
 
 def shifted(block, axis, distance):

time: 101 us -> 101 us (level); the launches traced: 101 us -> 99.5 us
  Pallas kernels: 14.1 us -> 12.3 us
    pallas_call x1, Pallas kernels: 14.1 us -> 12.3 us  [on_device(): pl.pallas_call(kernel, out_shape=jax.ShapeDtypeStruct(head_queries.shape,...]
where the time goes in v8:
time: 101 us; the launch traced here: 99.5 us
  starting transfers between devices  32.4 us (32%)
  blocking collectives  29.3 us (29%)
  waiting for transfers between devices  14.2 us (14%)
  Pallas kernels  12.3 us (12%)
  local copies, waits for them, and re-layouts  8.51 us (8%)
  other arithmetic  2.69 us (3%)
    all_to_all x1, blocking collectives, on_device(): lax.all_to_all(merged, 'kvh', split_axis=0, concat_axis=1, tiled=True)  29.3 us
    ppermute x8, starting transfers between devices, shifted(): return lax.ppermute(block, axis, route)  19.1 us
    pallas_call x1, Pallas kernels, on_device(): pl.pallas_call(kernel, out_shape=jax.ShapeDtypeStruct(head_queries.shape,...  12.3 us
    ppermute x8, waiting for transfers between devices, shifted(): return lax.ppermute(block, axis, route)  11.3 us
    ppermute x3, starting transfers between devices, on_device(): from_mirror = lax.ppermute(first_half, 'seq', mirror) if mirror else blank  6.15 us
    all_to_all x1, starting transfers between devices, on_device(): lax.all_to_all(queries, 'kvh', split_axis=1, concat_axis=0, tiled=True)  3.74 us
    all_to_all x1, starting transfers between devices, on_device(): lax.all_to_all(kv_local, 'kvh', split_axis=1, concat_axis=0, tiled=True)  3.4 us
    all_to_all x1, local copies, waits for them, and re-layouts, on_device(): lax.all_to_all(queries, 'kvh', split_axis=1, concat_axis=0, tiled=True)  3.13 us
  transfers between devices with their start and end apart: 13, of which 5 were waited for; matrix products, arithmetic and copies ran while one was open for 6% of the time, Pallas kernels for 0%

profile of v8, /device:TPU:16, one launch (start us, length us, event | category | flops | bytes accessed | tf_op | source)
XLA Modules:
  0.0 99.5 jit_solution(15940645735023509046)
XLA Ops:
  0.0 1.0 copy_bitcast_fusion.1
  1.0 0.7 pad_maximum_fusion
  1.7 3.4 %all-to-all-start.1 = ((bf16[64,4,512]{2,0,1:T(8,128)(2,1)}), bf16[64,4,512]{2,0,1:T(8,128)(2,1)S(1)}, u32[]{:S(2)}, u32[]{:S(2)}) async-start(bf16[64,4,512]{2,0,1:T(8,128)(2,1)} %pad_maximum_fusion), calls=%async_computation.1 | async-start | bytes 524288 | tf_op jit(solution)/shard_map/all_to_all | solution.py:100
  5.1 3.1 %copy.26 = bf16[8,4,8,4096]{3,2,0,1:T(8,128)(2,1)} copy(bf16[8,4,8,4096]{3,2,1,0:T(8,128)(2,1)} %bitcast.37) | data formatting | bytes 4194304 | tf_op jit(solution)/shard_map/all_to_all | solution.py:94
  8.2 2.9 %all-to-all-done.1 = bf16[64,4,512]{2,0,1:T(8,128)(2,1)S(1)} async-done(((bf16[64,4,512]{2,0,1:T(8,128)(2,1)}), bf16[64,4,512]{2,0,1:T(8,128)(2,1)S(1)}, u32[]{:S(2)}, u32[]{:S(2)}) %all-to-all-start.1) | async-done | bytes 262176 | tf_op jit(solution)/shard_map/all_to_all | solution.py:100
  11.1 0.0 copy-start.6
  11.1 3.7 %all-to-all-start = ((bf16[64,4,4096]{2,0,1:T(8,128)(2,1)}), bf16[64,4,4096]{2,0,1:T(8,128)(2,1)S(1)}, u32[]{:S(2)}, u32[]{:S(2)}) async-start(bf16[64,4,4096]{2,0,1:T(8,128)(2,1)} %bitcast.35), calls=%async_computation | async-start | bytes 4194304 | tf_op jit(solution)/shard_map/all_to_all | solution.py:94
  14.9 0.1 add_multiply_fusion
  15.0 0.0 copy-start.1
  15.0 0.0 copy-start.2
  15.0 3.3 %collective-permute-start.10 = (bf16[128,512]{1,0:T(8,128)(2,1)S(1)}, bf16[128,512]{1,0:T(8,128)(2,1)S(1)}, u32[]{:S(2)}, u32[]{:S(2)}) collective-permute-start(bf16[128,512]{1,0:T(8,128)(2,1)S(1)} %bitcast.47), channel_id=1, source_target_pairs={{4,0},{8,4},{12,8},{16,12},{20,16},{24,20},{28,24},{5,1},{9,5},{13... | collective-permute-start | bytes 393224 | tf_op jit(solution)/shard_map/ppermute | solution.py:18
  18.3 1.3 %collective-permute-start.4 = (bf16[128,512]{1,0:T(8,128)(2,1)S(1)}, bf16[128,512]{1,0:T(8,128)(2,1)S(1)}, u32[]{:S(2)}, u32[]{:S(2)}) collective-permute-start(bf16[128,512]{1,0:T(8,128)(2,1)S(1)} %bitcast.48), channel_id=1, source_target_pairs={{16,0},{20,4},{24,8},{28,12},{17,1},{21,5},{25,9},{29,13},{18,2},{... | collective-permute-start | bytes 393224 | tf_op jit(solution)/shard_map/ppermute | solution.py:18
  19.6 0.1 add_bitcast_fusion
  19.7 0.0 copy-done.6
  19.7 0.2 reduce-window.8
  19.8 0.1 select_reduce_fusion
  19.9 0.1 slice.15
  20.0 1.9 %collective-permute-start.6 = (bf16[128,512]{1,0:T(8,128)(2,1)S(1)}, bf16[128,512]{1,0:T(8,128)(2,1)S(1)}, u32[]{:S(2)}, u32[]{:S(2)}) collective-permute-start(bf16[128,512]{1,0:T(8,128)(2,1)S(1)} %bitcast.49), channel_id=1, source_target_pairs={{12,0},{16,4},{20,8},{24,12},{28,16},{13,1},{17,5},{21,9},{25,13},... | collective-permute-start | bytes 393224 | tf_op jit(solution)/shard_map/ppermute | solution.py:18
  21.9 4.8 %collective-permute-start.5 = (bf16[128,512]{1,0:T(8,128)(2,1)S(1)}, bf16[128,512]{1,0:T(8,128)(2,1)S(1)}, u32[]{:S(2)}, u32[]{:S(2)}) collective-permute-start(bf16[128,512]{1,0:T(8,128)(2,1)S(1)} %bitcast.38), channel_id=1, source_target_pairs={{16,28},{20,24},{24,20},{28,16},{17,29},{21,25},{25,21},{29,17},{1... | collective-permute-start | bytes 393224 | tf_op jit(solution)/shard_map/ppermute | solution.py:123
  26.8 0.7 collective-permute-start.7
  27.5 0.0 collective-permute-done.10
  27.5 1.9 %collective-permute-start.8 = (bf16[128,512]{1,0:T(8,128)(2,1)S(1)}, bf16[128,512]{1,0:T(8,128)(2,1)S(1)}, u32[]{:S(2)}, u32[]{:S(2)}) collective-permute-start(bf16[128,512]{1,0:T(8,128)(2,1)S(1)} %bitcast.50), channel_id=1, source_target_pairs={{8,0},{12,4},{16,8},{20,12},{24,16},{28,20},{9,1},{13,5},{17,9},{2... | collective-permute-start | bytes 393224 | tf_op jit(solution)/shard_map/ppermute | solution.py:18
  29.4 1.1 %collective-permute-done.4 = bf16[128,512]{1,0:T(8,128)(2,1)S(1)} collective-permute-done((bf16[128,512]{1,0:T(8,128)(2,1)S(1)}, bf16[128,512]{1,0:T(8,128)(2,1)S(1)}, u32[]{:S(2)}, u32[]{:S(2)}) %collective-permute-start.4) | collective-permute-done | bytes 131104 | tf_op jit(solution)/shard_map/ppermute | solution.py:18
  30.5 0.7 collective-permute-start.9
  31.2 0.1 clamp_add_fusion
  31.3 0.8 copy.17.start_ref
  32.1 0.6 pad_add_fusion.blocks_ref
  32.7 0.0 collective-permute-done.5
  32.7 1.3 %collective-permute-start = (bf16[128,512]{1,0:T(8,128)(2,1)S(1)}, bf16[128,512]{1,0:T(8,128)(2,1)S(1)}, u32[]{:S(2)}, u32[]{:S(2)}) collective-permute-start(bf16[128,512]{1,0:T(8,128)(2,1)S(1)} %bitcast.41), channel_id=1, source_target_pairs={{0,16},{4,20},{8,24},{12,28},{1,17},{5,21},{9,25},{13,29},{2,18},{... | collective-permute-start | bytes 393224 | tf_op jit(solution)/shard_map/ppermute | solution.py:18
  34.0 0.0 collective-permute-done.6
  34.0 5.5 %collective-permute-start.1 = (bf16[128,512]{1,0:T(8,128)(2,1)S(1)}, bf16[128,512]{1,0:T(8,128)(2,1)S(1)}, u32[]{:S(2)}, u32[]{:S(2)}) collective-permute-start(bf16[128,512]{1,0:T(8,128)(2,1)S(1)} %bitcast.42), channel_id=1, source_target_pairs={{0,12},{4,16},{8,20},{12,24},{16,28},{1,13},{5,17},{9,21},{13,25},... | collective-permute-start | bytes 393224 | tf_op jit(solution)/shard_map/ppermute | solution.py:18
  39.5 0.0 collective-permute-done.7
  39.5 1.9 %collective-permute-start.2 = (bf16[128,512]{1,0:T(8,128)(2,1)S(1)}, bf16[128,512]{1,0:T(8,128)(2,1)S(1)}, u32[]{:S(2)}, u32[]{:S(2)}) collective-permute-start(bf16[128,512]{1,0:T(8,128)(2,1)S(1)} %bitcast.43), channel_id=1, source_target_pairs={{0,8},{4,12},{8,16},{12,20},{16,24},{20,28},{1,9},{5,13},{9,17},{1... | collective-permute-start | bytes 393224 | tf_op jit(solution)/shard_map/ppermute | solution.py:18
  41.5 0.0 collective-permute-done.8
  41.5 1.9 %collective-permute-start.3 = (bf16[128,512]{1,0:T(8,128)(2,1)S(1)}, bf16[128,512]{1,0:T(8,128)(2,1)}, u32[]{:S(2)}, u32[]{:S(2)}) collective-permute-start(bf16[128,512]{1,0:T(8,128)(2,1)S(1)} %bitcast.44), channel_id=1, source_target_pairs={{0,4},{4,8},{8,12},{12,16},{16,20},{20,24},{24,28},{1,5},{5,9},{9,... | collective-permute-start | bytes 393224 | tf_op jit(solution)/shard_map/ppermute | solution.py:18
  43.4 0.0 collective-permute-done.9
  43.4 0.9 select_select_fusion
  44.3 0.0 collective-permute-done.refs_0_
  44.3 0.0 copy-start.3
  44.3 0.9 collective-permute-done.1.refs_1_
  45.2 0.0 copy-start.4
  45.2 3.7 %collective-permute-done.2.refs_2_ = bf16[128,512]{1,0:T(8,128)(2,1)S(1)} collective-permute-done((bf16[128,512]{1,0:T(8,128)(2,1)S(1)}, bf16[128,512]{1,0:T(8,128)(2,1)S(1)}, u32[]{:S(2)}, u32[]{:S(2)}) %collective-permute-start.2) | collective-permute-done | bytes 131104 | tf_op jit(solution)/shard_map/ppermute | solution.py:18
  48.9 0.0 copy-start.5
  48.9 0.7 copy-done.5
  49.6 5.5 %collective-permute-done.3.refs_3_ = bf16[128,512]{1,0:T(8,128)(2,1)} collective-permute-done((bf16[128,512]{1,0:T(8,128)(2,1)S(1)}, bf16[128,512]{1,0:T(8,128)(2,1)}, u32[]{:S(2)}, u32[]{:S(2)}) %collective-permute-start.3) | collective-permute-done | bytes 131104 | tf_op jit(solution)/shard_map/ppermute | solution.py:18
  55.1 0.0 all-to-all-done
  55.1 0.0 copy-start
  55.1 0.0 copy-done.1
  55.1 0.0 copy-done.2
  55.1 0.0 copy-done.3
  55.1 0.0 copy-done.4
  55.1 1.3 %copy-done = bf16[64,4,4096]{2,0,1:T(8,128)(2,1)} copy-done((bf16[64,4,4096]{2,0,1:T(8,128)(2,1)}, bf16[64,4,4096]{2,0,1:T(8,128)(2,1)S(1)}, u32[]{:S(2)}) %copy-start) | copy-done | bytes 2097176
  56.4 12.3 %shard_map.46 = bf16[256,4096]{1,0:T(8,128)(2,1)} custom-call(s32[4]{0:T(128)} %pad_add_fusion.blocks_ref, bf16[256,4096]{1,0:T(8,128)(2,1)} %bitcast.33, s32[2,128,1]{2,1,0:T(8,128)} %copy.17.start_ref, bf16[128,512]{1,0:T(8,128)(2,1)} %copy-done.3, bf16[128,512]{1,0:T(8,128)(2,1)} %copy-done.4, bf16[128,512]{1,0:T(8,128)(2,1)} %copy-done.5, ...), custom_call_target="tpu_custom_call" | custom-call | tf_op jit(solution)/shard_map/pallas_call | solution.py:149
  68.7 29.3 %all_to_all.53 = bf16[4,64,4096]{2,1,0:T(8,128)(2,1)S(1)} all-to-all(bf16[4,64,4096]{2,1,0:T(8,128)(2,1)} %bitcast.34), channel_id=1, replica_groups=mesh['seq'=8,'kvh'=4] {'kvh'}, dimensions={0} | all-to-all | bytes 4194304 | tf_op jit(solution)/shard_map/all_to_all | solution.py:167
  98.0 1.5 %copy.22 = bf16[4,8,8,4096]{3,2,0,1:T(8,128)(2,1)} copy(bf16[4,8,8,4096]{3,2,1,0:T(8,128)(2,1)S(1)} %bitcast.36) | data formatting | bytes 4194304 | tf_op jit(solution)/shard_map/all_to_all | solution.py:167
  (1 shorter events, 0.0 us)
Async XLA Ops:
  1.7 9.4 %all-to-all-start.1 = ((bf16[64,4,512]{2,0,1:T(8,128)(2,1)}), bf16[64,4,512]{2,0,1:T(8,128)(2,1)S(1)}, u32[]{:S(2)}, u32[]{:S(2)}) async-start(bf16[64,4,512]{2,0,1:T(8,128)(2,1)} %pad_maximum_fusion), calls=%async_computation.1 | async-start | bytes 524288 | tf_op jit(solution)/shard_map/all_to_all | solution.py:100
  11.1 8.5 %copy-start.6 = (s32[8]{0:T(128)S(1)}, s32[8]{0:T(128)}, u32[]{:S(2)}) copy-start(s32[8]{0:T(128)} %param.7) | copy-start | bytes 100
  11.1 44.0 %all-to-all-start = ((bf16[64,4,4096]{2,0,1:T(8,128)(2,1)}), bf16[64,4,4096]{2,0,1:T(8,128)(2,1)S(1)}, u32[]{:S(2)}, u32[]{:S(2)}) async-start(bf16[64,4,4096]{2,0,1:T(8,128)(2,1)} %bitcast.35), calls=%async_computation | async-start | bytes 4194304 | tf_op jit(solution)/shard_map/all_to_all | solution.py:94
  15.0 40.1 %copy-start.1 = (bf16[2,64,1,512]{3,1,0,2:T(8,128)(2,1)}, bf16[2,64,1,512]{3,1,0,2:T(8,128)(2,1)S(1)}, u32[]{:S(2)}) copy-start(bf16[2,64,1,512]{3,1,0,2:T(8,128)(2,1)S(1)} %get-tuple-element.6) | copy-start | bytes 393220
  15.0 40.1 %copy-start.2 = (bf16[2,64,1,512]{3,1,0,2:T(8,128)(2,1)}, bf16[2,64,1,512]{3,1,0,2:T(8,128)(2,1)S(1)}, u32[]{:S(2)}) copy-start(bf16[2,64,1,512]{3,1,0,2:T(8,128)(2,1)S(1)} %get-tuple-element.5) | copy-start | bytes 393220
  15.0 12.5 %collective-permute-start.10 = (bf16[128,512]{1,0:T(8,128)(2,1)S(1)}, bf16[128,512]{1,0:T(8,128)(2,1)S(1)}, u32[]{:S(2)}, u32[]{:S(2)}) collective-permute-start(bf16[128,512]{1,0:T(8,128)(2,1)S(1)} %bitcast.47), channel_id=1, source_target_pairs={{4,0},{8,4},{12,8},{16,12},{20,16},{24,20},{28,24},{5,1},{9,5},{13... | collective-permute-start | bytes 393224 | tf_op jit(solution)/shard_map/ppermute | solution.py:18
  18.3 12.2 %collective-permute-start.4 = (bf16[128,512]{1,0:T(8,128)(2,1)S(1)}, bf16[128,512]{1,0:T(8,128)(2,1)S(1)}, u32[]{:S(2)}, u32[]{:S(2)}) collective-permute-start(bf16[128,512]{1,0:T(8,128)(2,1)S(1)} %bitcast.48), channel_id=1, source_target_pairs={{16,0},{20,4},{24,8},{28,12},{17,1},{21,5},{25,9},{29,13},{18,2},{... | collective-permute-start | bytes 393224 | tf_op jit(solution)/shard_map/ppermute | solution.py:18
  20.0 13.9 %collective-permute-start.6 = (bf16[128,512]{1,0:T(8,128)(2,1)S(1)}, bf16[128,512]{1,0:T(8,128)(2,1)S(1)}, u32[]{:S(2)}, u32[]{:S(2)}) collective-permute-start(bf16[128,512]{1,0:T(8,128)(2,1)S(1)} %bitcast.49), channel_id=1, source_target_pairs={{12,0},{16,4},{20,8},{24,12},{28,16},{13,1},{17,5},{21,9},{25,13},... | collective-permute-start | bytes 393224 | tf_op jit(solution)/shard_map/ppermute | solution.py:18
  21.9 10.7 %collective-permute-start.5 = (bf16[128,512]{1,0:T(8,128)(2,1)S(1)}, bf16[128,512]{1,0:T(8,128)(2,1)S(1)}, u32[]{:S(2)}, u32[]{:S(2)}) collective-permute-start(bf16[128,512]{1,0:T(8,128)(2,1)S(1)} %bitcast.38), channel_id=1, source_target_pairs={{16,28},{20,24},{24,20},{28,16},{17,29},{21,25},{25,21},{29,17},{1... | collective-permute-start | bytes 393224 | tf_op jit(solution)/shard_map/ppermute | solution.py:123
  26.8 12.8 %collective-permute-start.7 = (bf16[128,512]{1,0:T(8,128)(2,1)S(1)}, bf16[128,512]{1,0:T(8,128)(2,1)S(1)}, u32[]{:S(2)}, u32[]{:S(2)}) collective-permute-start(bf16[128,512]{1,0:T(8,128)(2,1)S(1)} %bitcast.39), channel_id=1, source_target_pairs={{20,28},{28,20},{21,29},{29,21},{22,30},{30,22},{23,31},{31,23}} | collective-permute-start | bytes 393224 | tf_op jit(solution)/shard_map/ppermute | solution.py:123
  27.5 14.0 %collective-permute-start.8 = (bf16[128,512]{1,0:T(8,128)(2,1)S(1)}, bf16[128,512]{1,0:T(8,128)(2,1)S(1)}, u32[]{:S(2)}, u32[]{:S(2)}) collective-permute-start(bf16[128,512]{1,0:T(8,128)(2,1)S(1)} %bitcast.50), channel_id=1, source_target_pairs={{8,0},{12,4},{16,8},{20,12},{24,16},{28,20},{9,1},{13,5},{17,9},{2... | collective-permute-start | bytes 393224 | tf_op jit(solution)/shard_map/ppermute | solution.py:18
  30.5 12.9 %collective-permute-start.9 = (bf16[128,512]{1,0:T(8,128)(2,1)S(1)}, bf16[128,512]{1,0:T(8,128)(2,1)S(1)}, u32[]{:S(2)}, u32[]{:S(2)}) collective-permute-start(bf16[128,512]{1,0:T(8,128)(2,1)S(1)} %bitcast.40), channel_id=1, source_target_pairs={{24,28},{28,24},{25,29},{29,25},{26,30},{30,26},{27,31},{31,27}} | collective-permute-start | bytes 393224 | tf_op jit(solution)/shard_map/ppermute | solution.py:123
  32.7 11.6 %collective-permute-start = (bf16[128,512]{1,0:T(8,128)(2,1)S(1)}, bf16[128,512]{1,0:T(8,128)(2,1)S(1)}, u32[]{:S(2)}, u32[]{:S(2)}) collective-permute-start(bf16[128,512]{1,0:T(8,128)(2,1)S(1)} %bitcast.41), channel_id=1, source_target_pairs={{0,16},{4,20},{8,24},{12,28},{1,17},{5,21},{9,25},{13,29},{2,18},{... | collective-permute-start | bytes 393224 | tf_op jit(solution)/shard_map/ppermute | solution.py:18
  34.0 11.2 %collective-permute-start.1 = (bf16[128,512]{1,0:T(8,128)(2,1)S(1)}, bf16[128,512]{1,0:T(8,128)(2,1)S(1)}, u32[]{:S(2)}, u32[]{:S(2)}) collective-permute-start(bf16[128,512]{1,0:T(8,128)(2,1)S(1)} %bitcast.42), channel_id=1, source_target_pairs={{0,12},{4,16},{8,20},{12,24},{16,28},{1,13},{5,17},{9,21},{13,25},... | collective-permute-start | bytes 393224 | tf_op jit(solution)/shard_map/ppermute | solution.py:18
  39.5 9.4 %collective-permute-start.2 = (bf16[128,512]{1,0:T(8,128)(2,1)S(1)}, bf16[128,512]{1,0:T(8,128)(2,1)S(1)}, u32[]{:S(2)}, u32[]{:S(2)}) collective-permute-start(bf16[128,512]{1,0:T(8,128)(2,1)S(1)} %bitcast.43), channel_id=1, source_target_pairs={{0,8},{4,12},{8,16},{12,20},{16,24},{20,28},{1,9},{5,13},{9,17},{1... | collective-permute-start | bytes 393224 | tf_op jit(solution)/shard_map/ppermute | solution.py:18
  41.5 13.6 %collective-permute-start.3 = (bf16[128,512]{1,0:T(8,128)(2,1)S(1)}, bf16[128,512]{1,0:T(8,128)(2,1)}, u32[]{:S(2)}, u32[]{:S(2)}) collective-permute-start(bf16[128,512]{1,0:T(8,128)(2,1)S(1)} %bitcast.44), channel_id=1, source_target_pairs={{0,4},{4,8},{8,12},{12,16},{16,20},{20,24},{24,28},{1,5},{5,9},{9,... | collective-permute-start | bytes 393224 | tf_op jit(solution)/shard_map/ppermute | solution.py:18
  44.3 10.8 %copy-start.3 = (bf16[128,512]{1,0:T(8,128)(2,1)}, bf16[128,512]{1,0:T(8,128)(2,1)S(1)}, u32[]{:S(2)}) copy-start(bf16[128,512]{1,0:T(8,128)(2,1)S(1)} %collective-permute-done.refs_0_) | copy-start | bytes 393220
  45.2 9.9 %copy-start.4 = (bf16[128,512]{1,0:T(8,128)(2,1)}, bf16[128,512]{1,0:T(8,128)(2,1)S(1)}, u32[]{:S(2)}) copy-start(bf16[128,512]{1,0:T(8,128)(2,1)S(1)} %collective-permute-done.1.refs_1_) | copy-start | bytes 393220
  48.9 0.7 copy-start.5
  55.1 1.3 %copy-start = (bf16[64,4,4096]{2,0,1:T(8,128)(2,1)}, bf16[64,4,4096]{2,0,1:T(8,128)(2,1)S(1)}, u32[]{:S(2)}) copy-start(bf16[64,4,4096]{2,0,1:T(8,128)(2,1)S(1)} %all-to-all-done) | copy-start | bytes 6291460

commit v9 on v5

--- a/solution.py
+++ b/solution.py
@@ -46,8 +46,11 @@
                 kt_buf[:, keys_at] = piece_ref[:, k_lanes].T
                 v_buf[keys_at, :DH] = piece_ref[:, v_lanes]
 
-    lane = lax.broadcasted_iota(jnp.int32, (window, DH), 1)
-    v_buf[:, DH:] = jnp.where(lane == 0, 1.0, 0.0).astype(v_buf.dtype)
+    @pl.when((side == 0) & (head == 0))
+    def _():
+        lane = lax.broadcasted_iota(jnp.int32, (window, DH), 1)
+        v_buf[:, DH:] = jnp.where(lane == 0, 1.0, 0.0).astype(v_buf.dtype)
+
     scale = 1.0 / math.sqrt(DH)
     row_start = start_ref[...]
 

time: 101 us -> 99.8 us (0.988)
  Pallas kernels: 14.1 us -> 12.4 us
    pallas_call x1, Pallas kernels: 14.1 us -> 12.4 us  [on_device(): pl.pallas_call(kernel, out_shape=jax.ShapeDtypeStruct(head_queries.shape,...]
where the time goes in v9:
time: 99.8 us; the launch traced here: 99.6 us
  starting transfers between devices  32.4 us (32%)
  blocking collectives  29.3 us (29%)
  waiting for transfers between devices  14.2 us (14%)
  Pallas kernels  12.4 us (12%)
  local copies, waits for them, and re-layouts  8.51 us (9%)
  other arithmetic  2.69 us (3%)
    all_to_all x1, blocking collectives, on_device(): lax.all_to_all(merged, 'kvh', split_axis=0, concat_axis=1, tiled=True)  29.3 us
    ppermute x8, starting transfers between devices, shifted(): return lax.ppermute(block, axis, route)  19.1 us
    pallas_call x1, Pallas kernels, on_device(): pl.pallas_call(kernel, out_shape=jax.ShapeDtypeStruct(head_queries.shape,...  12.4 us
    ppermute x8, waiting for transfers between devices, shifted(): return lax.ppermute(block, axis, route)  11.3 us
    ppermute x3, starting transfers between devices, on_device(): from_mirror = lax.ppermute(first_half, 'seq', mirror) if mirror else blank  6.15 us
    all_to_all x1, starting transfers between devices, on_device(): lax.all_to_all(queries, 'kvh', split_axis=1, concat_axis=0, tiled=True)  3.74 us
    all_to_all x1, starting transfers between devices, on_device(): lax.all_to_all(kv_local, 'kvh', split_axis=1, concat_axis=0, tiled=True)  3.4 us
    all_to_all x1, local copies, waits for them, and re-layouts, on_device(): lax.all_to_all(queries, 'kvh', split_axis=1, concat_axis=0, tiled=True)  3.13 us
  transfers between devices with their start and end apart: 13, of which 5 were waited for; matrix products, arithmetic and copies ran while one was open for 6% of the time, Pallas kernels for 0%

profile of v9, /device:TPU:16, one launch (start us, length us, event | category | flops | bytes accessed | tf_op | source)
XLA Modules:
  0.0 99.6 jit_solution(10733252808347947371)
XLA Ops:
  0.0 1.0 copy_bitcast_fusion.1
  1.0 0.7 pad_maximum_fusion
  1.7 3.4 %all-to-all-start.1 = ((bf16[64,4,512]{2,0,1:T(8,128)(2,1)}), bf16[64,4,512]{2,0,1:T(8,128)(2,1)S(1)}, u32[]{:S(2)}, u32[]{:S(2)}) async-start(bf16[64,4,512]{2,0,1:T(8,128)(2,1)} %pad_maximum_fusion), calls=%async_computation.1 | async-start | bytes 524288 | tf_op jit(solution)/shard_map/all_to_all | solution.py:103
  5.1 3.1 %copy.26 = bf16[8,4,8,4096]{3,2,0,1:T(8,128)(2,1)} copy(bf16[8,4,8,4096]{3,2,1,0:T(8,128)(2,1)} %bitcast.37) | data formatting | bytes 4194304 | tf_op jit(solution)/shard_map/all_to_all | solution.py:97
  8.2 2.9 %all-to-all-done.1 = bf16[64,4,512]{2,0,1:T(8,128)(2,1)S(1)} async-done(((bf16[64,4,512]{2,0,1:T(8,128)(2,1)}), bf16[64,4,512]{2,0,1:T(8,128)(2,1)S(1)}, u32[]{:S(2)}, u32[]{:S(2)}) %all-to-all-start.1) | async-done | bytes 262176 | tf_op jit(solution)/shard_map/all_to_all | solution.py:103
  11.1 0.0 copy-start.6
  11.1 3.7 %all-to-all-start = ((bf16[64,4,4096]{2,0,1:T(8,128)(2,1)}), bf16[64,4,4096]{2,0,1:T(8,128)(2,1)S(1)}, u32[]{:S(2)}, u32[]{:S(2)}) async-start(bf16[64,4,4096]{2,0,1:T(8,128)(2,1)} %bitcast.35), calls=%async_computation | async-start | bytes 4194304 | tf_op jit(solution)/shard_map/all_to_all | solution.py:97
  14.9 0.1 add_multiply_fusion
  15.0 0.0 copy-start.1
  15.0 0.0 copy-start.2
  15.0 3.3 %collective-permute-start.10 = (bf16[128,512]{1,0:T(8,128)(2,1)S(1)}, bf16[128,512]{1,0:T(8,128)(2,1)S(1)}, u32[]{:S(2)}, u32[]{:S(2)}) collective-permute-start(bf16[128,512]{1,0:T(8,128)(2,1)S(1)} %bitcast.47), channel_id=1, source_target_pairs={{4,0},{8,4},{12,8},{16,12},{20,16},{24,20},{28,24},{5,1},{9,5},{13... | collective-permute-start | bytes 393224 | tf_op jit(solution)/shard_map/ppermute | solution.py:18
  18.3 1.3 %collective-permute-start.4 = (bf16[128,512]{1,0:T(8,128)(2,1)S(1)}, bf16[128,512]{1,0:T(8,128)(2,1)S(1)}, u32[]{:S(2)}, u32[]{:S(2)}) collective-permute-start(bf16[128,512]{1,0:T(8,128)(2,1)S(1)} %bitcast.48), channel_id=1, source_target_pairs={{16,0},{20,4},{24,8},{28,12},{17,1},{21,5},{25,9},{29,13},{18,2},{... | collective-permute-start | bytes 393224 | tf_op jit(solution)/shard_map/ppermute | solution.py:18
  19.6 0.1 add_bitcast_fusion
  19.7 0.0 copy-done.6
  19.7 0.2 reduce-window.8
  19.8 0.1 select_reduce_fusion
  19.9 0.1 slice.15
  20.0 1.9 %collective-permute-start.6 = (bf16[128,512]{1,0:T(8,128)(2,1)S(1)}, bf16[128,512]{1,0:T(8,128)(2,1)S(1)}, u32[]{:S(2)}, u32[]{:S(2)}) collective-permute-start(bf16[128,512]{1,0:T(8,128)(2,1)S(1)} %bitcast.49), channel_id=1, source_target_pairs={{12,0},{16,4},{20,8},{24,12},{28,16},{13,1},{17,5},{21,9},{25,13},... | collective-permute-start | bytes 393224 | tf_op jit(solution)/shard_map/ppermute | solution.py:18
  21.9 4.8 %collective-permute-start.5 = (bf16[128,512]{1,0:T(8,128)(2,1)S(1)}, bf16[128,512]{1,0:T(8,128)(2,1)S(1)}, u32[]{:S(2)}, u32[]{:S(2)}) collective-permute-start(bf16[128,512]{1,0:T(8,128)(2,1)S(1)} %bitcast.38), channel_id=1, source_target_pairs={{16,28},{20,24},{24,20},{28,16},{17,29},{21,25},{25,21},{29,17},{1... | collective-permute-start | bytes 393224 | tf_op jit(solution)/shard_map/ppermute | solution.py:126
  26.8 0.7 collective-permute-start.7
  27.5 0.0 collective-permute-done.10
  27.5 1.9 %collective-permute-start.8 = (bf16[128,512]{1,0:T(8,128)(2,1)S(1)}, bf16[128,512]{1,0:T(8,128)(2,1)S(1)}, u32[]{:S(2)}, u32[]{:S(2)}) collective-permute-start(bf16[128,512]{1,0:T(8,128)(2,1)S(1)} %bitcast.50), channel_id=1, source_target_pairs={{8,0},{12,4},{16,8},{20,12},{24,16},{28,20},{9,1},{13,5},{17,9},{2... | collective-permute-start | bytes 393224 | tf_op jit(solution)/shard_map/ppermute | solution.py:18
  29.4 1.1 %collective-permute-done.4 = bf16[128,512]{1,0:T(8,128)(2,1)S(1)} collective-permute-done((bf16[128,512]{1,0:T(8,128)(2,1)S(1)}, bf16[128,512]{1,0:T(8,128)(2,1)S(1)}, u32[]{:S(2)}, u32[]{:S(2)}) %collective-permute-start.4) | collective-permute-done | bytes 131104 | tf_op jit(solution)/shard_map/ppermute | solution.py:18
  30.5 0.7 collective-permute-start.9
  31.2 0.1 clamp_add_fusion
  31.3 0.8 copy.17.start_ref
  32.1 0.6 pad_add_fusion.blocks_ref
  32.7 0.0 collective-permute-done.5
  32.7 1.3 %collective-permute-start = (bf16[128,512]{1,0:T(8,128)(2,1)S(1)}, bf16[128,512]{1,0:T(8,128)(2,1)S(1)}, u32[]{:S(2)}, u32[]{:S(2)}) collective-permute-start(bf16[128,512]{1,0:T(8,128)(2,1)S(1)} %bitcast.41), channel_id=1, source_target_pairs={{0,16},{4,20},{8,24},{12,28},{1,17},{5,21},{9,25},{13,29},{2,18},{... | collective-permute-start | bytes 393224 | tf_op jit(solution)/shard_map/ppermute | solution.py:18
  34.0 0.0 collective-permute-done.6
  34.0 5.5 %collective-permute-start.1 = (bf16[128,512]{1,0:T(8,128)(2,1)S(1)}, bf16[128,512]{1,0:T(8,128)(2,1)S(1)}, u32[]{:S(2)}, u32[]{:S(2)}) collective-permute-start(bf16[128,512]{1,0:T(8,128)(2,1)S(1)} %bitcast.42), channel_id=1, source_target_pairs={{0,12},{4,16},{8,20},{12,24},{16,28},{1,13},{5,17},{9,21},{13,25},... | collective-permute-start | bytes 393224 | tf_op jit(solution)/shard_map/ppermute | solution.py:18
  39.5 0.0 collective-permute-done.7
  39.5 1.9 %collective-permute-start.2 = (bf16[128,512]{1,0:T(8,128)(2,1)S(1)}, bf16[128,512]{1,0:T(8,128)(2,1)S(1)}, u32[]{:S(2)}, u32[]{:S(2)}) collective-permute-start(bf16[128,512]{1,0:T(8,128)(2,1)S(1)} %bitcast.43), channel_id=1, source_target_pairs={{0,8},{4,12},{8,16},{12,20},{16,24},{20,28},{1,9},{5,13},{9,17},{1... | collective-permute-start | bytes 393224 | tf_op jit(solution)/shard_map/ppermute | solution.py:18
  41.5 0.0 collective-permute-done.8
  41.5 1.9 %collective-permute-start.3 = (bf16[128,512]{1,0:T(8,128)(2,1)S(1)}, bf16[128,512]{1,0:T(8,128)(2,1)}, u32[]{:S(2)}, u32[]{:S(2)}) collective-permute-start(bf16[128,512]{1,0:T(8,128)(2,1)S(1)} %bitcast.44), channel_id=1, source_target_pairs={{0,4},{4,8},{8,12},{12,16},{16,20},{20,24},{24,28},{1,5},{5,9},{9,... | collective-permute-start | bytes 393224 | tf_op jit(solution)/shard_map/ppermute | solution.py:18
  43.4 0.0 collective-permute-done.9
  43.4 0.9 select_select_fusion
  44.3 0.0 collective-permute-done.refs_0_
  44.3 0.0 copy-start.3
  44.3 0.9 collective-permute-done.1.refs_1_
  45.2 0.0 copy-start.4
  45.2 3.7 %collective-permute-done.2.refs_2_ = bf16[128,512]{1,0:T(8,128)(2,1)S(1)} collective-permute-done((bf16[128,512]{1,0:T(8,128)(2,1)S(1)}, bf16[128,512]{1,0:T(8,128)(2,1)S(1)}, u32[]{:S(2)}, u32[]{:S(2)}) %collective-permute-start.2) | collective-permute-done | bytes 131104 | tf_op jit(solution)/shard_map/ppermute | solution.py:18
  48.9 0.0 copy-start.5
  48.9 0.7 copy-done.5
  49.6 5.5 %collective-permute-done.3.refs_3_ = bf16[128,512]{1,0:T(8,128)(2,1)} collective-permute-done((bf16[128,512]{1,0:T(8,128)(2,1)S(1)}, bf16[128,512]{1,0:T(8,128)(2,1)}, u32[]{:S(2)}, u32[]{:S(2)}) %collective-permute-start.3) | collective-permute-done | bytes 131104 | tf_op jit(solution)/shard_map/ppermute | solution.py:18
  55.1 0.0 all-to-all-done
  55.1 0.0 copy-start
  55.1 0.0 copy-done.1
  55.1 0.0 copy-done.2
  55.1 0.0 copy-done.3
  55.1 0.0 copy-done.4
  55.1 1.3 %copy-done = bf16[64,4,4096]{2,0,1:T(8,128)(2,1)} copy-done((bf16[64,4,4096]{2,0,1:T(8,128)(2,1)}, bf16[64,4,4096]{2,0,1:T(8,128)(2,1)S(1)}, u32[]{:S(2)}) %copy-start) | copy-done | bytes 2097176
  56.4 12.4 %shard_map.46 = bf16[256,4096]{1,0:T(8,128)(2,1)} custom-call(s32[4]{0:T(128)} %pad_add_fusion.blocks_ref, bf16[256,4096]{1,0:T(8,128)(2,1)} %bitcast.33, s32[2,128,1]{2,1,0:T(8,128)} %copy.17.start_ref, bf16[128,512]{1,0:T(8,128)(2,1)} %copy-done.3, bf16[128,512]{1,0:T(8,128)(2,1)} %copy-done.4, bf16[128,512]{1,0:T(8,128)(2,1)} %copy-done.5, ...), custom_call_target="tpu_custom_call" | custom-call | tf_op jit(solution)/shard_map/pallas_call | solution.py:152
  68.8 29.3 %all_to_all.53 = bf16[4,64,4096]{2,1,0:T(8,128)(2,1)S(1)} all-to-all(bf16[4,64,4096]{2,1,0:T(8,128)(2,1)} %bitcast.34), channel_id=1, replica_groups=mesh['seq'=8,'kvh'=4] {'kvh'}, dimensions={0} | all-to-all | bytes 4194304 | tf_op jit(solution)/shard_map/all_to_all | solution.py:170
  98.1 1.5 %copy.22 = bf16[4,8,8,4096]{3,2,0,1:T(8,128)(2,1)} copy(bf16[4,8,8,4096]{3,2,1,0:T(8,128)(2,1)S(1)} %bitcast.36) | data formatting | bytes 4194304 | tf_op jit(solution)/shard_map/all_to_all | solution.py:170
  (1 shorter events, 0.0 us)
Async XLA Ops:
  1.7 9.4 %all-to-all-start.1 = ((bf16[64,4,512]{2,0,1:T(8,128)(2,1)}), bf16[64,4,512]{2,0,1:T(8,128)(2,1)S(1)}, u32[]{:S(2)}, u32[]{:S(2)}) async-start(bf16[64,4,512]{2,0,1:T(8,128)(2,1)} %pad_maximum_fusion), calls=%async_computation.1 | async-start | bytes 524288 | tf_op jit(solution)/shard_map/all_to_all | solution.py:103
  11.1 8.5 %copy-start.6 = (s32[8]{0:T(128)S(1)}, s32[8]{0:T(128)}, u32[]{:S(2)}) copy-start(s32[8]{0:T(128)} %param.7) | copy-start | bytes 100
  11.1 44.0 %all-to-all-start = ((bf16[64,4,4096]{2,0,1:T(8,128)(2,1)}), bf16[64,4,4096]{2,0,1:T(8,128)(2,1)S(1)}, u32[]{:S(2)}, u32[]{:S(2)}) async-start(bf16[64,4,4096]{2,0,1:T(8,128)(2,1)} %bitcast.35), calls=%async_computation | async-start | bytes 4194304 | tf_op jit(solution)/shard_map/all_to_all | solution.py:97
  15.0 40.1 %copy-start.1 = (bf16[2,64,1,512]{3,1,0,2:T(8,128)(2,1)}, bf16[2,64,1,512]{3,1,0,2:T(8,128)(2,1)S(1)}, u32[]{:S(2)}) copy-start(bf16[2,64,1,512]{3,1,0,2:T(8,128)(2,1)S(1)} %get-tuple-element.6) | copy-start | bytes 393220
  15.0 40.1 %copy-start.2 = (bf16[2,64,1,512]{3,1,0,2:T(8,128)(2,1)}, bf16[2,64,1,512]{3,1,0,2:T(8,128)(2,1)S(1)}, u32[]{:S(2)}) copy-start(bf16[2,64,1,512]{3,1,0,2:T(8,128)(2,1)S(1)} %get-tuple-element.5) | copy-start | bytes 393220
  15.0 12.5 %collective-permute-start.10 = (bf16[128,512]{1,0:T(8,128)(2,1)S(1)}, bf16[128,512]{1,0:T(8,128)(2,1)S(1)}, u32[]{:S(2)}, u32[]{:S(2)}) collective-permute-start(bf16[128,512]{1,0:T(8,128)(2,1)S(1)} %bitcast.47), channel_id=1, source_target_pairs={{4,0},{8,4},{12,8},{16,12},{20,16},{24,20},{28,24},{5,1},{9,5},{13... | collective-permute-start | bytes 393224 | tf_op jit(solution)/shard_map/ppermute | solution.py:18
  18.3 12.2 %collective-permute-start.4 = (bf16[128,512]{1,0:T(8,128)(2,1)S(1)}, bf16[128,512]{1,0:T(8,128)(2,1)S(1)}, u32[]{:S(2)}, u32[]{:S(2)}) collective-permute-start(bf16[128,512]{1,0:T(8,128)(2,1)S(1)} %bitcast.48), channel_id=1, source_target_pairs={{16,0},{20,4},{24,8},{28,12},{17,1},{21,5},{25,9},{29,13},{18,2},{... | collective-permute-start | bytes 393224 | tf_op jit(solution)/shard_map/ppermute | solution.py:18
  20.0 13.9 %collective-permute-start.6 = (bf16[128,512]{1,0:T(8,128)(2,1)S(1)}, bf16[128,512]{1,0:T(8,128)(2,1)S(1)}, u32[]{:S(2)}, u32[]{:S(2)}) collective-permute-start(bf16[128,512]{1,0:T(8,128)(2,1)S(1)} %bitcast.49), channel_id=1, source_target_pairs={{12,0},{16,4},{20,8},{24,12},{28,16},{13,1},{17,5},{21,9},{25,13},... | collective-permute-start | bytes 393224 | tf_op jit(solution)/shard_map/ppermute | solution.py:18
  21.9 10.7 %collective-permute-start.5 = (bf16[128,512]{1,0:T(8,128)(2,1)S(1)}, bf16[128,512]{1,0:T(8,128)(2,1)S(1)}, u32[]{:S(2)}, u32[]{:S(2)}) collective-permute-start(bf16[128,512]{1,0:T(8,128)(2,1)S(1)} %bitcast.38), channel_id=1, source_target_pairs={{16,28},{20,24},{24,20},{28,16},{17,29},{21,25},{25,21},{29,17},{1... | collective-permute-start | bytes 393224 | tf_op jit(solution)/shard_map/ppermute | solution.py:126
  26.8 12.8 %collective-permute-start.7 = (bf16[128,512]{1,0:T(8,128)(2,1)S(1)}, bf16[128,512]{1,0:T(8,128)(2,1)S(1)}, u32[]{:S(2)}, u32[]{:S(2)}) collective-permute-start(bf16[128,512]{1,0:T(8,128)(2,1)S(1)} %bitcast.39), channel_id=1, source_target_pairs={{20,28},{28,20},{21,29},{29,21},{22,30},{30,22},{23,31},{31,23}} | collective-permute-start | bytes 393224 | tf_op jit(solution)/shard_map/ppermute | solution.py:126
  27.5 14.0 %collective-permute-start.8 = (bf16[128,512]{1,0:T(8,128)(2,1)S(1)}, bf16[128,512]{1,0:T(8,128)(2,1)S(1)}, u32[]{:S(2)}, u32[]{:S(2)}) collective-permute-start(bf16[128,512]{1,0:T(8,128)(2,1)S(1)} %bitcast.50), channel_id=1, source_target_pairs={{8,0},{12,4},{16,8},{20,12},{24,16},{28,20},{9,1},{13,5},{17,9},{2... | collective-permute-start | bytes 393224 | tf_op jit(solution)/shard_map/ppermute | solution.py:18
  30.5 12.9 %collective-permute-start.9 = (bf16[128,512]{1,0:T(8,128)(2,1)S(1)}, bf16[128,512]{1,0:T(8,128)(2,1)S(1)}, u32[]{:S(2)}, u32[]{:S(2)}) collective-permute-start(bf16[128,512]{1,0:T(8,128)(2,1)S(1)} %bitcast.40), channel_id=1, source_target_pairs={{24,28},{28,24},{25,29},{29,25},{26,30},{30,26},{27,31},{31,27}} | collective-permute-start | bytes 393224 | tf_op jit(solution)/shard_map/ppermute | solution.py:126
  32.7 11.6 %collective-permute-start = (bf16[128,512]{1,0:T(8,128)(2,1)S(1)}, bf16[128,512]{1,0:T(8,128)(2,1)S(1)}, u32[]{:S(2)}, u32[]{:S(2)}) collective-permute-start(bf16[128,512]{1,0:T(8,128)(2,1)S(1)} %bitcast.41), channel_id=1, source_target_pairs={{0,16},{4,20},{8,24},{12,28},{1,17},{5,21},{9,25},{13,29},{2,18},{... | collective-permute-start | bytes 393224 | tf_op jit(solution)/shard_map/ppermute | solution.py:18
  34.0 11.2 %collective-permute-start.1 = (bf16[128,512]{1,0:T(8,128)(2,1)S(1)}, bf16[128,512]{1,0:T(8,128)(2,1)S(1)}, u32[]{:S(2)}, u32[]{:S(2)}) collective-permute-start(bf16[128,512]{1,0:T(8,128)(2,1)S(1)} %bitcast.42), channel_id=1, source_target_pairs={{0,12},{4,16},{8,20},{12,24},{16,28},{1,13},{5,17},{9,21},{13,25},... | collective-permute-start | bytes 393224 | tf_op jit(solution)/shard_map/ppermute | solution.py:18
  39.5 9.4 %collective-permute-start.2 = (bf16[128,512]{1,0:T(8,128)(2,1)S(1)}, bf16[128,512]{1,0:T(8,128)(2,1)S(1)}, u32[]{:S(2)}, u32[]{:S(2)}) collective-permute-start(bf16[128,512]{1,0:T(8,128)(2,1)S(1)} %bitcast.43), channel_id=1, source_target_pairs={{0,8},{4,12},{8,16},{12,20},{16,24},{20,28},{1,9},{5,13},{9,17},{1... | collective-permute-start | bytes 393224 | tf_op jit(solution)/shard_map/ppermute | solution.py:18
  41.5 13.6 %collective-permute-start.3 = (bf16[128,512]{1,0:T(8,128)(2,1)S(1)}, bf16[128,512]{1,0:T(8,128)(2,1)}, u32[]{:S(2)}, u32[]{:S(2)}) collective-permute-start(bf16[128,512]{1,0:T(8,128)(2,1)S(1)} %bitcast.44), channel_id=1, source_target_pairs={{0,4},{4,8},{8,12},{12,16},{16,20},{20,24},{24,28},{1,5},{5,9},{9,... | collective-permute-start | bytes 393224 | tf_op jit(solution)/shard_map/ppermute | solution.py:18
  44.3 10.8 %copy-start.3 = (bf16[128,512]{1,0:T(8,128)(2,1)}, bf16[128,512]{1,0:T(8,128)(2,1)S(1)}, u32[]{:S(2)}) copy-start(bf16[128,512]{1,0:T(8,128)(2,1)S(1)} %collective-permute-done.refs_0_) | copy-start | bytes 393220
  45.2 9.9 %copy-start.4 = (bf16[128,512]{1,0:T(8,128)(2,1)}, bf16[128,512]{1,0:T(8,128)(2,1)S(1)}, u32[]{:S(2)}) copy-start(bf16[128,512]{1,0:T(8,128)(2,1)S(1)} %collective-permute-done.1.refs_1_) | copy-start | bytes 393220
  48.9 0.7 copy-start.5
  55.1 1.3 %copy-start = (bf16[64,4,4096]{2,0,1:T(8,128)(2,1)}, bf16[64,4,4096]{2,0,1:T(8,128)(2,1)S(1)}, u32[]{:S(2)}) copy-start(bf16[64,4,4096]{2,0,1:T(8,128)(2,1)S(1)} %all-to-all-done) | copy-start | bytes 6291460
